TPU v7x, 512 devices: a whole 4x4x16 slice. The times are simulated.
512 devices in a mesh: blk: 16 (over x_hi, y, core), wide: 32 (over x_lo, z).
Axes of the slice: x: 4 (x_hi: 2, x_lo: 2; x = x_hi * 2 + x_lo), y: 4, z: 16, core: 2. Of those that a mesh axis runs over, the one named last changes fastest.
Arguments:
- series: bfloat16 [90112, 640], P(('blk', 'wide'))
- scrub_mask: int32 [640], replicated, may hold values from 0 to 1, as said below
- seed_index: int32 [4096], P(('blk', 'wide')), may hold values from 0 to 90111, as said below
Outputs:
- dispersion: bfloat16 [16, 5632, 4096], P(None, 'wide', 'blk')
- statistic: bfloat16 [16, 5632, 4096], P(None, 'wide', 'blk')
Inputs may be any that keep to these rules, and one draw needn't show every extreme that they name: Entry i of seed_index lies among the rows (i // 8) * 176 to (i // 8 + 1) * 176 - 1, and the 8 entries of one such block are distinct. `scrub_mask`: every frame of even position is kept.
All inputs are finite; a program needn't handle non-finite values.
Results may differ from a plain program's by a relative error of at most 0.0057.
Values may be sent and summed in bfloat16 or wider, within the bound.
No kernel may reach another device: no remote copies, remote signals or barrier semaphores. Data moves between devices by JAX's collectives and lax.ppermute only.
A program may use at most 128 MiB of HBM per device.

v0:
```python
import jax
import jax.numpy as jnp
from jax import lax
from jax.sharding import PartitionSpec as P

WIN = 60
STRIDE = 30
NWIN = 20


EPSILON = 1e-05
CLIP_LEVEL = 0.99


def shifted(block, axis, distance):
    devices = range(lax.axis_size(axis))
    route = [((i - distance) % len(devices), i) for i in devices]
    return lax.ppermute(block, axis, route)


def fisher_of(values):
    clipped = jnp.clip(values, -CLIP_LEVEL, CLIP_LEVEL)
    return 0.5 * (jnp.log(1.0 + clipped) - jnp.log(1.0 - clipped))


def prepare(raw_rows, scrub_mask):
    values = raw_rows.astype(jnp.float32)
    row_count = values.shape[0]
    weight = scrub_mask.astype(jnp.float32)
    covered = STRIDE * (NWIN + 1)
    pieces = values[:, :covered].reshape(row_count, NWIN + 1, STRIDE)
    framed = jnp.concatenate([pieces[:, :-1], pieces[:, 1:]], axis=2)
    mask_pieces = weight[:covered].reshape(NWIN + 1, STRIDE)
    mask_framed = jnp.concatenate([mask_pieces[:-1], mask_pieces[1:]], axis=1)
    valid_count = jnp.sum(mask_framed, axis=1)
    centre = jnp.sum(framed * mask_framed, axis=2) / valid_count
    centred = (framed - centre[:, :, None]) * mask_framed
    spread = jnp.sum(centred * centred, axis=2)
    windows = (centred * lax.rsqrt(spread + EPSILON)[:, :, None]).astype(jnp.bfloat16)
    total_valid = jnp.sum(weight)
    mean_all = jnp.sum(values * weight, axis=1) / total_valid
    centred_all = (values - mean_all[:, None]) * weight
    spread_all = jnp.sum(centred_all * centred_all, axis=1)
    whole_std = (centred_all * lax.rsqrt(spread_all + EPSILON)[:, None]).astype(jnp.bfloat16)
    return (windows, whole_std)


def compare(target_windows, target_whole, seed_window, seed_whole, total_valid):
    window_corr = jnp.einsum(
        "tnw,snw->nts", target_windows, seed_window, preferred_element_type=jnp.float32
    )
    fisher = fisher_of(window_corr)
    first_moment = jnp.mean(fisher, axis=0)
    second = jnp.mean(fisher * fisher, axis=0)
    dispersion = ((WIN - 3) * (second - first_moment * first_moment)).astype(jnp.bfloat16)
    static = jnp.einsum("tf,sf->ts", target_whole, seed_whole, preferred_element_type=jnp.float32)
    statistic = (jnp.sqrt(total_valid - 3.0) * fisher_of(static)).astype(jnp.bfloat16)
    return (dispersion, statistic)


def body(series, scrub_mask, seed_index):
    row_count = series.shape[0]
    local_rows = seed_index % row_count
    own_seeds = jnp.take(series, local_rows, axis=0)
    total_valid = jnp.sum(scrub_mask.astype(jnp.float32))
    target_windows, target_whole = prepare(series, scrub_mask)
    blocks = lax.axis_size("blk")
    panel_rows = lax.all_gather(own_seeds, "wide", axis=0, tiled=True)
    seed_window, seed_whole = prepare(panel_rows, scrub_mask)
    panel_size = panel_rows.shape[0]
    own_block = lax.axis_index("blk")

    def record(results, source, raw_rows):
        block_windows, block_whole = prepare(raw_rows, scrub_mask)
        dispersion, statistic = compare(
            block_windows, block_whole, seed_window, seed_whole, total_valid
        )
        return (
            lax.dynamic_update_index_in_dim(results[0], dispersion, source, 0),
            lax.dynamic_update_index_in_dim(results[1], statistic, source, 0),
        )

    empty = jnp.zeros((blocks, row_count, panel_size), jnp.bfloat16)
    own_dispersion, own_statistic = compare(
        target_windows, target_whole, seed_window, seed_whole, total_valid
    )
    results = (
        lax.dynamic_update_index_in_dim(empty, own_dispersion, own_block, 0),
        lax.dynamic_update_index_in_dim(empty, own_statistic, own_block, 0),
    )

    def advance(offset, carry):
        stored, moving = carry
        moving = shifted(moving, "blk", 1)
        stored = record(stored, (own_block - offset) % blocks, moving)
        return (stored, moving)

    results, moving = lax.fori_loop(1, blocks, advance, (results, series))
    return (results[0], results[1])


def solution(mesh):
    in_specs = (P(("blk", "wide"), None), P(), P(("blk", "wide")))
    out_specs = (P(None, "wide", "blk"), P(None, "wide", "blk"))
    return jax.shard_map(body, mesh=mesh, in_specs=in_specs, out_specs=out_specs, check_vma=False)
```

profile of v0, /device:TPU:4, one launch (start us, length us, event | category | flops | bytes accessed | tf_op | source)
XLA Modules:
  0.0 359.1 jit_solution(2068689304347063946)
XLA Ops:
  8.9 70.2 %all_gather.3 = bf16[256,640]{1,0:T(8,128)(2,1)S(1)} all-gather(bf16[8,640]{1,0:T(8,128)(2,1)S(1)} %broadcast_select_fusion), channel_id=1, replica_groups=mesh['blk'=16,'wide'=32] {'wide'}, dimensions={0}, use_global_device_ids=true | all-gather | bytes 337920 | tf_op jit(solution)/shard_map/all_gather | solution.py:68
  85.3 2.3 multiply_reduce_fusion.5
  90.4 267.5 %while.20 = (s32[]{:T(128)}, bf16[16,176,256]{2,1,0:T(8,128)(2,1)}, bf16[16,176,256]{2,1,0:T(8,128)(2,1)S(1)}, bf16[176,640]{0,1:T(8,128)(2,1)S(1)}, f32[20,60]{...) while((s32[]{:T(128)}, bf16[16,176,256]{2,1,0:T(8,128)(2,1)}, ...), condition=%wide.region_20.21_spmd, body=%wide.region_13.20_spmd.sunk | while | flops 177675536 | bytes 12591712 | solution.py:98
  92.4 10.0 %collective-permute-done = bf16[176,640]{0,1:T(8,128)(2,1)S(1)} collective-permute-done((bf16[176,640]{0,1:T(8,128)(2,1)S(1)}, bf16[176,640]{0,1:T(8,128)(2,1)S(1)}, u32[]{:S(2)}, u32[]{:S(2)}) %collective-permute-start) | collective-permute-done | bytes 225312 | tf_op jit(solution)/shard_map/while/body/eval_jaxpr/ppermute | solution.py:18
  110.2 10.0 %collective-permute-done = bf16[176,640]{0,1:T(8,128)(2,1)S(1)} collective-permute-done((bf16[176,640]{0,1:T(8,128)(2,1)S(1)}, bf16[176,640]{0,1:T(8,128)(2,1)S(1)}, u32[]{:S(2)}, u32[]{:S(2)}) %collective-permute-start) | collective-permute-done | bytes 225312 | tf_op jit(solution)/shard_map/while/body/eval_jaxpr/ppermute | solution.py:18
  122.6 2.3 multiply_reduce_fusion.21
  128.1 10.0 %collective-permute-done = bf16[176,640]{0,1:T(8,128)(2,1)S(1)} collective-permute-done((bf16[176,640]{0,1:T(8,128)(2,1)S(1)}, bf16[176,640]{0,1:T(8,128)(2,1)S(1)}, u32[]{:S(2)}, u32[]{:S(2)}) %collective-permute-start) | collective-permute-done | bytes 225312 | tf_op jit(solution)/shard_map/while/body/eval_jaxpr/ppermute | solution.py:18
  140.4 2.3 multiply_reduce_fusion.21
  145.9 10.0 %collective-permute-done = bf16[176,640]{0,1:T(8,128)(2,1)S(1)} collective-permute-done((bf16[176,640]{0,1:T(8,128)(2,1)S(1)}, bf16[176,640]{0,1:T(8,128)(2,1)S(1)}, u32[]{:S(2)}, u32[]{:S(2)}) %collective-permute-start) | collective-permute-done | bytes 225312 | tf_op jit(solution)/shard_map/while/body/eval_jaxpr/ppermute | solution.py:18
  158.2 2.3 multiply_reduce_fusion.21
  163.7 10.0 %collective-permute-done = bf16[176,640]{0,1:T(8,128)(2,1)S(1)} collective-permute-done((bf16[176,640]{0,1:T(8,128)(2,1)S(1)}, bf16[176,640]{0,1:T(8,128)(2,1)S(1)}, u32[]{:S(2)}, u32[]{:S(2)}) %collective-permute-start) | collective-permute-done | bytes 225312 | tf_op jit(solution)/shard_map/while/body/eval_jaxpr/ppermute | solution.py:18
  176.1 2.3 multiply_reduce_fusion.21
  181.6 10.0 %collective-permute-done = bf16[176,640]{0,1:T(8,128)(2,1)S(1)} collective-permute-done((bf16[176,640]{0,1:T(8,128)(2,1)S(1)}, bf16[176,640]{0,1:T(8,128)(2,1)S(1)}, u32[]{:S(2)}, u32[]{:S(2)}) %collective-permute-start) | collective-permute-done | bytes 225312 | tf_op jit(solution)/shard_map/while/body/eval_jaxpr/ppermute | solution.py:18
  193.9 2.3 multiply_reduce_fusion.21
  199.4 10.0 %collective-permute-done = bf16[176,640]{0,1:T(8,128)(2,1)S(1)} collective-permute-done((bf16[176,640]{0,1:T(8,128)(2,1)S(1)}, bf16[176,640]{0,1:T(8,128)(2,1)S(1)}, u32[]{:S(2)}, u32[]{:S(2)}) %collective-permute-start) | collective-permute-done | bytes 225312 | tf_op jit(solution)/shard_map/while/body/eval_jaxpr/ppermute | solution.py:18
  211.8 2.3 multiply_reduce_fusion.21
  217.2 10.0 %collective-permute-done = bf16[176,640]{0,1:T(8,128)(2,1)S(1)} collective-permute-done((bf16[176,640]{0,1:T(8,128)(2,1)S(1)}, bf16[176,640]{0,1:T(8,128)(2,1)S(1)}, u32[]{:S(2)}, u32[]{:S(2)}) %collective-permute-start) | collective-permute-done | bytes 225312 | tf_op jit(solution)/shard_map/while/body/eval_jaxpr/ppermute | solution.py:18
  235.1 10.0 %collective-permute-done = bf16[176,640]{0,1:T(8,128)(2,1)S(1)} collective-permute-done((bf16[176,640]{0,1:T(8,128)(2,1)S(1)}, bf16[176,640]{0,1:T(8,128)(2,1)S(1)}, u32[]{:S(2)}, u32[]{:S(2)}) %collective-permute-start) | collective-permute-done | bytes 225312 | tf_op jit(solution)/shard_map/while/body/eval_jaxpr/ppermute | solution.py:18
  252.9 10.0 %collective-permute-done = bf16[176,640]{0,1:T(8,128)(2,1)S(1)} collective-permute-done((bf16[176,640]{0,1:T(8,128)(2,1)S(1)}, bf16[176,640]{0,1:T(8,128)(2,1)S(1)}, u32[]{:S(2)}, u32[]{:S(2)}) %collective-permute-start) | collective-permute-done | bytes 225312 | tf_op jit(solution)/shard_map/while/body/eval_jaxpr/ppermute | solution.py:18
  270.7 10.0 %collective-permute-done = bf16[176,640]{0,1:T(8,128)(2,1)S(1)} collective-permute-done((bf16[176,640]{0,1:T(8,128)(2,1)S(1)}, bf16[176,640]{0,1:T(8,128)(2,1)S(1)}, u32[]{:S(2)}, u32[]{:S(2)}) %collective-permute-start) | collective-permute-done | bytes 225312 | tf_op jit(solution)/shard_map/while/body/eval_jaxpr/ppermute | solution.py:18
  288.6 10.0 %collective-permute-done = bf16[176,640]{0,1:T(8,128)(2,1)S(1)} collective-permute-done((bf16[176,640]{0,1:T(8,128)(2,1)S(1)}, bf16[176,640]{0,1:T(8,128)(2,1)S(1)}, u32[]{:S(2)}, u32[]{:S(2)}) %collective-permute-start) | collective-permute-done | bytes 225312 | tf_op jit(solution)/shard_map/while/body/eval_jaxpr/ppermute | solution.py:18
  306.4 10.0 %collective-permute-done = bf16[176,640]{0,1:T(8,128)(2,1)S(1)} collective-permute-done((bf16[176,640]{0,1:T(8,128)(2,1)S(1)}, bf16[176,640]{0,1:T(8,128)(2,1)S(1)}, u32[]{:S(2)}, u32[]{:S(2)}) %collective-permute-start) | collective-permute-done | bytes 225312 | tf_op jit(solution)/shard_map/while/body/eval_jaxpr/ppermute | solution.py:18
  324.3 10.0 %collective-permute-done = bf16[176,640]{0,1:T(8,128)(2,1)S(1)} collective-permute-done((bf16[176,640]{0,1:T(8,128)(2,1)S(1)}, bf16[176,640]{0,1:T(8,128)(2,1)S(1)}, u32[]{:S(2)}, u32[]{:S(2)}) %collective-permute-start) | collective-permute-done | bytes 225312 | tf_op jit(solution)/shard_map/while/body/eval_jaxpr/ppermute | solution.py:18
  342.1 10.0 %collective-permute-done = bf16[176,640]{0,1:T(8,128)(2,1)S(1)} collective-permute-done((bf16[176,640]{0,1:T(8,128)(2,1)S(1)}, bf16[176,640]{0,1:T(8,128)(2,1)S(1)}, u32[]{:S(2)}, u32[]{:S(2)}) %collective-permute-start) | collective-permute-done | bytes 225312 | tf_op jit(solution)/shard_map/while/body/eval_jaxpr/ppermute | solution.py:18
  (332 shorter events, 118.6 us)
Async XLA Ops:
  85.2 2.3 copy-start.2
  90.4 12.0 %collective-permute-start = (bf16[176,640]{0,1:T(8,128)(2,1)S(1)}, bf16[176,640]{0,1:T(8,128)(2,1)S(1)}, u32[]{:S(2)}, u32[]{:S(2)}) collective-permute-start(bf16[176,640]{0,1:T(8,128)(2,1)S(1)} %get-tuple-element.459), channel_id=1, source_target_pairs={{480,0},{0,32},{32,64},{64,96},{96,128},{128,160},{160,192},{192,2... | collective-permute-start | bytes 675848 | tf_op jit(solution)/shard_map/while/body/eval_jaxpr/ppermute | solution.py:18
  103.7 1.1 copy-start.3
  108.3 12.0 %collective-permute-start = (bf16[176,640]{0,1:T(8,128)(2,1)S(1)}, bf16[176,640]{0,1:T(8,128)(2,1)S(1)}, u32[]{:S(2)}, u32[]{:S(2)}) collective-permute-start(bf16[176,640]{0,1:T(8,128)(2,1)S(1)} %get-tuple-element.459), channel_id=1, source_target_pairs={{480,0},{0,32},{32,64},{64,96},{96,128},{128,160},{160,192},{192,2... | collective-permute-start | bytes 675848 | tf_op jit(solution)/shard_map/while/body/eval_jaxpr/ppermute | solution.py:18
  121.5 1.1 copy-start.3
  126.1 12.0 %collective-permute-start = (bf16[176,640]{0,1:T(8,128)(2,1)S(1)}, bf16[176,640]{0,1:T(8,128)(2,1)S(1)}, u32[]{:S(2)}, u32[]{:S(2)}) collective-permute-start(bf16[176,640]{0,1:T(8,128)(2,1)S(1)} %get-tuple-element.459), channel_id=1, source_target_pairs={{480,0},{0,32},{32,64},{64,96},{96,128},{128,160},{160,192},{192,2... | collective-permute-start | bytes 675848 | tf_op jit(solution)/shard_map/while/body/eval_jaxpr/ppermute | solution.py:18
  139.3 1.1 copy-start.3
  143.9 12.0 %collective-permute-start = (bf16[176,640]{0,1:T(8,128)(2,1)S(1)}, bf16[176,640]{0,1:T(8,128)(2,1)S(1)}, u32[]{:S(2)}, u32[]{:S(2)}) collective-permute-start(bf16[176,640]{0,1:T(8,128)(2,1)S(1)} %get-tuple-element.459), channel_id=1, source_target_pairs={{480,0},{0,32},{32,64},{64,96},{96,128},{128,160},{160,192},{192,2... | collective-permute-start | bytes 675848 | tf_op jit(solution)/shard_map/while/body/eval_jaxpr/ppermute | solution.py:18
  157.2 1.1 copy-start.3
  161.8 12.0 %collective-permute-start = (bf16[176,640]{0,1:T(8,128)(2,1)S(1)}, bf16[176,640]{0,1:T(8,128)(2,1)S(1)}, u32[]{:S(2)}, u32[]{:S(2)}) collective-permute-start(bf16[176,640]{0,1:T(8,128)(2,1)S(1)} %get-tuple-element.459), channel_id=1, source_target_pairs={{480,0},{0,32},{32,64},{64,96},{96,128},{128,160},{160,192},{192,2... | collective-permute-start | bytes 675848 | tf_op jit(solution)/shard_map/while/body/eval_jaxpr/ppermute | solution.py:18
  175.0 1.1 copy-start.3
  179.6 12.0 %collective-permute-start = (bf16[176,640]{0,1:T(8,128)(2,1)S(1)}, bf16[176,640]{0,1:T(8,128)(2,1)S(1)}, u32[]{:S(2)}, u32[]{:S(2)}) collective-permute-start(bf16[176,640]{0,1:T(8,128)(2,1)S(1)} %get-tuple-element.459), channel_id=1, source_target_pairs={{480,0},{0,32},{32,64},{64,96},{96,128},{128,160},{160,192},{192,2... | collective-permute-start | bytes 675848 | tf_op jit(solution)/shard_map/while/body/eval_jaxpr/ppermute | solution.py:18
  192.8 1.1 copy-start.3
  197.4 12.0 %collective-permute-start = (bf16[176,640]{0,1:T(8,128)(2,1)S(1)}, bf16[176,640]{0,1:T(8,128)(2,1)S(1)}, u32[]{:S(2)}, u32[]{:S(2)}) collective-permute-start(bf16[176,640]{0,1:T(8,128)(2,1)S(1)} %get-tuple-element.459), channel_id=1, source_target_pairs={{480,0},{0,32},{32,64},{64,96},{96,128},{128,160},{160,192},{192,2... | collective-permute-start | bytes 675848 | tf_op jit(solution)/shard_map/while/body/eval_jaxpr/ppermute | solution.py:18
  210.7 1.1 copy-start.3
  215.3 12.0 %collective-permute-start = (bf16[176,640]{0,1:T(8,128)(2,1)S(1)}, bf16[176,640]{0,1:T(8,128)(2,1)S(1)}, u32[]{:S(2)}, u32[]{:S(2)}) collective-permute-start(bf16[176,640]{0,1:T(8,128)(2,1)S(1)} %get-tuple-element.459), channel_id=1, source_target_pairs={{480,0},{0,32},{32,64},{64,96},{96,128},{128,160},{160,192},{192,2... | collective-permute-start | bytes 675848 | tf_op jit(solution)/shard_map/while/body/eval_jaxpr/ppermute | solution.py:18
  233.1 12.0 %collective-permute-start = (bf16[176,640]{0,1:T(8,128)(2,1)S(1)}, bf16[176,640]{0,1:T(8,128)(2,1)S(1)}, u32[]{:S(2)}, u32[]{:S(2)}) collective-permute-start(bf16[176,640]{0,1:T(8,128)(2,1)S(1)} %get-tuple-element.459), channel_id=1, source_target_pairs={{480,0},{0,32},{32,64},{64,96},{96,128},{128,160},{160,192},{192,2... | collective-permute-start | bytes 675848 | tf_op jit(solution)/shard_map/while/body/eval_jaxpr/ppermute | solution.py:18
  250.9 12.0 %collective-permute-start = (bf16[176,640]{0,1:T(8,128)(2,1)S(1)}, bf16[176,640]{0,1:T(8,128)(2,1)S(1)}, u32[]{:S(2)}, u32[]{:S(2)}) collective-permute-start(bf16[176,640]{0,1:T(8,128)(2,1)S(1)} %get-tuple-element.459), channel_id=1, source_target_pairs={{480,0},{0,32},{32,64},{64,96},{96,128},{128,160},{160,192},{192,2... | collective-permute-start | bytes 675848 | tf_op jit(solution)/shard_map/while/body/eval_jaxpr/ppermute | solution.py:18
  268.8 12.0 %collective-permute-start = (bf16[176,640]{0,1:T(8,128)(2,1)S(1)}, bf16[176,640]{0,1:T(8,128)(2,1)S(1)}, u32[]{:S(2)}, u32[]{:S(2)}) collective-permute-start(bf16[176,640]{0,1:T(8,128)(2,1)S(1)} %get-tuple-element.459), channel_id=1, source_target_pairs={{480,0},{0,32},{32,64},{64,96},{96,128},{128,160},{160,192},{192,2... | collective-permute-start | bytes 675848 | tf_op jit(solution)/shard_map/while/body/eval_jaxpr/ppermute | solution.py:18
  286.6 12.0 %collective-permute-start = (bf16[176,640]{0,1:T(8,128)(2,1)S(1)}, bf16[176,640]{0,1:T(8,128)(2,1)S(1)}, u32[]{:S(2)}, u32[]{:S(2)}) collective-permute-start(bf16[176,640]{0,1:T(8,128)(2,1)S(1)} %get-tuple-element.459), channel_id=1, source_target_pairs={{480,0},{0,32},{32,64},{64,96},{96,128},{128,160},{160,192},{192,2... | collective-permute-start | bytes 675848 | tf_op jit(solution)/shard_map/while/body/eval_jaxpr/ppermute | solution.py:18
  304.4 12.0 %collective-permute-start = (bf16[176,640]{0,1:T(8,128)(2,1)S(1)}, bf16[176,640]{0,1:T(8,128)(2,1)S(1)}, u32[]{:S(2)}, u32[]{:S(2)}) collective-permute-start(bf16[176,640]{0,1:T(8,128)(2,1)S(1)} %get-tuple-element.459), channel_id=1, source_target_pairs={{480,0},{0,32},{32,64},{64,96},{96,128},{128,160},{160,192},{192,2... | collective-permute-start | bytes 675848 | tf_op jit(solution)/shard_map/while/body/eval_jaxpr/ppermute | solution.py:18
  322.3 12.0 %collective-permute-start = (bf16[176,640]{0,1:T(8,128)(2,1)S(1)}, bf16[176,640]{0,1:T(8,128)(2,1)S(1)}, u32[]{:S(2)}, u32[]{:S(2)}) collective-permute-start(bf16[176,640]{0,1:T(8,128)(2,1)S(1)} %get-tuple-element.459), channel_id=1, source_target_pairs={{480,0},{0,32},{32,64},{64,96},{96,128},{128,160},{160,192},{192,2... | collective-permute-start | bytes 675848 | tf_op jit(solution)/shard_map/while/body/eval_jaxpr/ppermute | solution.py:18
  340.1 12.0 %collective-permute-start = (bf16[176,640]{0,1:T(8,128)(2,1)S(1)}, bf16[176,640]{0,1:T(8,128)(2,1)S(1)}, u32[]{:S(2)}, u32[]{:S(2)}) collective-permute-start(bf16[176,640]{0,1:T(8,128)(2,1)S(1)} %get-tuple-element.459), channel_id=1, source_target_pairs={{480,0},{0,32},{32,64},{64,96},{96,128},{128,160},{160,192},{192,2... | collective-permute-start | bytes 675848 | tf_op jit(solution)/shard_map/while/body/eval_jaxpr/ppermute | solution.py:18
  358.0 1.1 copy-start.1
  (10 other events, 10.7 us)
where the time goes:
time: 361 us; the launch traced here: 359 us
  waiting for transfers between devices  151 us (42%)
  blocking collectives  70.2 us (19%)
  other arithmetic  48.3 us (13%)
  matrix products  44.4 us (12%)
  starting transfers between devices  28.8 us (8%)
  local copies, waits for them, and re-layouts  13.3 us (4%)
    ppermute x15, waiting for transfers between devices, shifted(): return lax.ppermute(block, axis, route)  151 us
    all_gather x1, blocking collectives, body(): panel_rows = lax.all_gather(own_seeds, 'wide', axis=0, tiled=True)  70.2 us
    dot_general x16, matrix products, compare(): jnp.einsum('tnw,snw->nts', target_windows, seed_window, preferred_element...  36.8 us
    ppermute x15, starting transfers between devices, shifted(): return lax.ppermute(block, axis, route)  28.8 us
    dynamic_update_slice x15, other arithmetic, record(): lax.dynamic_update_index_in_dim(results[0], dispersion, source, 0)  10.2 us
    div x17, other arithmetic, prepare(): mean_all = jnp.sum(values * weight, axis=1) / total_valid  9.57 us
    reduce_sum x17, other arithmetic, prepare(): spread = jnp.sum(centred * centred, axis=2)  8.51 us
    dot_general x16, matrix products, compare(): jnp.einsum('tf,sf->ts', target_whole, seed_whole, preferred_element_type=...  7.54 us
  transfers between devices with their start and end apart: 15, of which 15 were waited for; matrix products, arithmetic and copies ran while one was open for 0% of the time, Pallas kernels for 0%

commit v1 on v0

--- a/solution.py
+++ b/solution.py
@@ -10,12 +10,6 @@
 
 EPSILON = 1e-05
 CLIP_LEVEL = 0.99
-
-
-def shifted(block, axis, distance):
-    devices = range(lax.axis_size(axis))
-    route = [((i - distance) % len(devices), i) for i in devices]
-    return lax.ppermute(block, axis, route)
 
 
 def fisher_of(values):
@@ -59,44 +53,20 @@
 
 
 def body(series, scrub_mask, seed_index):
-    row_count = series.shape[0]
+    row_count, frames = series.shape
     local_rows = seed_index % row_count
     own_seeds = jnp.take(series, local_rows, axis=0)
     total_valid = jnp.sum(scrub_mask.astype(jnp.float32))
-    target_windows, target_whole = prepare(series, scrub_mask)
-    blocks = lax.axis_size("blk")
     panel_rows = lax.all_gather(own_seeds, "wide", axis=0, tiled=True)
     seed_window, seed_whole = prepare(panel_rows, scrub_mask)
-    panel_size = panel_rows.shape[0]
-    own_block = lax.axis_index("blk")
-
-    def record(results, source, raw_rows):
-        block_windows, block_whole = prepare(raw_rows, scrub_mask)
-        dispersion, statistic = compare(
-            block_windows, block_whole, seed_window, seed_whole, total_valid
-        )
-        return (
-            lax.dynamic_update_index_in_dim(results[0], dispersion, source, 0),
-            lax.dynamic_update_index_in_dim(results[1], statistic, source, 0),
-        )
-
-    empty = jnp.zeros((blocks, row_count, panel_size), jnp.bfloat16)
-    own_dispersion, own_statistic = compare(
+    blocks = lax.axis_size("blk")
+    gathered = lax.all_gather(series, "blk", axis=0, tiled=True)
+    target_windows, target_whole = prepare(gathered, scrub_mask)
+    dispersion, statistic = compare(
         target_windows, target_whole, seed_window, seed_whole, total_valid
     )
-    results = (
-        lax.dynamic_update_index_in_dim(empty, own_dispersion, own_block, 0),
-        lax.dynamic_update_index_in_dim(empty, own_statistic, own_block, 0),
-    )
-
-    def advance(offset, carry):
-        stored, moving = carry
-        moving = shifted(moving, "blk", 1)
-        stored = record(stored, (own_block - offset) % blocks, moving)
-        return (stored, moving)
-
-    results, moving = lax.fori_loop(1, blocks, advance, (results, series))
-    return (results[0], results[1])
+    shape = (blocks, row_count, panel_rows.shape[0])
+    return (dispersion.reshape(shape), statistic.reshape(shape))
 
 
 def solution(mesh):

time: 361 us -> 187 us (0.52)
  the two profiles are of different devices: /device:TPU:4 before, /device:TPU:24 now
where the time goes in v1:
time: 187 us; the launch traced here: 186 us
  blocking collectives  70.7 us (38%)
  matrix products  35.9 us (19%)
  local copies, waits for them, and re-layouts  35.3 us (19%)
  other arithmetic  28.5 us (15%)
  between operations  14.9 us (8%)
    all_gather x1, blocking collectives, body(): panel_rows = lax.all_gather(own_seeds, 'wide', axis=0, tiled=True)  70.7 us
    dot_general x1, matrix products, compare(): jnp.einsum('tnw,snw->nts', target_windows, seed_window, preferred_element...  32.3 us
    slice x4, local copies, waits for them, and re-layouts, prepare(): pieces = values[:, :covered].reshape(row_count, NWIN + 1, STRIDE)  12.3 us
    slice x2, local copies, waits for them, and re-layouts, prepare(): framed = jnp.concatenate([pieces[:, :-1], pieces[:, 1:]], axis=2)  12 us
    reduce_sum x2, other arithmetic, prepare(): centre = jnp.sum(framed * mask_framed, axis=2) / valid_count  8.33 us
    reshape x2, local copies, waits for them, and re-layouts, prepare(): pieces = values[:, :covered].reshape(row_count, NWIN + 1, STRIDE)  7.96 us
    another operation x1, other arithmetic  4.49 us
    reduce_sum x2, other arithmetic, prepare(): spread_all = jnp.sum(centred_all * centred_all, axis=1)  4.02 us
  transfers between devices with their start and end apart: 1, of which 0 were waited for; matrix products, arithmetic and copies ran while one was open for 4% of the time, Pallas kernels for 0%

profile of v1, /device:TPU:24, one launch (start us, length us, event | category | flops | bytes accessed | tf_op | source)
XLA Modules:
  0.0 186.0 jit_solution(18207394981131811877)
XLA Ops:
  7.2 0.7 all-gather.2.cloned.1.call-update
  7.9 0.7 convert_element_type.29
  8.6 1.3 convert_reduce_fusion
  10.6 0.7 compare_and_fusion
  11.3 1.5 gather_fusion
  13.4 70.7 %all_gather.7 = bf16[256,640]{1,0:T(8,128)(2,1)S(1)} all-gather(bf16[8,640]{1,0:T(8,128)(2,1)S(1)} %broadcast_select_fusion), channel_id=1, replica_groups=mesh['blk'=16,'wide'=32] {'wide'}, dimensions={0}, use_global_device_ids=true | all-gather | bytes 337920 | tf_op jit(solution)/shard_map/all_gather | solution.py:60
  84.1 0.2 copy.10
  84.7 0.7 broadcast_divide_fusion.3
  85.3 0.2 multiply_reduce_fusion.7
  85.7 0.3 multiply_reduce_fusion.6
  86.2 0.5 multiply_reduce_fusion.5
  86.7 3.0 %multiply_reduce_fusion.4 = f32[2816]{0:T(1024)S(1)} fusion(bf16[2816,640]{1,0:T(8,128)(2,1)} %all-gather.2.cloned.1.call-done, f32[640]{0:T(1024)S(1)} %convert_element_type.29), kind=kLoop, calls=%fused_computation.13 | loop fusion | flops 5403904 | bytes 3618304 | tf_op jit(solution)/shard_map/reduce_sum | solution.py:35
  89.7 0.7 broadcast_divide_fusion.2
  90.3 3.8 %multiply_reduce_fusion.3 = f32[2816]{0:T(1024)S(1)} fusion(bf16[2816,640]{1,0:T(8,128)(2,1)} %all-gather.2.cloned.1.call-done, f32[2816]{0:T(1024)S(1)} %broadcast_divide_fusion.2, f32[640]{0:T(1024)S(1)} %convert_element_type.29), kind=kLoop, calls=%fused_computation.11 | loop fusion | flops 9008384 | bytes 3629568 | tf_op jit(solution)/shard_map/reduce_sum | solution.py:37
  94.1 3.4 %slice.52 = f32[2816,630]{1,0:T(8,128)} slice(bf16[2816,640]{1,0:T(8,128)(2,1)S(1)} %copy-done.2), slice={[0:2816], [0:630]} | slice | bytes 14192640 | tf_op jit(solution)/shard_map/slice | solution.py:25
  97.5 8.6 %copy.9 = f32[2816,630]{0,1:T(8,128)} copy(f32[2816,630]{1,0:T(8,128)} %slice.52) | data formatting | bytes 14192640 | tf_op jit(solution)/shard_map/slice | solution.py:25
  106.1 7.9 %reshape.97 = f32[2816,21,30]{0,2,1:T(8,128)} reshape(f32[2816,630]{0,1:T(8,128)} %copy.9) | data formatting | bytes 14192640 | tf_op jit(solution)/shard_map/reshape | solution.py:25
  114.0 11.9 %fusion.15 = (f32[2816,20,30]{0,2,1:T(8,128)}, f32[2816,20,30]{0,2,1:T(8,128)}) fusion(f32[2816,21,30]{0,2,1:T(8,128)} %reshape.97), kind=kLoop, calls=%fused_computation.54 | loop fusion | bytes 27033600 | tf_op jit(solution)/shard_map/slice | solution.py:26
  125.9 8.0 %multiply_reduce_fusion.2 = f32[2816,20]{0,1:T(8,128)S(1)} fusion(f32[2816,20,30]{0,2,1:T(8,128)} %get-tuple-element.7, f32[2816,20,30]{0,2,1:T(8,128)} %get-tuple-element.6, f32[20,60]{1,0:T(8,128)S(1)} %pad_maximum_fusion.2), kind=kLoop, calls=%fused_computation.8 | loop fusion | flops 10081280 | bytes 13746880 | tf_op jit(solution)/shard_map/reduce_sum | solution.py:30
  134.0 1.2 copy-done.1
  135.3 3.5 %multiply_reduce_fusion.1 = f32[2816,20]{0,1:T(8,128)S(1)} fusion(f32[2816,20,30]{0,2,1:T(8,128)S(1)} %copy-done.1, f32[2816,20,30]{0,2,1:T(8,128)S(1)} %copy-done, f32[2816,20]{0,1:T(8,128)S(1)} %broadcast_divide_fusion, f32[20,60]{1,0:T(8,128)S(1)} %pad_maximum_fusion.2), kind=kLoop, calls=%fused_computation.6 | loop fusion | flops 16839680 | bytes 13972160 | tf_op jit(solution)/shard_map/reduce_sum | solution.py:32
  138.8 32.3 %multiply_reduce_fusion = (f32[2816,256]{1,0:T(8,128)}, f32[2816,256]{1,0:T(8,128)}) fusion(f32[256,20,30]{0,2,1:T(8,128)S(1)} %get-tuple-element.9, f32[256,20,30]{0,2,1:T(8,128)S(1)} %get-tuple-element.8, f32[256,20]{0,1:T(8,128)S(1)} %add_rsqrt_fusion.1, f32[256,20]{0,1:T(8,128)S(1)} %broadcast_divide_fusion.1, f32[20,60]{1,0:T(8,128)S(1)} %pad_maximum_fusion.2, ...), kind=kOutput, calls=%fused_computation.1 | convolution fusion | flops 1862483968 | bytes 21009088 | tf_op jit(solution)/shard_map/tnw,snw->nts/dot_general | solution.py:43
  171.1 4.5 %multiply_convert_fusion.7 = bf16[2816,256]{1,0:T(8,128)(2,1)} fusion(f32[2816,256]{1,0:T(8,128)} %get-tuple-element.3, f32[2816,256]{1,0:T(8,128)} %get-tuple-element.2), kind=kLoop, calls=%fused_computation.22 | loop fusion | flops 4325376 | bytes 7208960 | tf_op jit(solution)/shard_map/convert
  175.6 3.6 %multiply_convert_fusion.4 = bf16[2816,256]{1,0:T(8,128)(2,1)} fusion(bf16[2816,640]{1,0:T(8,128)(2,1)S(1)} %copy-done.3, f32[2816]{0:T(1024)S(1)} %add_rsqrt_fusion.2, f32[2816]{0:T(1024)S(1)} %broadcast_divide_fusion.2, f32[640]{0:T(1024)S(1)} %convert_element_type.29, f32[]{:T(128)S(6)} %mul.165, bf16[256,640]{1,0:T(8,128)(2,1)S(1)} %all_gather.7, ...), kind=kOutput, calls=%fused_computation.21 | convolution fusion | flops 936902656 | bytes 5401092 | tf_op jit(solution)/shard_map/tf,sf->ts/dot_general | solution.py:50
  (28 shorter events, 1.3 us)
Async XLA Ops:
  7.2 79.5 %all-gather.2.cloned.1.call-start = ((), (), s32[]{:S(2)}) async-start(), calls=%async_computation | async-start | bytes 3829760 | tf_op jit(solution)/shard_map/all_gather | solution.py:63
  86.7 7.4 %copy-start.2 = (bf16[2816,640]{1,0:T(8,128)(2,1)S(1)}, bf16[2816,640]{1,0:T(8,128)(2,1)}, u32[]{:S(2)}) copy-start(bf16[2816,640]{1,0:T(8,128)(2,1)} %all-gather.2.cloned.1.call-done) | copy-start | bytes 10813444
  125.9 8.1 %copy-start = (f32[2816,20,30]{0,2,1:T(8,128)S(1)}, f32[2816,20,30]{0,2,1:T(8,128)}, u32[]{:S(2)}) copy-start(f32[2816,20,30]{0,2,1:T(8,128)} %get-tuple-element.6) | copy-start | bytes 20275204
  125.9 9.4 %copy-start.1 = (f32[2816,20,30]{0,2,1:T(8,128)S(1)}, f32[2816,20,30]{0,2,1:T(8,128)}, u32[]{:S(2)}) copy-start(f32[2816,20,30]{0,2,1:T(8,128)} %get-tuple-element.7) | copy-start | bytes 20275204
  171.1 4.5 %copy-start.3 = (bf16[2816,640]{1,0:T(8,128)(2,1)S(1)}, bf16[2816,640]{1,0:T(8,128)(2,1)}, u32[]{:S(2)}) copy-start(bf16[2816,640]{1,0:T(8,128)(2,1)} %all-gather.2.cloned.1.call-done) | copy-start | bytes 10813444
Sparse Core Ops, SparseCore 0:
  11.2 71.5 all-gather.1

commit v2 on v1

--- a/solution.py
+++ b/solution.py
@@ -1,11 +1,18 @@
+import functools
+
+import numpy as np
 import jax
 import jax.numpy as jnp
 from jax import lax
+from jax.experimental import pallas as pl
+from jax.experimental.pallas import tpu as pltpu
 from jax.sharding import PartitionSpec as P
 
 WIN = 60
 STRIDE = 30
 NWIN = 20
+LANES = 128
+SPAN = 256
 
 
 EPSILON = 1e-05
@@ -15,6 +22,14 @@
 def fisher_of(values):
     clipped = jnp.clip(values, -CLIP_LEVEL, CLIP_LEVEL)
     return 0.5 * (jnp.log(1.0 + clipped) - jnp.log(1.0 - clipped))
+
+
+def window_frames(frames):
+    out = []
+    for n in range(NWIN):
+        start = LANES * ((STRIDE * n) // LANES)
+        out.append((start, min(SPAN, frames - start)))
+    return out
 
 
 def prepare(raw_rows, scrub_mask):
@@ -39,32 +54,101 @@
     return (windows, whole_std)
 
 
-def compare(target_windows, target_whole, seed_window, seed_whole, total_valid):
-    window_corr = jnp.einsum(
-        "tnw,snw->nts", target_windows, seed_window, preferred_element_type=jnp.float32
+def seed_operands(seed_window, seed_whole, frames):
+    blocks = []
+    for n, (start, width) in enumerate(window_frames(frames)):
+        left = STRIDE * n - start
+        part = seed_window[:, n, :]
+        part = jnp.pad(part, ((0, 0), (left, SPAN - WIN - left)))
+        blocks.append(part.T)
+    return jnp.stack(blocks), seed_whole.T
+
+
+def window_masks(weight, frames):
+    rows = []
+    for n, (start, width) in enumerate(window_frames(frames)):
+        local = np.arange(SPAN) + start
+        inside = (local >= STRIDE * n) & (local < STRIDE * n + WIN) & (local < frames)
+        idx = np.minimum(local, frames - 1)
+        rows.append(jnp.where(jnp.asarray(inside), weight[idx], 0.0))
+    return jnp.stack(rows)
+
+
+def compare_kernel(x_ref, m_ref, mw_ref, sw_ref, sh_ref, disp_ref, stat_ref):
+    frames = x_ref.shape[1]
+    x = x_ref[...].astype(jnp.float32)
+    m = m_ref[...]
+    total_valid = jnp.sum(m)
+    mean_all = jnp.sum(x * m, axis=1, keepdims=True) / total_valid
+    centred = (x - mean_all) * m
+    spread = jnp.sum(centred * centred, axis=1, keepdims=True)
+    whole = (centred * lax.rsqrt(spread + EPSILON)).astype(jnp.bfloat16)
+    q = jnp.dot(whole, sh_ref[...], preferred_element_type=jnp.float32)
+    stat_ref[...] = (jnp.sqrt(total_valid - 3.0) * fisher_of(q)).astype(stat_ref.dtype)
+    first = None
+    second = None
+    for n, (start, width) in enumerate(window_frames(frames)):
+        xw = x[:, start:start + width]
+        mw = mw_ref[n:n + 1, :width]
+        count = jnp.sum(mw)
+        centre = jnp.sum(xw * mw, axis=1, keepdims=True) / count
+        cw = (xw - centre) * mw
+        sp = jnp.sum(cw * cw, axis=1, keepdims=True)
+        w = (cw * lax.rsqrt(sp + EPSILON)).astype(jnp.bfloat16)
+        r = jnp.dot(w, sw_ref[n, :width, :], preferred_element_type=jnp.float32)
+        z = fisher_of(r)
+        if first is None:
+            first, second = z, z * z
+        else:
+            first, second = first + z, second + z * z
+    first = first / NWIN
+    second = second / NWIN
+    disp_ref[...] = ((WIN - 3) * (second - first * first)).astype(disp_ref.dtype)
+
+
+def compare_rows(rows, weight, seed_window, seed_whole, block):
+    count, frames = rows.shape
+    seeds = seed_whole.shape[0]
+    sw, sh = seed_operands(seed_window, seed_whole, frames)
+    mw = window_masks(weight, frames)
+    steps = count // block
+    flops = 2 * count * seeds * (frames + NWIN * SPAN)
+    cost = pl.CostEstimate(
+        flops=flops,
+        transcendentals=2 * count * seeds * (NWIN + 1),
+        bytes_accessed=count * frames * 2 + sw.size * 2 + 2 * count * seeds * 2,
     )
-    fisher = fisher_of(window_corr)
-    first_moment = jnp.mean(fisher, axis=0)
-    second = jnp.mean(fisher * fisher, axis=0)
-    dispersion = ((WIN - 3) * (second - first_moment * first_moment)).astype(jnp.bfloat16)
-    static = jnp.einsum("tf,sf->ts", target_whole, seed_whole, preferred_element_type=jnp.float32)
-    statistic = (jnp.sqrt(total_valid - 3.0) * fisher_of(static)).astype(jnp.bfloat16)
-    return (dispersion, statistic)
+    out = jax.ShapeDtypeStruct((count, seeds), jnp.bfloat16)
+    return pl.pallas_call(
+        compare_kernel,
+        grid=(steps,),
+        in_specs=[
+            pl.BlockSpec((block, frames), lambda i: (i, 0)),
+            pl.BlockSpec((1, frames), lambda i: (0, 0)),
+            pl.BlockSpec((NWIN, SPAN), lambda i: (0, 0)),
+            pl.BlockSpec((NWIN, SPAN, seeds), lambda i: (0, 0, 0)),
+            pl.BlockSpec((frames, seeds), lambda i: (0, 0)),
+        ],
+        out_specs=[
+            pl.BlockSpec((block, seeds), lambda i: (i, 0)),
+            pl.BlockSpec((block, seeds), lambda i: (i, 0)),
+        ],
+        out_shape=[out, out],
+        cost_estimate=cost,
+        compiler_params=pltpu.CompilerParams(vmem_limit_bytes=48 * 1024 * 1024),
+    )(rows, weight[None, :], mw, sw, sh)
 
 
 def body(series, scrub_mask, seed_index):
     row_count, frames = series.shape
     local_rows = seed_index % row_count
     own_seeds = jnp.take(series, local_rows, axis=0)
-    total_valid = jnp.sum(scrub_mask.astype(jnp.float32))
+    weight = scrub_mask.astype(jnp.float32)
     panel_rows = lax.all_gather(own_seeds, "wide", axis=0, tiled=True)
     seed_window, seed_whole = prepare(panel_rows, scrub_mask)
     blocks = lax.axis_size("blk")
     gathered = lax.all_gather(series, "blk", axis=0, tiled=True)
-    target_windows, target_whole = prepare(gathered, scrub_mask)
-    dispersion, statistic = compare(
-        target_windows, target_whole, seed_window, seed_whole, total_valid
-    )
+    dispersion, statistic = compare_rows(gathered, weight, seed_window, seed_whole, row_count)
     shape = (blocks, row_count, panel_rows.shape[0])
     return (dispersion.reshape(shape), statistic.reshape(shape))
 

time: 187 us -> 154 us (0.82)
  Pallas kernels: 0 us -> 52.2 us
  matrix products: 35.9 us -> 0 us
  local copies, waits for them, and re-layouts: 35.3 us -> 9.61 us
  other arithmetic: 28.5 us -> 5.62 us
    pallas_call x0 -> x1, Pallas kernels: none -> 52.2 us  [compare_rows(): pl.pallas_call(compare_kernel, grid=(steps,), in_specs=[pl.BlockSpec((blo...]
    dot_general x2 -> x0, matrix products: 35.9 us -> none  [the longest x1 32.3 us: compare(): jnp.einsum('tnw,snw->nts', target_windows, seed_window, preferred_element...]
    slice x4 -> x1, local copies, waits for them, and re-layouts: 12.3 us -> 0.04 us  [prepare(): pieces = values[:, :covered].reshape(row_count, NWIN + 1, STRIDE)]
    slice x2 -> x1, local copies, waits for them, and re-layouts: 12 us -> 0.15 us  [prepare(): framed = jnp.concatenate([pieces[:, :-1], pieces[:, 1:]], axis=2)]
    reduce_sum x2 -> x1, other arithmetic: 8.33 us -> 0.35 us  [prepare(): centre = jnp.sum(framed * mask_framed, axis=2) / valid_count]
    reshape x2 -> x1, local copies, waits for them, and re-layouts: 7.96 us -> 0.08 us  [prepare(): pieces = values[:, :covered].reshape(row_count, NWIN + 1, STRIDE)]
    gather x0 -> x5, local copies, waits for them, and re-layouts: none -> 6.83 us  [window_masks(): rows.append(jnp.where(jnp.asarray(inside), weight[idx], 0.0))]
    another operation x1 -> x0, other arithmetic: 4.49 us -> none
  transfers between devices with their start and end apart: 1 -> 1, of which waited for: 0 -> 0; matrix products, arithmetic and copies ran while one was open for 4% -> 10% of each run, Pallas kernels for 0% -> 0%
where the time goes in v2:
time: 154 us
  blocking collectives  70.8 us (46%)
  Pallas kernels  52.2 us (34%)
  between operations  14.8 us (10%)
  local copies, waits for them, and re-layouts  9.61 us (6%)
  other arithmetic  5.62 us (4%)
    all_gather x1, blocking collectives, body(): panel_rows = lax.all_gather(own_seeds, 'wide', axis=0, tiled=True)  70.8 us
    pallas_call x1, Pallas kernels, compare_rows(): pl.pallas_call(compare_kernel, grid=(steps,), in_specs=[pl.BlockSpec((blo...  52.2 us
    gather x5, local copies, waits for them, and re-layouts, window_masks(): rows.append(jnp.where(jnp.asarray(inside), weight[idx], 0.0))  6.83 us
  transfers between devices with their start and end apart: 1, of which 0 were waited for; matrix products, arithmetic and copies ran while one was open for 10% of the time, Pallas kernels for 0%

profile of v2, /device:TPU:24, one launch (start us, length us, event | category | flops | bytes accessed | tf_op | source)
XLA Modules:
  0.0 153.8 jit_solution(1727364281152508755)
XLA Ops:
  7.2 0.7 all-gather.2.cloned.1.call-update
  7.9 0.7 convert_element_type.53
  8.6 0.7 compare_and_fusion
  9.3 0.7 pad_clamp_fusion
  10.0 1.5 %gather_fusion.5 = bf16[8,640]{1,0:T(8,128)(2,1)S(1)} fusion(bf16[176,640]{1,0:T(8,128)(2,1)} %param.63, s32[1024]{0:T(1024)S(1)} %get-tuple-element.51), kind=kCustom, calls=%fused_computation.5 | custom fusion | bytes 20512 | tf_op jit(solution)/shard_map/jit(_take)/gather | solution.py:145
  11.9 70.8 %all_gather.7 = bf16[256,640]{1,0:T(8,128)(2,1)S(1)} all-gather(bf16[8,640]{1,0:T(8,128)(2,1)S(1)} %broadcast_select_fusion), channel_id=1, replica_groups=mesh['blk'=16,'wide'=32] {'wide'}, dimensions={0}, use_global_device_ids=true | all-gather | bytes 337920 | tf_op jit(solution)/shard_map/all_gather | solution.py:147
  82.7 0.2 copy.67
  83.0 0.1 reduce_sum.66
  83.1 0.1 reduce_sum.67
  83.5 1.4 gather_fusion
  84.9 1.4 gather_fusion.3
  86.3 1.4 gather_fusion.1
  87.7 1.4 gather_fusion.2
  89.0 1.4 gather_fusion.4
  90.8 0.6 convert_reduce_fusion
  91.5 0.1 fusion.1
  91.6 0.3 multiply_reduce_fusion.1
  92.1 0.5 multiply_reduce_fusion
  92.6 0.4 multiply_convert_fusion
  93.5 0.2 multiply_reduce_fusion.3
  93.7 0.7 broadcast_divide_fusion.1
  94.3 0.2 multiply_reduce_fusion.2
  94.5 0.2 fusion.sh_ref
  94.7 52.2 %shard_map.590 = (bf16[2816,256]{1,0:T(8,128)(2,1)}, bf16[2816,256]{1,0:T(8,128)(2,1)}) custom-call(bf16[2816,640]{1,0:T(8,128)(2,1)} %all-gather.2.cloned.1.call-done.x_ref, f32[1,640]{1,0:T(1,128)S(1)} %broadcast_in_dim.107.m_ref, f32[20,256]{1,0:T(8,128)S(1)} %stack.146.mw_ref, bf16[20,256,256]{2,1,0:T(8,128)(2,1)S(1)} %bitcast_dynamic-update-slice_fusion.sw_ref, ...), custom_call_target="tpu_custom_call" | custom-call | flops 8304721920 | bytes 9109504 | tf_op jit(solution)/shard_map/pallas_call | solution.py:122
  (93 shorter events, 1.3 us)
Async XLA Ops:
  7.2 76.1 %copy-start.3 = (s32[256]{0:T(256)S(1)}, s32[256]{0:T(256)}, u32[]{:S(2)}) copy-start(s32[256]{0:T(256)} %constant.159) | copy-start | bytes 3076
  7.2 77.7 %copy-start.1 = (s32[256]{0:T(256)S(1)}, s32[256]{0:T(256)}, u32[]{:S(2)}) copy-start(s32[256]{0:T(256)} %constant.160) | copy-start | bytes 3076
  7.2 77.7 %copy-start.2 = (s32[256]{0:T(256)S(1)}, s32[256]{0:T(256)}, u32[]{:S(2)}) copy-start(s32[256]{0:T(256)} %constant.161) | copy-start | bytes 3076
  7.2 87.5 %all-gather.2.cloned.1.call-start = ((), (), s32[]{:S(2)}) async-start(), calls=%async_computation | async-start | bytes 3829760 | tf_op jit(solution)/shard_map/all_gather | solution.py:150
  83.3 7.2 %copy-start.22 = (pred[256]{0:T(512)(128)(4,1)S(1)}, pred[256]{0:T(512)(128)(4,1)}, u32[]{:S(2)}) copy-start(pred[256]{0:T(512)(128)(4,1)} %constant.110.clone) | copy-start | bytes 772
  83.3 7.2 %copy-start.8 = (pred[256]{0:T(512)(128)(4,1)S(1)}, pred[256]{0:T(512)(128)(4,1)}, u32[]{:S(2)}) copy-start(pred[256]{0:T(512)(128)(4,1)} %constant.94.clone) | copy-start | bytes 772
  83.3 7.2 %copy-start.9 = (pred[256]{0:T(512)(128)(4,1)S(1)}, pred[256]{0:T(512)(128)(4,1)}, u32[]{:S(2)}) copy-start(pred[256]{0:T(512)(128)(4,1)} %constant.96.clone) | copy-start | bytes 772
  83.3 7.2 %copy-start.10 = (pred[256]{0:T(512)(128)(4,1)S(1)}, pred[256]{0:T(512)(128)(4,1)}, u32[]{:S(2)}) copy-start(pred[256]{0:T(512)(128)(4,1)} %constant.97.clone) | copy-start | bytes 772
  83.3 7.2 %copy-start.11 = (pred[256]{0:T(512)(128)(4,1)S(1)}, pred[256]{0:T(512)(128)(4,1)}, u32[]{:S(2)}) copy-start(pred[256]{0:T(512)(128)(4,1)} %constant.98.clone) | copy-start | bytes 772
  83.3 7.2 %copy-start.4 = (pred[256]{0:T(512)(128)(4,1)S(1)}, pred[256]{0:T(512)(128)(4,1)}, u32[]{:S(2)}) copy-start(pred[256]{0:T(512)(128)(4,1)} %constant.101.clone) | copy-start | bytes 772
  83.3 7.2 %copy-start.5 = (pred[256]{0:T(512)(128)(4,1)S(1)}, pred[256]{0:T(512)(128)(4,1)}, u32[]{:S(2)}) copy-start(pred[256]{0:T(512)(128)(4,1)} %constant.102.clone) | copy-start | bytes 772
  83.4 7.2 %copy-start.6 = (pred[256]{0:T(512)(128)(4,1)S(1)}, pred[256]{0:T(512)(128)(4,1)}, u32[]{:S(2)}) copy-start(pred[256]{0:T(512)(128)(4,1)} %constant.103.clone) | copy-start | bytes 772
  83.4 7.2 %copy-start.7 = (pred[256]{0:T(512)(128)(4,1)S(1)}, pred[256]{0:T(512)(128)(4,1)}, u32[]{:S(2)}) copy-start(pred[256]{0:T(512)(128)(4,1)} %constant.99.clone) | copy-start | bytes 772
  83.4 7.2 %copy-start.17 = (pred[256]{0:T(512)(128)(4,1)S(1)}, pred[256]{0:T(512)(128)(4,1)}, u32[]{:S(2)}) copy-start(pred[256]{0:T(512)(128)(4,1)} %constant.88.clone) | copy-start | bytes 772
  83.4 7.2 %copy-start.18 = (pred[256]{0:T(512)(128)(4,1)S(1)}, pred[256]{0:T(512)(128)(4,1)}, u32[]{:S(2)}) copy-start(pred[256]{0:T(512)(128)(4,1)} %constant.90.clone) | copy-start | bytes 772
  83.4 7.2 %copy-start.19 = (pred[256]{0:T(512)(128)(4,1)S(1)}, pred[256]{0:T(512)(128)(4,1)}, u32[]{:S(2)}) copy-start(pred[256]{0:T(512)(128)(4,1)} %constant.91.clone) | copy-start | bytes 772
  83.4 7.2 %copy-start.20 = (pred[256]{0:T(512)(128)(4,1)S(1)}, pred[256]{0:T(512)(128)(4,1)}, u32[]{:S(2)}) copy-start(pred[256]{0:T(512)(128)(4,1)} %constant.92.clone) | copy-start | bytes 772
  83.4 7.2 %copy-start.21 = (pred[256]{0:T(512)(128)(4,1)S(1)}, pred[256]{0:T(512)(128)(4,1)}, u32[]{:S(2)}) copy-start(pred[256]{0:T(512)(128)(4,1)} %constant.93.clone) | copy-start | bytes 772
  83.4 7.2 %copy-start.12 = (pred[256]{0:T(512)(128)(4,1)S(1)}, pred[256]{0:T(512)(128)(4,1)}, u32[]{:S(2)}) copy-start(pred[256]{0:T(512)(128)(4,1)} %constant.104.clone) | copy-start | bytes 772
  83.5 7.2 %copy-start.13 = (pred[256]{0:T(512)(128)(4,1)S(1)}, pred[256]{0:T(512)(128)(4,1)}, u32[]{:S(2)}) copy-start(pred[256]{0:T(512)(128)(4,1)} %constant.106.clone) | copy-start | bytes 772
  83.5 7.2 %copy-start.14 = (pred[256]{0:T(512)(128)(4,1)S(1)}, pred[256]{0:T(512)(128)(4,1)}, u32[]{:S(2)}) copy-start(pred[256]{0:T(512)(128)(4,1)} %constant.107.clone) | copy-start | bytes 772
  83.5 7.2 %copy-start.15 = (pred[256]{0:T(512)(128)(4,1)S(1)}, pred[256]{0:T(512)(128)(4,1)}, u32[]{:S(2)}) copy-start(pred[256]{0:T(512)(128)(4,1)} %constant.108.clone) | copy-start | bytes 772
  83.5 7.2 %copy-start.16 = (pred[256]{0:T(512)(128)(4,1)S(1)}, pred[256]{0:T(512)(128)(4,1)}, u32[]{:S(2)}) copy-start(pred[256]{0:T(512)(128)(4,1)} %constant.109.clone) | copy-start | bytes 772
  83.5 7.3 %copy-start = (s32[640]{0:T(1024)S(1)}, s32[640]{0:T(1024)}, u32[]{:S(2)}) copy-start(s32[640]{0:T(1024)} %param.64) | copy-start | bytes 7684
  (1 other events, 7.2 us)
Sparse Core Ops, SparseCore 0:
  11.3 71.4 all-gather.1

commit v3 on v2

--- a/solution.py
+++ b/solution.py
@@ -1,5 +1,3 @@
-import functools
-
 import numpy as np
 import jax
 import jax.numpy as jnp
@@ -13,6 +11,7 @@
 NWIN = 20
 LANES = 128
 SPAN = 256
+ROW_TILE = 16
 
 
 EPSILON = 1e-05
@@ -65,12 +64,12 @@
 
 
 def window_masks(weight, frames):
+    padded = jnp.pad(weight, (0, SPAN))
     rows = []
     for n, (start, width) in enumerate(window_frames(frames)):
         local = np.arange(SPAN) + start
-        inside = (local >= STRIDE * n) & (local < STRIDE * n + WIN) & (local < frames)
-        idx = np.minimum(local, frames - 1)
-        rows.append(jnp.where(jnp.asarray(inside), weight[idx], 0.0))
+        inside = (local >= STRIDE * n) & (local < STRIDE * n + WIN)
+        rows.append(padded[start:start + SPAN] * inside.astype(np.float32))
     return jnp.stack(rows)
 
 
@@ -106,15 +105,12 @@
     disp_ref[...] = ((WIN - 3) * (second - first * first)).astype(disp_ref.dtype)
 
 
-def compare_rows(rows, weight, seed_window, seed_whole, block):
+def compare_rows(rows, m, mw, sw, sh, block):
     count, frames = rows.shape
-    seeds = seed_whole.shape[0]
-    sw, sh = seed_operands(seed_window, seed_whole, frames)
-    mw = window_masks(weight, frames)
+    seeds = sh.shape[1]
     steps = count // block
-    flops = 2 * count * seeds * (frames + NWIN * SPAN)
     cost = pl.CostEstimate(
-        flops=flops,
+        flops=2 * count * seeds * (frames + NWIN * SPAN),
         transcendentals=2 * count * seeds * (NWIN + 1),
         bytes_accessed=count * frames * 2 + sw.size * 2 + 2 * count * seeds * 2,
     )
@@ -136,7 +132,37 @@
         out_shape=[out, out],
         cost_estimate=cost,
         compiler_params=pltpu.CompilerParams(vmem_limit_bytes=48 * 1024 * 1024),
-    )(rows, weight[None, :], mw, sw, sh)
+    )(rows, m, mw, sw, sh)
+
+
+def doubling_gather(block, axis):
+    size = lax.axis_size(axis)
+    me = lax.axis_index(axis)
+    bits = size.bit_length() - 1
+    low = list(range(bits - 1))[::-1]
+    order = low + [bits - 1] if bits > 1 else [0]
+    held = block[None]
+    for bit in order:
+        stride = 1 << bit
+        route = [(i, i ^ stride) for i in range(size)]
+        other = lax.ppermute(held, axis, route)
+        mine_low = ((me >> bit) & 1) == 0
+        held = jnp.where(mine_low, jnp.stack([held, other]), jnp.stack([other, held]))
+    placed = order[::-1]
+    perm = [placed.index(bits - 1 - j) for j in range(bits)]
+    held = held.reshape((2,) * bits + block.shape)
+    held = jnp.transpose(held, perm + [bits + k for k in range(block.ndim)])
+    return held.reshape((size * block.shape[0],) + block.shape[1:])
+
+
+def row_chunks(row_count):
+    tiles = row_count // ROW_TILE
+    counts = [tiles // 2 + (1 if k < tiles % 2 else 0) for k in range(2)]
+    out, start = [], 0
+    for c in counts:
+        out.append((start * ROW_TILE, c * ROW_TILE))
+        start += c
+    return out
 
 
 def body(series, scrub_mask, seed_index):
@@ -144,13 +170,22 @@
     local_rows = seed_index % row_count
     own_seeds = jnp.take(series, local_rows, axis=0)
     weight = scrub_mask.astype(jnp.float32)
-    panel_rows = lax.all_gather(own_seeds, "wide", axis=0, tiled=True)
+    blocks = lax.axis_size("blk")
+    gathered = [
+        lax.all_gather(series[start:start + n], "blk", axis=0, tiled=True)
+        for start, n in row_chunks(row_count)
+    ]
+    panel_rows = doubling_gather(own_seeds, "wide")
     seed_window, seed_whole = prepare(panel_rows, scrub_mask)
-    blocks = lax.axis_size("blk")
-    gathered = lax.all_gather(series, "blk", axis=0, tiled=True)
-    dispersion, statistic = compare_rows(gathered, weight, seed_window, seed_whole, row_count)
-    shape = (blocks, row_count, panel_rows.shape[0])
-    return (dispersion.reshape(shape), statistic.reshape(shape))
+    sw, sh = seed_operands(seed_window, seed_whole, frames)
+    mw = window_masks(weight, frames)
+    seeds = panel_rows.shape[0]
+    parts_d, parts_s = [], []
+    for (start, n), rows in zip(row_chunks(row_count), gathered):
+        d, s = compare_rows(rows, weight[None, :], mw, sw, sh, n)
+        parts_d.append(d.reshape(blocks, n, seeds))
+        parts_s.append(s.reshape(blocks, n, seeds))
+    return (jnp.concatenate(parts_d, axis=1), jnp.concatenate(parts_s, axis=1))
 
 
 def solution(mesh):

time: 154 us -> 183 us (1.19); the launches traced: 154 us -> 181 us
  blocking collectives: 70.8 us -> 0 us
  waiting for transfers between devices: 0.7 us -> 63.3 us
  starting transfers between devices: 0.04 us -> 29.1 us
  other arithmetic: 5.62 us -> 10.2 us
  local copies, waits for them, and re-layouts: 9.61 us -> 12.5 us
    all_gather x1 -> x0, blocking collectives: 70.8 us -> none  [body(): panel_rows = lax.all_gather(own_seeds, 'wide', axis=0, tiled=True)]
    all_gather x1 -> x2, waiting for transfers between devices: 0.02 us -> 47.9 us  [body(): lax.all_gather(series[start:start + n], 'blk', axis=0, tiled=True)]
    ppermute x0 -> x5, starting transfers between devices: none -> 29 us  [doubling_gather(): other = lax.ppermute(held, axis, route)]
    ppermute x0 -> x5, waiting for transfers between devices: none -> 15.4 us  [doubling_gather(): other = lax.ppermute(held, axis, route)]
    gather x5 -> x0, local copies, waits for them, and re-layouts: 6.83 us -> none  [window_masks(): rows.append(jnp.where(jnp.asarray(inside), weight[idx], 0.0))]
    unnamed x67 -> x27, local copies, waits for them, and re-layouts: 0.41 us -> 6.48 us
    slice x0 -> x2, local copies, waits for them, and re-layouts: none -> 3.11 us  [body(): series[start:start + n]]
    mul x0 -> x3, other arithmetic: none -> 2.34 us  [window_masks(): rows.append(padded[start:start + SPAN] * inside.astype(np.float32))]
  transfers between devices with their start and end apart: 1 -> 7, of which waited for: 0 -> 6; matrix products, arithmetic and copies ran while one was open for 10% -> 7% of each run, Pallas kernels for 0% -> 13%
where the time goes in v3:
time: 183 us; the launch traced here: 181 us
  waiting for transfers between devices  63.3 us (35%)
  Pallas kernels  51 us (28%)
  starting transfers between devices  29.1 us (16%)
  between operations  14.5 us (8%)
  local copies, waits for them, and re-layouts  12.5 us (7%)
  other arithmetic  10.2 us (6%)
    pallas_call x2, Pallas kernels, compare_rows(): pl.pallas_call(compare_kernel, grid=(steps,), in_specs=[pl.BlockSpec((blo...  51 us
    all_gather x2, waiting for transfers between devices, body(): lax.all_gather(series[start:start + n], 'blk', axis=0, tiled=True)  47.9 us
    ppermute x5, starting transfers between devices, doubling_gather(): other = lax.ppermute(held, axis, route)  29 us
    ppermute x5, waiting for transfers between devices, doubling_gather(): other = lax.ppermute(held, axis, route)  15.4 us
    unnamed x27, local copies, waits for them, and re-layouts  6.48 us
  transfers between devices with their start and end apart: 7, of which 6 were waited for; matrix products, arithmetic and copies ran while one was open for 7% of the time, Pallas kernels for 13%

profile of v3, /device:TPU:24, one launch (start us, length us, event | category | flops | bytes accessed | tf_op | source)
XLA Modules:
  0.0 180.5 jit_solution(2878017728090842967)
XLA Ops:
  7.2 1.5 slice.161
  9.5 1.5 gather_fusion
  11.1 15.7 %collective-permute-start = (bf16[1,8,640]{2,1,0:T(8,128)(2,1)S(1)}, bf16[1,8,640]{2,1,0:T(8,128)(2,1)S(1)}, u32[]{:S(2)}, u32[]{:S(2)}) collective-permute-start(bf16[1,8,640]{2,1,0:T(8,128)(2,1)S(1)} %bitcast_select_fusion), channel_id=1, source_target_pairs={{0,8},{1,9},{2,10},{3,11},{4,12},{5,13},{6,14},{7,15},{8,0},{9,1},... | collective-permute-start | bytes 30728 | tf_op jit(solution)/shard_map/ppermute | solution.py:148
  26.9 1.6 slice.128
  30.2 0.8 fusion.8
  31.0 0.8 fusion.7
  31.9 4.3 %collective-permute-start.1 = (bf16[2,1,8,640]{3,2,1,0:T(8,128)(2,1)S(1)}, bf16[2,1,8,640]{3,2,1,0:T(8,128)(2,1)S(1)}, u32[]{:S(2)}, u32[]{:S(2)}) collective-permute-start(bf16[2,1,8,640]{3,2,1,0:T(8,128)(2,1)S(1)} %maximum_select_fusion.8), channel_id=1, source_target_pairs={{0,4},{1,5},{2,6},{3,7},{4,0},{5,1},{6,2},{7,3},{8,12},{9,13},{10,... | collective-permute-start | bytes 61448 | tf_op jit(solution)/shard_map/ppermute | solution.py:148
  36.2 5.4 %collective-permute-done.1 = bf16[2,1,8,640]{3,2,1,0:T(8,128)(2,1)S(1)} collective-permute-done((bf16[2,1,8,640]{3,2,1,0:T(8,128)(2,1)S(1)}, bf16[2,1,8,640]{3,2,1,0:T(8,128)(2,1)S(1)}, u32[]{:S(2)}, u32[]{:S(2)}) %collective-permute-start.1) | collective-permute-done | bytes 20512 | tf_op jit(solution)/shard_map/ppermute | solution.py:148
  41.7 3.2 %collective-permute-start.2 = (bf16[2,2,1,8,640]{4,3,1,2,0:T(8,128)(2,1)S(1)}, bf16[2,2,1,8,640]{4,3,1,2,0:T(8,128)(2,1)S(1)}, u32[]{:S(2)}, u32[]{:S(2)}) collective-permute-start(bf16[2,2,1,8,640]{4,3,1,2,0:T(8,128)(2,1)S(1)} %maximum_select_fusion.6), channel_id=1, source_target_pairs={{0,2},{1,3},{2,0},{3,1},{4,6},{5,7},{6,4},{7,5},{8,10},{9,11},{10,... | collective-permute-start | bytes 122888 | tf_op jit(solution)/shard_map/ppermute | solution.py:148
  44.9 4.0 %collective-permute-done.2 = bf16[2,2,1,8,640]{4,3,1,2,0:T(8,128)(2,1)S(1)} collective-permute-done((bf16[2,2,1,8,640]{4,3,1,2,0:T(8,128)(2,1)S(1)}, bf16[2,2,1,8,640]{4,3,1,2,0:T(8,128)(2,1)S(1)}, u32[]{:S(2)}, u32[]{:S(2)}) %collective-permute-start.2) | collective-permute-done | bytes 40992 | tf_op jit(solution)/shard_map/ppermute | solution.py:148
  48.9 2.4 %collective-permute-start.3 = (bf16[2,2,2,1,8,640]{5,4,2,1,3,0:T(8,128)(2,1)S(1)}, bf16[2,2,2,1,8,640]{5,4,2,1,3,0:T(8,128)(2,1)S(1)}, u32[]{:S(2)}, u32[]{:S(2)}) collective-permute-start(bf16[2,2,2,1,8,640]{5,4,2,1,3,0:T(8,128)(2,1)S(1)} %maximum_select_fusion.4), channel_id=1, source_target_pairs={{0,1},{1,0},{2,3},{3,2},{4,5},{5,4},{6,7},{7,6},{8,9},{9,8},{10,11... | collective-permute-start | bytes 245768 | tf_op jit(solution)/shard_map/ppermute | solution.py:148
  51.4 3.9 %collective-permute-done.3 = bf16[2,2,2,1,8,640]{5,4,2,1,3,0:T(8,128)(2,1)S(1)} collective-permute-done((bf16[2,2,2,1,8,640]{5,4,2,1,3,0:T(8,128)(2,1)S(1)}, bf16[2,2,2,1,8,640]{5,4,2,1,3,0:T(8,128)(2,1)S(1)}, u32[]{:S(2)}, u32[]{:S(2)}) %collective-permute-start.3) | collective-permute-done | bytes 81952 | tf_op jit(solution)/shard_map/ppermute | solution.py:148
  55.3 3.4 %collective-permute-start.4 = (bf16[2,2,2,2,1,8,640]{6,5,3,2,1,4,0:T(8,128)(2,1)S(1)}, bf16[2,2,2,2,1,8,640]{6,5,3,2,1,4,0:T(8,128)(2,1)S(1)}, u32[]{:S(2)}, u32[]{:S(2)}) collective-permute-start(bf16[2,2,2,2,1,8,640]{6,5,3,2,1,4,0:T(8,128)(2,1)S(1)} %maximum_select_fusion.2), channel_id=1, source_target_pairs={{0,16},{1,17},{2,18},{3,19},{4,20},{5,21},{6,22},{7,23},{8,24},{9,... | collective-permute-start | bytes 491528 | tf_op jit(solution)/shard_map/ppermute | solution.py:148
  58.7 1.4 convert_reduce_fusion
  60.4 2.1 %collective-permute-done.4 = bf16[2,2,2,2,1,8,640]{6,5,3,2,1,4,0:T(8,128)(2,1)S(1)} collective-permute-done((bf16[2,2,2,2,1,8,640]{6,5,3,2,1,4,0:T(8,128)(2,1)S(1)}, bf16[2,2,2,2,1,8,640]{6,5,3,2,1,4,0:T(8,128)(2,1)S(1)}, u32[]{:S(2)}, u32[]{:S(2)}) %collective-permute-start.4) | collective-permute-done | bytes 163872 | tf_op jit(solution)/shard_map/ppermute | solution.py:148
  66.6 1.5 copy-done
  68.3 9.0 %all-gather.5.cloned.1.call-done.x_ref = bf16[1280,640]{1,0:T(8,128)(2,1)} async-done(((bf16[80,640]{1,0:T(8,128)(2,1)}), bf16[1280,640]{1,0:T(8,128)(2,1)}) %all-gather.5.cloned.1.call-update) | async-done | bytes 1638416 | tf_op jit(solution)/shard_map/all_gather | solution.py:175
  77.3 1.7 copy-done.1
  79.0 1.4 copy-done.3
  80.4 23.2 %shard_map.231 = (bf16[1280,256]{1,0:T(8,128)(2,1)S(1)}, bf16[1280,256]{1,0:T(8,128)(2,1)S(1)}) custom-call(bf16[1280,640]{1,0:T(8,128)(2,1)S(1)} %copy-done.3, f32[1,640]{1,0:T(1,128)S(1)} %broadcast_in_dim.14.m_ref, f32[20,256]{1,0:T(8,128)S(1)} %stack.240.mw_ref, bf16[20,256,256]{2,1,0:T(8,128)(2,1)S(1)} %copy-done.1, bf16[640,256]{1,0:T(8,128)(2,1)S(1)} %fusion.sh_ref), custom_call_target="tpu_custom_call" | custom-call | flops 3774873600 | bytes 5570560 | tf_op jit(solution)/shard_map/pallas_call | solution.py:118
  103.7 38.9 %all-gather.3.cloned.1.call-done.x_ref = bf16[1536,640]{1,0:T(8,128)(2,1)} async-done(((bf16[96,640]{1,0:T(8,128)(2,1)}), bf16[1536,640]{1,0:T(8,128)(2,1)}) %all-gather.3.cloned.1.call-update) | async-done | bytes 1966096 | tf_op jit(solution)/shard_map/all_gather | solution.py:175
  142.6 1.5 copy-done.2
  144.2 27.7 %shard_map.230 = (bf16[1536,256]{1,0:T(8,128)(2,1)S(1)}, bf16[1536,256]{1,0:T(8,128)(2,1)S(1)}) custom-call(bf16[1536,640]{1,0:T(8,128)(2,1)S(1)} %copy-done.2, f32[1,640]{1,0:T(1,128)S(1)} %broadcast_in_dim.14.m_ref, f32[20,256]{1,0:T(8,128)S(1)} %stack.240.mw_ref, bf16[20,256,256]{2,1,0:T(8,128)(2,1)} %copy-done, bf16[640,256]{1,0:T(8,128)(2,1)S(1)} %fusion.sh_ref), custom_call_target="tpu_custom_call" | custom-call | flops 4529848320 | bytes 6160384 | tf_op jit(solution)/shard_map/pallas_call | solution.py:118
  171.9 1.8 pad_maximum_fusion
  (74 shorter events, 7.1 us)
Async XLA Ops:
  7.2 70.1 %all-gather.5.cloned.1.call-start = ((), (), s32[]{:S(2)}) async-start(), calls=%async_computation.1 | async-start | bytes 1740800 | tf_op jit(solution)/shard_map/all_gather | solution.py:175
  8.8 133.9 %all-gather.3.cloned.1.call-start = ((), (), s32[]{:S(2)}) async-start(), calls=%async_computation | async-start | bytes 2088960 | tf_op jit(solution)/shard_map/all_gather | solution.py:175
  11.1 20.7 %collective-permute-start = (bf16[1,8,640]{2,1,0:T(8,128)(2,1)S(1)}, bf16[1,8,640]{2,1,0:T(8,128)(2,1)S(1)}, u32[]{:S(2)}, u32[]{:S(2)}) collective-permute-start(bf16[1,8,640]{2,1,0:T(8,128)(2,1)S(1)} %bitcast_select_fusion), channel_id=1, source_target_pairs={{0,8},{1,9},{2,10},{3,11},{4,12},{5,13},{6,14},{7,15},{8,0},{9,1},... | collective-permute-start | bytes 30728 | tf_op jit(solution)/shard_map/ppermute | solution.py:148
  31.9 9.8 %collective-permute-start.1 = (bf16[2,1,8,640]{3,2,1,0:T(8,128)(2,1)S(1)}, bf16[2,1,8,640]{3,2,1,0:T(8,128)(2,1)S(1)}, u32[]{:S(2)}, u32[]{:S(2)}) collective-permute-start(bf16[2,1,8,640]{3,2,1,0:T(8,128)(2,1)S(1)} %maximum_select_fusion.8), channel_id=1, source_target_pairs={{0,4},{1,5},{2,6},{3,7},{4,0},{5,1},{6,2},{7,3},{8,12},{9,13},{10,... | collective-permute-start | bytes 61448 | tf_op jit(solution)/shard_map/ppermute | solution.py:148
  41.7 7.2 %collective-permute-start.2 = (bf16[2,2,1,8,640]{4,3,1,2,0:T(8,128)(2,1)S(1)}, bf16[2,2,1,8,640]{4,3,1,2,0:T(8,128)(2,1)S(1)}, u32[]{:S(2)}, u32[]{:S(2)}) collective-permute-start(bf16[2,2,1,8,640]{4,3,1,2,0:T(8,128)(2,1)S(1)} %maximum_select_fusion.6), channel_id=1, source_target_pairs={{0,2},{1,3},{2,0},{3,1},{4,6},{5,7},{6,4},{7,5},{8,10},{9,11},{10,... | collective-permute-start | bytes 122888 | tf_op jit(solution)/shard_map/ppermute | solution.py:148
  48.9 6.3 %collective-permute-start.3 = (bf16[2,2,2,1,8,640]{5,4,2,1,3,0:T(8,128)(2,1)S(1)}, bf16[2,2,2,1,8,640]{5,4,2,1,3,0:T(8,128)(2,1)S(1)}, u32[]{:S(2)}, u32[]{:S(2)}) collective-permute-start(bf16[2,2,2,1,8,640]{5,4,2,1,3,0:T(8,128)(2,1)S(1)} %maximum_select_fusion.4), channel_id=1, source_target_pairs={{0,1},{1,0},{2,3},{3,2},{4,5},{5,4},{6,7},{7,6},{8,9},{9,8},{10,11... | collective-permute-start | bytes 245768 | tf_op jit(solution)/shard_map/ppermute | solution.py:148
  55.3 7.2 %collective-permute-start.4 = (bf16[2,2,2,2,1,8,640]{6,5,3,2,1,4,0:T(8,128)(2,1)S(1)}, bf16[2,2,2,2,1,8,640]{6,5,3,2,1,4,0:T(8,128)(2,1)S(1)}, u32[]{:S(2)}, u32[]{:S(2)}) collective-permute-start(bf16[2,2,2,2,1,8,640]{6,5,3,2,1,4,0:T(8,128)(2,1)S(1)} %maximum_select_fusion.2), channel_id=1, source_target_pairs={{0,16},{1,17},{2,18},{3,19},{4,20},{5,21},{6,22},{7,23},{8,24},{9,... | collective-permute-start | bytes 491528 | tf_op jit(solution)/shard_map/ppermute | solution.py:148
  66.6 1.5 copy-start
  77.3 1.7 copy-start.1
  79.0 1.4 copy-start.3
  142.6 1.5 copy-start.2
Sparse Core Ops, SparseCore 0:
  11.8 65.4 all-gather.4
  81.2 61.4 all-gather.2

commit v4 on v3

--- a/solution.py
+++ b/solution.py
@@ -146,8 +146,17 @@
         stride = 1 << bit
         route = [(i, i ^ stride) for i in range(size)]
         other = lax.ppermute(held, axis, route)
-        mine_low = ((me >> bit) & 1) == 0
-        held = jnp.where(mine_low, jnp.stack([held, other]), jnp.stack([other, held]))
+        held = place_pair(held, other, me, bit)
+    return unpermute(held, order, size, block)
+
+
+def place_pair(held, other, me, bit):
+    mine_low = ((me >> bit) & 1) == 0
+    return jnp.where(mine_low, jnp.stack([held, other]), jnp.stack([other, held]))
+
+
+def unpermute(held, order, size, block):
+    bits = len(order)
     placed = order[::-1]
     perm = [placed.index(bits - 1 - j) for j in range(bits)]
     held = held.reshape((2,) * bits + block.shape)
@@ -155,14 +164,8 @@
     return held.reshape((size * block.shape[0],) + block.shape[1:])
 
 
-def row_chunks(row_count):
-    tiles = row_count // ROW_TILE
-    counts = [tiles // 2 + (1 if k < tiles % 2 else 0) for k in range(2)]
-    out, start = [], 0
-    for c in counts:
-        out.append((start * ROW_TILE, c * ROW_TILE))
-        start += c
-    return out
+BLK_AXES = ("x_hi", "y", "core")
+WIDE_AXES = ("x_lo", "z")
 
 
 def body(series, scrub_mask, seed_index):
@@ -170,25 +173,49 @@
     local_rows = seed_index % row_count
     own_seeds = jnp.take(series, local_rows, axis=0)
     weight = scrub_mask.astype(jnp.float32)
-    blocks = lax.axis_size("blk")
-    gathered = [
-        lax.all_gather(series[start:start + n], "blk", axis=0, tiled=True)
-        for start, n in row_chunks(row_count)
-    ]
-    panel_rows = doubling_gather(own_seeds, "wide")
+    panel_rows = lax.all_gather(own_seeds, "z", axis=0, tiled=True)
+    panel_rows = lax.all_gather(panel_rows, "x_lo", axis=0, tiled=True)
     seed_window, seed_whole = prepare(panel_rows, scrub_mask)
     sw, sh = seed_operands(seed_window, seed_whole, frames)
     mw = window_masks(weight, frames)
+    m = weight[None, :]
     seeds = panel_rows.shape[0]
-    parts_d, parts_s = [], []
-    for (start, n), rows in zip(row_chunks(row_count), gathered):
-        d, s = compare_rows(rows, weight[None, :], mw, sw, sh, n)
-        parts_d.append(d.reshape(blocks, n, seeds))
-        parts_s.append(s.reshape(blocks, n, seeds))
-    return (jnp.concatenate(parts_d, axis=1), jnp.concatenate(parts_s, axis=1))
+    size = 1
+    for a in BLK_AXES:
+        size *= lax.axis_size(a)
+    me = lax.axis_index(BLK_AXES)
+    bits = size.bit_length() - 1
+    order = list(range(bits))[::-1]
+
+    def run(rows):
+        count = rows.shape[0] * rows.shape[1]
+        d, s = compare_rows(rows.reshape(count, frames), m, mw, sw, sh, row_count)
+        return d.reshape(rows.shape[0], row_count, seeds), s.reshape(rows.shape[0], row_count, seeds)
+
+    held = series[None]
+    held_d, held_s = run(held)
+    for bit in order:
+        stride = 1 << bit
+        route = [(i, i ^ stride) for i in range(size)]
+        other = lax.ppermute(held, BLK_AXES, route)
+        other_d, other_s = run(other)
+        held = place_pair(held, other, me, bit)
+        held_d = place_pair(held_d, other_d, me, bit)
+        held_s = place_pair(held_s, other_s, me, bit)
+        shape = (-1,) + series.shape
+        held = held.reshape(shape)
+        held_d = held_d.reshape((-1, row_count, seeds))
+        held_s = held_s.reshape((-1, row_count, seeds))
+    out_block = jnp.zeros((row_count, seeds), jnp.bfloat16)
+    dispersion = unpermute(held_d.reshape((2,) * bits + (row_count, seeds)), order, size, out_block)
+    statistic = unpermute(held_s.reshape((2,) * bits + (row_count, seeds)), order, size, out_block)
+    return (dispersion.reshape(size, row_count, seeds), statistic.reshape(size, row_count, seeds))
 
 
 def solution(mesh):
-    in_specs = (P(("blk", "wide"), None), P(), P(("blk", "wide")))
-    out_specs = (P(None, "wide", "blk"), P(None, "wide", "blk"))
-    return jax.shard_map(body, mesh=mesh, in_specs=in_specs, out_specs=out_specs, check_vma=False)
+    from jax.sharding import Mesh
+    split = Mesh(mesh.devices.reshape(2, 4, 2, 2, 16), BLK_AXES + WIDE_AXES)
+    every = BLK_AXES + WIDE_AXES
+    in_specs = (P(every, None), P(), P(every))
+    out_specs = (P(None, WIDE_AXES, BLK_AXES), P(None, WIDE_AXES, BLK_AXES))
+    return jax.shard_map(body, mesh=split, in_specs=in_specs, out_specs=out_specs, check_vma=False)

time: 183 us -> 158 us (0.86)
  blocking collectives: 0 us -> 42.3 us
  waiting for transfers between devices: 63.3 us -> 22.5 us
  starting transfers between devices: 29.1 us -> 12.6 us
  between operations: 14.5 us -> 1.1 us
  local copies, waits for them, and re-layouts: 12.5 us -> 17 us
    all_gather x2 -> x0, waiting for transfers between devices: 47.9 us -> none  [body(): lax.all_gather(series[start:start + n], 'blk', axis=0, tiled=True)]
    all_gather x0 -> x2, blocking collectives: none -> 42.3 us  [the longest x1 36.3 us: body(): panel_rows = lax.all_gather(own_seeds, 'z', axis=0, tiled=True)]
    ppermute x5 -> x4, starting transfers between devices: 29 us -> 12.6 us  [body(): other = lax.ppermute(held, BLK_AXES, route)]
    ppermute x5 -> x4, waiting for transfers between devices: 15.4 us -> 22.5 us  [body(): other = lax.ppermute(held, BLK_AXES, route)]
    slice x2 -> x0, local copies, waits for them, and re-layouts: 3.11 us -> none  [body(): series[start:start + n]]
    unnamed x27 -> x35, local copies, waits for them, and re-layouts: 6.48 us -> 9.41 us
    transpose x0 -> x2, local copies, waits for them, and re-layouts: none -> 2.41 us  [unpermute(): held = jnp.transpose(held, perm + [bits + k for k in range(block.ndim)])]
    another operation x1, local copies, waits for them, and re-layouts: 0.08 us -> 2.14 us  [window_masks(): return jnp.stack(rows)]
  transfers between devices with their start and end apart: 7 -> 4, of which waited for: 6 -> 2; matrix products, arithmetic and copies ran while one was open for 7% -> 15% of each run, Pallas kernels for 13% -> 16%
where the time goes in v4:
time: 158 us; the launch traced here: 156 us
  Pallas kernels  50.8 us (32%)
  blocking collectives  42.3 us (27%)
  waiting for transfers between devices  22.5 us (14%)
  local copies, waits for them, and re-layouts  17 us (11%)
  starting transfers between devices  12.6 us (8%)
  other arithmetic  9.92 us (6%)
    pallas_call x5, Pallas kernels, compare_rows(): pl.pallas_call(compare_kernel, grid=(steps,), in_specs=[pl.BlockSpec((blo...  50.8 us
    all_gather x1, blocking collectives, body(): panel_rows = lax.all_gather(own_seeds, 'z', axis=0, tiled=True)  36.3 us
    ppermute x4, waiting for transfers between devices, body(): other = lax.ppermute(held, BLK_AXES, route)  22.5 us
    ppermute x4, starting transfers between devices, body(): other = lax.ppermute(held, BLK_AXES, route)  12.6 us
    unnamed x35, local copies, waits for them, and re-layouts  9.41 us
    all_gather x1, blocking collectives, body(): panel_rows = lax.all_gather(panel_rows, 'x_lo', axis=0, tiled=True)  6.01 us
    mul x3, other arithmetic, window_masks(): rows.append(padded[start:start + SPAN] * inside.astype(np.float32))  3.41 us
  transfers between devices with their start and end apart: 4, of which 2 were waited for; matrix products, arithmetic and copies ran while one was open for 15% of the time, Pallas kernels for 16%

profile of v4, /device:TPU:24, one launch (start us, length us, event | category | flops | bytes accessed | tf_op | source)
XLA Modules:
  0.0 156.3 jit_solution(9996113518096338952)
XLA Ops:
  0.6 4.9 %collective-permute-start = (bf16[1,176,640]{2,1,0:T(8,128)(2,1)}, bf16[1,176,640]{2,1,0:T(8,128)(2,1)S(1)}, u32[]{:S(2)}, u32[]{:S(2)}) collective-permute-start(bf16[1,176,640]{2,1,0:T(8,128)(2,1)} %bitcast.180), channel_id=1, source_target_pairs={{0,256},{32,288},{64,320},{96,352},{128,384},{160,416},{192,448},{... | collective-permute-start | bytes 675848 | tf_op jit(solution)/shard_map/ppermute | solution.py:200
  7.5 1.5 gather_fusion
  9.1 36.3 %all_gather.6 = bf16[128,640]{1,0:T(8,128)(2,1)S(1)} all-gather(bf16[8,640]{1,0:T(8,128)(2,1)S(1)} %broadcast_select_fusion), channel_id=1, replica_groups=mesh['x_hi'=2,'y'=4,'core'=2,'x_lo'=2,'z'=16] {'z'}, dimensions={0}, use_global_device_ids=true | all-gather | bytes 174080 | tf_op jit(solution)/shard_map/all_gather | solution.py:176
  45.6 6.0 %all_gather.7 = bf16[256,640]{0,1:T(8,128)(2,1)S(1)} all-gather(bf16[128,640]{0,1:T(8,128)(2,1)S(1)} %copy.29), channel_id=1, replica_groups=mesh['x_hi'=2,'y'=4,'core'=2,'x_lo'=2,'z'=16] {'x_lo'}, dimensions={0}, use_global_device_ids=true | all-gather | bytes 491520 | tf_op jit(solution)/shard_map/all_gather | solution.py:177
  53.3 0.8 slice_bitcast_fusion
  54.2 0.8 bitcast_dynamic-update-slice_fusion.18
  54.9 0.8 bitcast_dynamic-update-slice_fusion.17
  57.3 0.8 bitcast_dynamic-update-slice_fusion.14
  60.2 1.4 fusion.8
  61.6 1.4 fusion.7
  63.0 2.1 %stack.258.mw_ref = f32[20,256]{1,0:T(8,128)S(1)} concatenate(f32[1,256]{1,0:T(1,128)} %bitcast.215, f32[1,256]{1,0:T(1,128)} %bitcast.222, f32[1,256]{1,0:T(1,128)S(1)} %bitcast.206, f32[1,256]{1,0:T(1,128)S(1)} %bitcast.207, f32[1,256]{1,0:T(1,128)S(1)} %bitcast.208, f32[1,256]{1,0:T(1,128)} %bitcast.214, f32[1,256]{1,0:T(1,128)} %bitcast.213, f32[1,256]{1,0:T(1,128)} %bitcast.217, ...), dimensions={0} | concatenate | bytes 40960 | tf_op jit(solution)/shard_map/stack | solution.py:73
  65.2 0.8 bitcast_dynamic-update-slice_fusion.10
  66.9 3.1 %collective-permute-start.1 = (bf16[2,176,640]{2,1,0:T(8,128)(2,1)S(1)}, bf16[2,176,640]{2,1,0:T(8,128)(2,1)S(1)}, u32[]{:S(2)}, u32[]{:S(2)}) collective-permute-start(bf16[2,176,640]{2,1,0:T(8,128)(2,1)S(1)} %maximum_select_fusion.6), channel_id=1, source_target_pairs={{0,128},{32,160},{64,192},{96,224},{128,0},{160,32},{192,64},{224,... | collective-permute-start | bytes 1351688 | tf_op jit(solution)/shard_map/ppermute | solution.py:200
  72.4 11.1 %collective-permute-done.1 = bf16[2,176,640]{2,1,0:T(8,128)(2,1)S(1)} collective-permute-done((bf16[2,176,640]{2,1,0:T(8,128)(2,1)S(1)}, bf16[2,176,640]{2,1,0:T(8,128)(2,1)S(1)}, u32[]{:S(2)}, u32[]{:S(2)}) %collective-permute-start.1) | collective-permute-done | bytes 450592 | tf_op jit(solution)/shard_map/ppermute | solution.py:200
  83.7 2.6 %collective-permute-start.2 = (bf16[4,176,640]{2,1,0:T(8,128)(2,1)S(1)}, bf16[4,176,640]{2,1,0:T(8,128)(2,1)S(1)}, u32[]{:S(2)}, u32[]{:S(2)}) collective-permute-start(bf16[4,176,640]{2,1,0:T(8,128)(2,1)S(1)} %bitcast.200), channel_id=1, source_target_pairs={{0,64},{32,96},{64,0},{96,32},{128,192},{160,224},{192,128},{224,1... | collective-permute-start | bytes 2703368 | tf_op jit(solution)/shard_map/ppermute | solution.py:200
  87.3 11.5 %collective-permute-done.2 = bf16[4,176,640]{2,1,0:T(8,128)(2,1)S(1)} collective-permute-done((bf16[4,176,640]{2,1,0:T(8,128)(2,1)S(1)}, bf16[4,176,640]{2,1,0:T(8,128)(2,1)S(1)}, u32[]{:S(2)}, u32[]{:S(2)}) %collective-permute-start.2) | collective-permute-done | bytes 901152 | tf_op jit(solution)/shard_map/ppermute | solution.py:200
  99.1 1.9 %collective-permute-start.3 = (bf16[8,176,640]{2,1,0:T(8,128)(2,1)S(1)}, bf16[8,176,640]{2,1,0:T(8,128)(2,1)S(1)}, u32[]{:S(2)}, u32[]{:S(2)}) collective-permute-start(bf16[8,176,640]{2,1,0:T(8,128)(2,1)S(1)} %bitcast.202), channel_id=1, source_target_pairs={{0,32},{32,0},{64,96},{96,64},{128,160},{160,128},{192,224},{224,1... | collective-permute-start | bytes 5406728 | tf_op jit(solution)/shard_map/ppermute | solution.py:200
  102.1 3.1 %shard_map.230 = (bf16[176,256]{1,0:T(8,128)(2,1)S(1)}, bf16[176,256]{1,0:T(8,128)(2,1)S(1)}) custom-call(bf16[176,640]{1,0:T(8,128)(2,1)S(1)} %copy-done, f32[1,640]{1,0:T(1,128)S(1)} %broadcast_in_dim.16.m_ref, f32[20,256]{1,0:T(8,128)S(1)} %stack.258.mw_ref, bf16[20,256,256]{2,1,0:T(8,128)(2,1)S(1)} %bitcast_dynamic-update-slice_fusion.sw_ref, ...), custom_call_target="tpu_custom_call" | custom-call | flops 519045120 | bytes 3026944 | tf_op jit(solution)/shard_map/pallas_call | solution.py:118
  105.2 3.1 %shard_map.231 = (bf16[176,256]{1,0:T(8,128)(2,1)S(1)}, bf16[176,256]{1,0:T(8,128)(2,1)S(1)}) custom-call(bf16[176,640]{1,0:T(8,128)(2,1)S(1)} %bitcast.184, f32[1,640]{1,0:T(1,128)S(1)} %broadcast_in_dim.16.m_ref, f32[20,256]{1,0:T(8,128)S(1)} %stack.258.mw_ref, bf16[20,256,256]{2,1,0:T(8,128)(2,1)S(1)} %bitcast_dynamic-update-slice_fusion.sw_ref, ...), custom_call_target="tpu_custom_call" | custom-call | flops 519045120 | bytes 3026944 | tf_op jit(solution)/shard_map/pallas_call | solution.py:118
  108.4 6.5 %shard_map.232 = (bf16[352,256]{1,0:T(8,128)(2,1)S(1)}, bf16[352,256]{1,0:T(8,128)(2,1)S(1)}) custom-call(bf16[352,640]{1,0:T(8,128)(2,1)S(1)} %bitcast.190, f32[1,640]{1,0:T(1,128)S(1)} %broadcast_in_dim.16.m_ref, f32[20,256]{1,0:T(8,128)S(1)} %stack.258.mw_ref, bf16[20,256,256]{2,1,0:T(8,128)(2,1)S(1)} %bitcast_dynamic-update-slice_fusion.sw_ref, ...), custom_call_target="tpu_custom_call" | custom-call | flops 1038090240 | bytes 3432448 | tf_op jit(solution)/shard_map/pallas_call | solution.py:118
  115.1 12.7 %shard_map.233 = (bf16[704,256]{1,0:T(8,128)(2,1)S(1)}, bf16[704,256]{1,0:T(8,128)(2,1)S(1)}) custom-call(bf16[704,640]{1,0:T(8,128)(2,1)S(1)} %bitcast.186, f32[1,640]{1,0:T(1,128)S(1)} %broadcast_in_dim.16.m_ref, f32[20,256]{1,0:T(8,128)S(1)} %stack.258.mw_ref, bf16[20,256,256]{2,1,0:T(8,128)(2,1)S(1)} %bitcast_dynamic-update-slice_fusion.sw_ref, ...), custom_call_target="tpu_custom_call" | custom-call | flops 2076180480 | bytes 4243456 | tf_op jit(solution)/shard_map/pallas_call | solution.py:118
  128.0 25.3 %shard_map.234 = (bf16[1408,256]{1,0:T(8,128)(2,1)S(1)}, bf16[1408,256]{1,0:T(8,128)(2,1)S(1)}) custom-call(bf16[1408,640]{1,0:T(8,128)(2,1)S(1)} %bitcast.199, f32[1,640]{1,0:T(1,128)S(1)} %broadcast_in_dim.16.m_ref, f32[20,256]{1,0:T(8,128)S(1)} %stack.258.mw_ref, bf16[20,256,256]{2,1,0:T(8,128)(2,1)S(1)} %bitcast_dynamic-update-slice_fusion.sw_ref, ...), custom_call_target="tpu_custom_call" | custom-call | flops 4152360960 | bytes 5865472 | tf_op jit(solution)/shard_map/pallas_call | solution.py:118
  153.6 1.2 copy.31
  155.0 1.2 copy.30
  (74 shorter events, 14.1 us)
Async XLA Ops:
  0.6 66.1 %collective-permute-start = (bf16[1,176,640]{2,1,0:T(8,128)(2,1)}, bf16[1,176,640]{2,1,0:T(8,128)(2,1)S(1)}, u32[]{:S(2)}, u32[]{:S(2)}) collective-permute-start(bf16[1,176,640]{2,1,0:T(8,128)(2,1)} %bitcast.180), channel_id=1, source_target_pairs={{0,256},{32,288},{64,320},{96,352},{128,384},{160,416},{192,448},{... | collective-permute-start | bytes 675848 | tf_op jit(solution)/shard_map/ppermute | solution.py:200
  52.8 6.8 %copy-start.5 = (f32[256]{0:T(256)S(1)}, f32[256]{0:T(256)}, u32[]{:S(2)}) copy-start(f32[256]{0:T(256)} %constant.104.clone) | copy-start | bytes 3076
  52.8 6.8 %copy-start.6 = (f32[256]{0:T(256)S(1)}, f32[256]{0:T(256)}, u32[]{:S(2)}) copy-start(f32[256]{0:T(256)} %constant.99.clone) | copy-start | bytes 3076
  52.8 7.4 %copy-start.7 = (f32[256]{0:T(256)S(1)}, f32[256]{0:T(256)}, u32[]{:S(2)}) copy-start(f32[256]{0:T(256)} %constant.100.clone) | copy-start | bytes 3076
  52.9 13.9 %copy-start = (bf16[176,640]{1,0:T(8,128)(2,1)S(1)}, bf16[176,640]{1,0:T(8,128)(2,1)}, u32[]{:S(2)}) copy-start(bf16[176,640]{1,0:T(8,128)(2,1)} %x_ref.1) | copy-start | bytes 675844
  57.2 29.1 %copy-start.4 = (s32[640]{0:T(1024)S(1)}, s32[640]{0:T(1024)}, u32[]{:S(2)}) copy-start(s32[640]{0:T(1024)} %param.24) | copy-start | bytes 7684
  65.2 21.8 %copy-start.3 = (bf16[256,60]{0,1:T(8,128)(2,1)S(1)}, bf16[256,60]{0,1:T(8,128)(2,1)}, u32[]{:S(2)}) copy-start(bf16[256,60]{0,1:T(8,128)(2,1)} %get-tuple-element.31) | copy-start | bytes 92164
  65.2 21.8 %copy-start.2 = (bf16[256,60]{0,1:T(8,128)(2,1)S(1)}, bf16[256,60]{0,1:T(8,128)(2,1)}, u32[]{:S(2)}) copy-start(bf16[256,60]{0,1:T(8,128)(2,1)} %get-tuple-element.30) | copy-start | bytes 92164
  65.2 21.9 %copy-start.1 = (bf16[256,60]{0,1:T(8,128)(2,1)S(1)}, bf16[256,60]{0,1:T(8,128)(2,1)}, u32[]{:S(2)}) copy-start(bf16[256,60]{0,1:T(8,128)(2,1)} %get-tuple-element.29) | copy-start | bytes 92164
  66.9 16.6 %collective-permute-start.1 = (bf16[2,176,640]{2,1,0:T(8,128)(2,1)S(1)}, bf16[2,176,640]{2,1,0:T(8,128)(2,1)S(1)}, u32[]{:S(2)}, u32[]{:S(2)}) collective-permute-start(bf16[2,176,640]{2,1,0:T(8,128)(2,1)S(1)} %maximum_select_fusion.6), channel_id=1, source_target_pairs={{0,128},{32,160},{64,192},{96,224},{128,0},{160,32},{192,64},{224,... | collective-permute-start | bytes 1351688 | tf_op jit(solution)/shard_map/ppermute | solution.py:200
  83.7 15.1 %collective-permute-start.2 = (bf16[4,176,640]{2,1,0:T(8,128)(2,1)S(1)}, bf16[4,176,640]{2,1,0:T(8,128)(2,1)S(1)}, u32[]{:S(2)}, u32[]{:S(2)}) collective-permute-start(bf16[4,176,640]{2,1,0:T(8,128)(2,1)S(1)} %bitcast.200), channel_id=1, source_target_pairs={{0,64},{32,96},{64,0},{96,32},{128,192},{160,224},{192,128},{224,1... | collective-permute-start | bytes 2703368 | tf_op jit(solution)/shard_map/ppermute | solution.py:200
  99.1 28.9 %collective-permute-start.3 = (bf16[8,176,640]{2,1,0:T(8,128)(2,1)S(1)}, bf16[8,176,640]{2,1,0:T(8,128)(2,1)S(1)}, u32[]{:S(2)}, u32[]{:S(2)}) collective-permute-start(bf16[8,176,640]{2,1,0:T(8,128)(2,1)S(1)} %bitcast.202), channel_id=1, source_target_pairs={{0,32},{32,0},{64,96},{96,64},{128,160},{160,128},{192,224},{224,1... | collective-permute-start | bytes 5406728 | tf_op jit(solution)/shard_map/ppermute | solution.py:200

commit v5 on v4

--- a/solution.py
+++ b/solution.py
@@ -27,7 +27,8 @@
     out = []
     for n in range(NWIN):
         start = LANES * ((STRIDE * n) // LANES)
-        out.append((start, min(SPAN, frames - start)))
+        width = LANES if STRIDE * n - start + WIN <= LANES else SPAN
+        out.append((start, min(width, frames - start)))
     return out
 
 
@@ -71,6 +72,11 @@
         inside = (local >= STRIDE * n) & (local < STRIDE * n + WIN)
         rows.append(padded[start:start + SPAN] * inside.astype(np.float32))
     return jnp.stack(rows)
+
+
+def fisher_ratio(values):
+    clipped = jnp.clip(values, -CLIP_LEVEL, CLIP_LEVEL)
+    return 0.5 * jnp.log((1.0 + clipped) / (1.0 - clipped))
 
 
 def compare_kernel(x_ref, m_ref, mw_ref, sw_ref, sh_ref, disp_ref, stat_ref):
@@ -95,7 +101,7 @@
         sp = jnp.sum(cw * cw, axis=1, keepdims=True)
         w = (cw * lax.rsqrt(sp + EPSILON)).astype(jnp.bfloat16)
         r = jnp.dot(w, sw_ref[n, :width, :], preferred_element_type=jnp.float32)
-        z = fisher_of(r)
+        z = fisher_ratio(r)
         if first is None:
             first, second = z, z * z
         else:
@@ -193,19 +199,21 @@
         return d.reshape(rows.shape[0], row_count, seeds), s.reshape(rows.shape[0], row_count, seeds)
 
     held = series[None]
-    held_d, held_s = run(held)
-    for bit in order:
+    outs = [run(held)]
+    for idx, bit in enumerate(order):
         stride = 1 << bit
         route = [(i, i ^ stride) for i in range(size)]
+        if idx > 0:
+            held, prev_d, prev_s = lax.optimization_barrier((held,) + outs[idx - 1])
+            outs[idx - 1] = (prev_d, prev_s)
         other = lax.ppermute(held, BLK_AXES, route)
-        other_d, other_s = run(other)
-        held = place_pair(held, other, me, bit)
-        held_d = place_pair(held_d, other_d, me, bit)
-        held_s = place_pair(held_s, other_s, me, bit)
-        shape = (-1,) + series.shape
-        held = held.reshape(shape)
-        held_d = held_d.reshape((-1, row_count, seeds))
-        held_s = held_s.reshape((-1, row_count, seeds))
+        outs.append(run(other))
+        held = place_pair(held, other, me, bit).reshape((-1,) + series.shape)
+    held_d, held_s = outs[0]
+    for idx, bit in enumerate(order):
+        other_d, other_s = outs[idx + 1]
+        held_d = place_pair(held_d, other_d, me, bit).reshape((-1, row_count, seeds))
+        held_s = place_pair(held_s, other_s, me, bit).reshape((-1, row_count, seeds))
     out_block = jnp.zeros((row_count, seeds), jnp.bfloat16)
     dispersion = unpermute(held_d.reshape((2,) * bits + (row_count, seeds)), order, size, out_block)
     statistic = unpermute(held_s.reshape((2,) * bits + (row_count, seeds)), order, size, out_block)

time: 158 us -> 161 us (1.019)
  local copies, waits for them, and re-layouts: 17 us -> 29.8 us
  waiting for transfers between devices: 22.5 us -> 13.3 us
  Pallas kernels: 50.8 us -> 48.5 us
    unnamed x35 -> x37, local copies, waits for them, and re-layouts: 9.41 us -> 22.3 us
    ppermute x4, waiting for transfers between devices: 22.5 us -> 13.3 us  [body(): other = lax.ppermute(held, BLK_AXES, route)]
    pallas_call x5, Pallas kernels: 50.8 us -> 48.5 us  [compare_rows(): pl.pallas_call(compare_kernel, grid=(steps,), in_specs=[pl.BlockSpec((blo...]
  transfers between devices with their start and end apart: 4 -> 4, of which waited for: 2 -> 2; matrix products, arithmetic and copies ran while one was open for 15% -> 16% of each run, Pallas kernels for 16% -> 15%
where the time goes in v5:
time: 161 us; the launch traced here: 158 us
  Pallas kernels  48.5 us (30%)
  blocking collectives  42.3 us (26%)
  local copies, waits for them, and re-layouts  29.8 us (19%)
  waiting for transfers between devices  13.3 us (8%)
  starting transfers between devices  12.8 us (8%)
  other arithmetic  10.6 us (7%)
    pallas_call x5, Pallas kernels, compare_rows(): pl.pallas_call(compare_kernel, grid=(steps,), in_specs=[pl.BlockSpec((blo...  48.5 us
    all_gather x1, blocking collectives, body(): panel_rows = lax.all_gather(own_seeds, 'z', axis=0, tiled=True)  36.3 us
    unnamed x37, local copies, waits for them, and re-layouts  22.3 us
    ppermute x4, waiting for transfers between devices, body(): other = lax.ppermute(held, BLK_AXES, route)  13.3 us
    ppermute x4, starting transfers between devices, body(): other = lax.ppermute(held, BLK_AXES, route)  12.8 us
    all_gather x1, blocking collectives, body(): panel_rows = lax.all_gather(panel_rows, 'x_lo', axis=0, tiled=True)  6.02 us
  transfers between devices with their start and end apart: 4, of which 2 were waited for; matrix products, arithmetic and copies ran while one was open for 16% of the time, Pallas kernels for 15%

profile of v5, /device:TPU:24, one launch (start us, length us, event | category | flops | bytes accessed | tf_op | source)
XLA Modules:
  0.0 158.3 jit_solution(6313745962610697502)
XLA Ops:
  0.6 4.9 %collective-permute-start = (bf16[1,176,640]{2,1,0:T(8,128)(2,1)}, bf16[1,176,640]{2,1,0:T(8,128)(2,1)S(1)}, u32[]{:S(2)}, u32[]{:S(2)}) collective-permute-start(bf16[1,176,640]{2,1,0:T(8,128)(2,1)} %bitcast.191), channel_id=1, source_target_pairs={{0,256},{32,288},{64,320},{96,352},{128,384},{160,416},{192,448},{... | collective-permute-start | bytes 675848 | tf_op jit(solution)/shard_map/ppermute | solution.py:209
  5.6 1.4 convert_reduce_fusion
  8.9 1.5 gather_fusion
  10.5 36.3 %all_gather.6 = bf16[128,640]{1,0:T(8,128)(2,1)S(1)} all-gather(bf16[8,640]{1,0:T(8,128)(2,1)S(1)} %broadcast_select_fusion), channel_id=1, replica_groups=mesh['x_hi'=2,'y'=4,'core'=2,'x_lo'=2,'z'=16] {'z'}, dimensions={0}, use_global_device_ids=true | all-gather | bytes 174080 | tf_op jit(solution)/shard_map/all_gather | solution.py:182
  46.9 6.0 %all_gather.7 = bf16[256,640]{0,1:T(8,128)(2,1)S(1)} all-gather(bf16[128,640]{0,1:T(8,128)(2,1)S(1)} %copy.29), channel_id=1, replica_groups=mesh['x_hi'=2,'y'=4,'core'=2,'x_lo'=2,'z'=16] {'x_lo'}, dimensions={0}, use_global_device_ids=true | all-gather | bytes 491520 | tf_op jit(solution)/shard_map/all_gather | solution.py:183
  69.7 1.4 fusion.8
  71.9 1.4 stack.275.mw_ref
  73.4 1.5 copy-done.1
  74.9 1.7 %copy-done.2 = bf16[20,256,256]{2,1,0:T(8,128)(2,1)S(1)} copy-done((bf16[20,256,256]{2,1,0:T(8,128)(2,1)S(1)}, bf16[20,256,256]{2,1,0:T(8,128)(2,1)}, u32[]{:S(2)}) %copy-start.2) | copy-done | bytes 2621464
  76.6 3.0 %shard_map.230 = (bf16[176,256]{1,0:T(8,128)(2,1)S(1)}, bf16[176,256]{1,0:T(8,128)(2,1)S(1)}) custom-call(bf16[176,640]{1,0:T(8,128)(2,1)S(1)} %copy-done, f32[1,640]{1,0:T(1,128)S(1)} %broadcast_in_dim.14.m_ref, f32[20,256]{1,0:T(8,128)S(1)} %stack.275.mw_ref, bf16[20,256,256]{2,1,0:T(8,128)(2,1)S(1)} %copy-done.2, bf16[640,256]{1,0:T(8,128)(2,1)S(1)} %fusion.4.sh_ref), custom_call_target="tpu_custom_call" | custom-call | flops 519045120 | bytes 3026944 | tf_op jit(solution)/shard_map/pallas_call | solution.py:124
  79.7 3.1 %collective-permute-start.1 = (bf16[2,176,640]{2,1,0:T(8,128)(2,1)S(1)}, bf16[2,176,640]{2,1,0:T(8,128)(2,1)S(1)}, u32[]{:S(2)}, u32[]{:S(2)}) collective-permute-start(bf16[2,176,640]{2,1,0:T(8,128)(2,1)S(1)} %maximum_select_fusion.6), channel_id=1, source_target_pairs={{0,128},{32,160},{64,192},{96,224},{128,0},{160,32},{192,64},{224,... | collective-permute-start | bytes 1351688 | tf_op jit(solution)/shard_map/ppermute | solution.py:209
  82.9 1.7 %copy-done.3 = bf16[20,256,256]{2,1,0:T(8,128)(2,1)S(1)} copy-done((bf16[20,256,256]{2,1,0:T(8,128)(2,1)S(1)}, bf16[20,256,256]{2,1,0:T(8,128)(2,1)}, u32[]{:S(2)}) %copy-start.3) | copy-done | bytes 2621464
  84.6 3.0 %shard_map.231 = (bf16[176,256]{1,0:T(8,128)(2,1)S(1)}, bf16[176,256]{1,0:T(8,128)(2,1)S(1)}) custom-call(bf16[176,640]{1,0:T(8,128)(2,1)S(1)} %bitcast.195, f32[1,640]{1,0:T(1,128)S(1)} %broadcast_in_dim.14.m_ref, f32[20,256]{1,0:T(8,128)S(1)} %stack.275.mw_ref, bf16[20,256,256]{2,1,0:T(8,128)(2,1)S(1)} %copy-done.3, bf16[640,256]{1,0:T(8,128)(2,1)S(1)} %fusion.4.sh_ref), custom_call_target="tpu_custom_call" | custom-call | flops 519045120 | bytes 3026944 | tf_op jit(solution)/shard_map/pallas_call | solution.py:124
  87.6 8.7 %collective-permute-done.1 = bf16[2,176,640]{2,1,0:T(8,128)(2,1)S(1)} collective-permute-done((bf16[2,176,640]{2,1,0:T(8,128)(2,1)S(1)}, bf16[2,176,640]{2,1,0:T(8,128)(2,1)S(1)}, u32[]{:S(2)}, u32[]{:S(2)}) %collective-permute-start.1) | collective-permute-done | bytes 450592 | tf_op jit(solution)/shard_map/ppermute | solution.py:209
  96.5 2.8 %collective-permute-start.2 = (bf16[4,176,640]{2,1,0:T(8,128)(2,1)S(1)}, bf16[4,176,640]{2,1,0:T(8,128)(2,1)S(1)}, u32[]{:S(2)}, u32[]{:S(2)}) collective-permute-start(bf16[4,176,640]{2,1,0:T(8,128)(2,1)S(1)} %bitcast.202), channel_id=1, source_target_pairs={{0,64},{32,96},{64,0},{96,32},{128,192},{160,224},{192,128},{224,1... | collective-permute-start | bytes 2703368 | tf_op jit(solution)/shard_map/ppermute | solution.py:209
  99.4 1.7 %copy-done.4 = bf16[20,256,256]{2,1,0:T(8,128)(2,1)S(1)} copy-done((bf16[20,256,256]{2,1,0:T(8,128)(2,1)S(1)}, bf16[20,256,256]{2,1,0:T(8,128)(2,1)}, u32[]{:S(2)}) %copy-start.4) | copy-done | bytes 2621464
  101.1 6.0 %shard_map.232 = (bf16[352,256]{1,0:T(8,128)(2,1)S(1)}, bf16[352,256]{1,0:T(8,128)(2,1)S(1)}) custom-call(bf16[352,640]{1,0:T(8,128)(2,1)S(1)} %bitcast.190, f32[1,640]{1,0:T(1,128)S(1)} %broadcast_in_dim.14.m_ref, f32[20,256]{1,0:T(8,128)S(1)} %stack.275.mw_ref, bf16[20,256,256]{2,1,0:T(8,128)(2,1)S(1)} %copy-done.4, bf16[640,256]{1,0:T(8,128)(2,1)S(1)} %fusion.4.sh_ref), custom_call_target="tpu_custom_call" | custom-call | flops 1038090240 | bytes 3432448 | tf_op jit(solution)/shard_map/pallas_call | solution.py:124
  107.1 4.5 %collective-permute-done.2 = bf16[4,176,640]{2,1,0:T(8,128)(2,1)S(1)} collective-permute-done((bf16[4,176,640]{2,1,0:T(8,128)(2,1)S(1)}, bf16[4,176,640]{2,1,0:T(8,128)(2,1)S(1)}, u32[]{:S(2)}, u32[]{:S(2)}) %collective-permute-start.2) | collective-permute-done | bytes 901152 | tf_op jit(solution)/shard_map/ppermute | solution.py:209
  111.6 1.6 %maximum_select_fusion = bf16[2,4,176,640]{3,2,1,0:T(8,128)(2,1)} fusion(bf16[1,4,176,640]{3,2,1,0:T(8,128)(2,1)S(1)} %bitcast.185, bf16[1,4,176,640]{3,2,1,0:T(8,128)(2,1)S(1)} %bitcast.203, pred[]{:T(512)S(6)} %eq.11), kind=kLoop, calls=%fused_computation.1 | loop fusion | flops 2703360 | bytes 3604481 | tf_op jit(solution)/shard_map/jit(_where)/select_n | solution.py:161
  113.2 1.9 %collective-permute-start.3 = (bf16[8,176,640]{2,1,0:T(8,128)(2,1)}, bf16[8,176,640]{2,1,0:T(8,128)(2,1)}, u32[]{:S(2)}, u32[]{:S(2)}) collective-permute-start(bf16[8,176,640]{2,1,0:T(8,128)(2,1)} %bitcast.95), channel_id=1, source_target_pairs={{0,32},{32,0},{64,96},{96,64},{128,160},{160,128},{192,224},{224,1... | collective-permute-start | bytes 5406728 | tf_op jit(solution)/shard_map/ppermute | solution.py:209
  115.3 1.7 %copy-done.5 = bf16[20,256,256]{2,1,0:T(8,128)(2,1)S(1)} copy-done((bf16[20,256,256]{2,1,0:T(8,128)(2,1)S(1)}, bf16[20,256,256]{2,1,0:T(8,128)(2,1)}, u32[]{:S(2)}) %copy-start.5) | copy-done | bytes 2621464
  117.0 11.9 %shard_map.233 = (bf16[704,256]{1,0:T(8,128)(2,1)S(1)}, bf16[704,256]{1,0:T(8,128)(2,1)S(1)}) custom-call(bf16[704,640]{1,0:T(8,128)(2,1)S(1)} %bitcast.186, f32[1,640]{1,0:T(1,128)S(1)} %broadcast_in_dim.14.m_ref, f32[20,256]{1,0:T(8,128)S(1)} %stack.275.mw_ref, bf16[20,256,256]{2,1,0:T(8,128)(2,1)S(1)} %copy-done.5, bf16[640,256]{1,0:T(8,128)(2,1)S(1)} %fusion.4.sh_ref), custom_call_target="tpu_custom_call" | custom-call | flops 2076180480 | bytes 4243456 | tf_op jit(solution)/shard_map/pallas_call | solution.py:124
  129.3 1.5 copy-done.6
  130.7 24.7 %shard_map.234 = (bf16[1408,256]{1,0:T(8,128)(2,1)S(1)}, bf16[1408,256]{1,0:T(8,128)(2,1)S(1)}) custom-call(bf16[1408,640]{1,0:T(8,128)(2,1)} %bitcast.103.x_ref, f32[1,640]{1,0:T(1,128)S(1)} %broadcast_in_dim.14.m_ref, f32[20,256]{1,0:T(8,128)S(1)} %stack.275.mw_ref, bf16[20,256,256]{2,1,0:T(8,128)(2,1)S(1)} %copy-done.6, bf16[640,256]{1,0:T(8,128)(2,1)S(1)} %fusion.4.sh_ref), custom_call_target="tpu_custom_call" | custom-call | flops 4152360960 | bytes 5865472 | tf_op jit(solution)/shard_map/pallas_call | solution.py:124
  (75 shorter events, 23.1 us)
Async XLA Ops:
  0.6 79.0 %collective-permute-start = (bf16[1,176,640]{2,1,0:T(8,128)(2,1)}, bf16[1,176,640]{2,1,0:T(8,128)(2,1)S(1)}, u32[]{:S(2)}, u32[]{:S(2)}) collective-permute-start(bf16[1,176,640]{2,1,0:T(8,128)(2,1)} %bitcast.191), channel_id=1, source_target_pairs={{0,256},{32,288},{64,320},{96,352},{128,384},{160,416},{192,448},{... | collective-permute-start | bytes 675848 | tf_op jit(solution)/shard_map/ppermute | solution.py:209
  54.3 3.7 %copy-start.7 = (f32[256]{0:T(256)S(1)}, f32[256]{0:T(256)}, u32[]{:S(2)}) copy-start(f32[256]{0:T(256)} %constant.104.clone) | copy-start | bytes 3076
  54.4 3.6 %copy-start.8 = (f32[256]{0:T(256)S(1)}, f32[256]{0:T(256)}, u32[]{:S(2)}) copy-start(f32[256]{0:T(256)} %constant.99.clone) | copy-start | bytes 3076
  55.5 19.4 %copy-start = (bf16[176,640]{1,0:T(8,128)(2,1)S(1)}, bf16[176,640]{1,0:T(8,128)(2,1)}, u32[]{:S(2)}) copy-start(bf16[176,640]{1,0:T(8,128)(2,1)} %x_ref.1) | copy-start | bytes 675844
  73.4 1.5 copy-start.1
  74.9 1.7 %copy-start.2 = (bf16[20,256,256]{2,1,0:T(8,128)(2,1)S(1)}, bf16[20,256,256]{2,1,0:T(8,128)(2,1)}, u32[]{:S(2)}) copy-start(bf16[20,256,256]{2,1,0:T(8,128)(2,1)} %copy-done.1) | copy-start | bytes 7864324
  79.7 16.6 %collective-permute-start.1 = (bf16[2,176,640]{2,1,0:T(8,128)(2,1)S(1)}, bf16[2,176,640]{2,1,0:T(8,128)(2,1)S(1)}, u32[]{:S(2)}, u32[]{:S(2)}) collective-permute-start(bf16[2,176,640]{2,1,0:T(8,128)(2,1)S(1)} %maximum_select_fusion.6), channel_id=1, source_target_pairs={{0,128},{32,160},{64,192},{96,224},{128,0},{160,32},{192,64},{224,... | collective-permute-start | bytes 1351688 | tf_op jit(solution)/shard_map/ppermute | solution.py:209
  82.9 1.7 %copy-start.3 = (bf16[20,256,256]{2,1,0:T(8,128)(2,1)S(1)}, bf16[20,256,256]{2,1,0:T(8,128)(2,1)}, u32[]{:S(2)}) copy-start(bf16[20,256,256]{2,1,0:T(8,128)(2,1)} %copy-done.1) | copy-start | bytes 7864324
  96.5 15.1 %collective-permute-start.2 = (bf16[4,176,640]{2,1,0:T(8,128)(2,1)S(1)}, bf16[4,176,640]{2,1,0:T(8,128)(2,1)S(1)}, u32[]{:S(2)}, u32[]{:S(2)}) collective-permute-start(bf16[4,176,640]{2,1,0:T(8,128)(2,1)S(1)} %bitcast.202), channel_id=1, source_target_pairs={{0,64},{32,96},{64,0},{96,32},{128,192},{160,224},{192,128},{224,1... | collective-permute-start | bytes 2703368 | tf_op jit(solution)/shard_map/ppermute | solution.py:209
  99.3 1.7 %copy-start.4 = (bf16[20,256,256]{2,1,0:T(8,128)(2,1)S(1)}, bf16[20,256,256]{2,1,0:T(8,128)(2,1)}, u32[]{:S(2)}) copy-start(bf16[20,256,256]{2,1,0:T(8,128)(2,1)} %copy-done.1) | copy-start | bytes 7864324
  113.2 16.0 %collective-permute-start.3 = (bf16[8,176,640]{2,1,0:T(8,128)(2,1)}, bf16[8,176,640]{2,1,0:T(8,128)(2,1)}, u32[]{:S(2)}, u32[]{:S(2)}) collective-permute-start(bf16[8,176,640]{2,1,0:T(8,128)(2,1)} %bitcast.95), channel_id=1, source_target_pairs={{0,32},{32,0},{64,96},{96,64},{128,160},{160,128},{192,224},{224,1... | collective-permute-start | bytes 5406728 | tf_op jit(solution)/shard_map/ppermute | solution.py:209
  115.3 1.7 %copy-start.5 = (bf16[20,256,256]{2,1,0:T(8,128)(2,1)S(1)}, bf16[20,256,256]{2,1,0:T(8,128)(2,1)}, u32[]{:S(2)}) copy-start(bf16[20,256,256]{2,1,0:T(8,128)(2,1)} %copy-done.1) | copy-start | bytes 7864324
  129.0 1.7 %copy-start.6 = (bf16[20,256,256]{2,1,0:T(8,128)(2,1)S(1)}, bf16[20,256,256]{2,1,0:T(8,128)(2,1)}, u32[]{:S(2)}) copy-start(bf16[20,256,256]{2,1,0:T(8,128)(2,1)} %copy-done.1) | copy-start | bytes 7864324

commit v6 on v5

--- a/solution.py
+++ b/solution.py
@@ -12,6 +12,7 @@
 LANES = 128
 SPAN = 256
 ROW_TILE = 16
+NT = (((1,), (1,)), ((), ()))
 
 
 EPSILON = 1e-05
@@ -88,7 +89,7 @@
     centred = (x - mean_all) * m
     spread = jnp.sum(centred * centred, axis=1, keepdims=True)
     whole = (centred * lax.rsqrt(spread + EPSILON)).astype(jnp.bfloat16)
-    q = jnp.dot(whole, sh_ref[...], preferred_element_type=jnp.float32)
+    q = lax.dot_general(whole, sh_ref[...], NT, preferred_element_type=jnp.float32)
     stat_ref[...] = (jnp.sqrt(total_valid - 3.0) * fisher_of(q)).astype(stat_ref.dtype)
     first = None
     second = None
@@ -100,7 +101,7 @@
         cw = (xw - centre) * mw
         sp = jnp.sum(cw * cw, axis=1, keepdims=True)
         w = (cw * lax.rsqrt(sp + EPSILON)).astype(jnp.bfloat16)
-        r = jnp.dot(w, sw_ref[n, :width, :], preferred_element_type=jnp.float32)
+        r = lax.dot_general(w, sw_ref[n, :, :width], NT, preferred_element_type=jnp.float32)
         z = fisher_ratio(r)
         if first is None:
             first, second = z, z * z
@@ -111,9 +112,44 @@
     disp_ref[...] = ((WIN - 3) * (second - first * first)).astype(disp_ref.dtype)
 
 
+def seed_kernel(x_ref, m_ref, mw_ref, sw_ref, sh_ref):
+    frames = x_ref.shape[1]
+    x = x_ref[...].astype(jnp.float32)
+    m = m_ref[...]
+    total_valid = jnp.sum(m)
+    mean_all = jnp.sum(x * m, axis=1, keepdims=True) / total_valid
+    centred = (x - mean_all) * m
+    spread = jnp.sum(centred * centred, axis=1, keepdims=True)
+    sh_ref[...] = (centred * lax.rsqrt(spread + EPSILON)).astype(sh_ref.dtype)
+    for n, (start, width) in enumerate(window_frames(frames)):
+        xw = x[:, start:start + width]
+        mw = mw_ref[n:n + 1, :width]
+        count = jnp.sum(mw)
+        centre = jnp.sum(xw * mw, axis=1, keepdims=True) / count
+        cw = (xw - centre) * mw
+        sp = jnp.sum(cw * cw, axis=1, keepdims=True)
+        sw_ref[n, :, :width] = (cw * lax.rsqrt(sp + EPSILON)).astype(sw_ref.dtype)
+        if width < SPAN:
+            sw_ref[n, :, width:] = jnp.zeros((x.shape[0], SPAN - width), sw_ref.dtype)
+
+
+def seed_rows(rows, m, mw):
+    seeds, frames = rows.shape
+    vmem = pl.BlockSpec(memory_space=pltpu.VMEM)
+    return pl.pallas_call(
+        seed_kernel,
+        in_specs=[vmem, vmem, vmem],
+        out_specs=[vmem, vmem],
+        out_shape=[
+            jax.ShapeDtypeStruct((NWIN, seeds, SPAN), jnp.bfloat16),
+            jax.ShapeDtypeStruct((seeds, frames), jnp.bfloat16),
+        ],
+    )(rows, m, mw)
+
+
 def compare_rows(rows, m, mw, sw, sh, block):
     count, frames = rows.shape
-    seeds = sh.shape[1]
+    seeds = sh.shape[0]
     steps = count // block
     cost = pl.CostEstimate(
         flops=2 * count * seeds * (frames + NWIN * SPAN),
@@ -128,8 +164,8 @@
             pl.BlockSpec((block, frames), lambda i: (i, 0)),
             pl.BlockSpec((1, frames), lambda i: (0, 0)),
             pl.BlockSpec((NWIN, SPAN), lambda i: (0, 0)),
-            pl.BlockSpec((NWIN, SPAN, seeds), lambda i: (0, 0, 0)),
-            pl.BlockSpec((frames, seeds), lambda i: (0, 0)),
+            pl.BlockSpec((NWIN, seeds, SPAN), lambda i: (0, 0, 0)),
+            pl.BlockSpec((seeds, frames), lambda i: (0, 0)),
         ],
         out_specs=[
             pl.BlockSpec((block, seeds), lambda i: (i, 0)),
@@ -181,10 +217,9 @@
     weight = scrub_mask.astype(jnp.float32)
     panel_rows = lax.all_gather(own_seeds, "z", axis=0, tiled=True)
     panel_rows = lax.all_gather(panel_rows, "x_lo", axis=0, tiled=True)
-    seed_window, seed_whole = prepare(panel_rows, scrub_mask)
-    sw, sh = seed_operands(seed_window, seed_whole, frames)
     mw = window_masks(weight, frames)
     m = weight[None, :]
+    sw, sh = seed_rows(panel_rows, m, mw)
     seeds = panel_rows.shape[0]
     size = 1
     for a in BLK_AXES:

time: 161 us -> 148 us (0.919)
  local copies, waits for them, and re-layouts: 29.8 us -> 16.6 us
  Pallas kernels: 48.5 us -> 53.7 us
  other arithmetic: 10.6 us -> 6.5 us
    unnamed x37 -> x22, local copies, waits for them, and re-layouts: 22.3 us -> 10.3 us
    pallas_call x0 -> x1, Pallas kernels: none -> 5.91 us  [seed_rows(): pl.pallas_call(seed_kernel, in_specs=[vmem, vmem, vmem], out_specs=[vmem,...]
    reduce_sum x8 -> x0, other arithmetic: 2.77 us -> none  [the longest x1 1.36 us: prepare(): total_valid = jnp.sum(weight)]
  transfers between devices with their start and end apart: 4 -> 4, of which waited for: 2 -> 2; matrix products, arithmetic and copies ran while one was open for 16% -> 6% of each run, Pallas kernels for 15% -> 20%
where the time goes in v6:
time: 148 us; the launch traced here: 146 us
  Pallas kernels  53.7 us (36%)
  blocking collectives  42.3 us (29%)
  local copies, waits for them, and re-layouts  16.6 us (11%)
  waiting for transfers between devices  13.4 us (9%)
  starting transfers between devices  12.8 us (9%)
  other arithmetic  6.5 us (4%)
    pallas_call x5, Pallas kernels, compare_rows(): pl.pallas_call(compare_kernel, grid=(steps,), in_specs=[pl.BlockSpec((blo...  47.8 us
    all_gather x1, blocking collectives, body(): panel_rows = lax.all_gather(own_seeds, 'z', axis=0, tiled=True)  36.3 us
    ppermute x4, waiting for transfers between devices, body(): other = lax.ppermute(held, BLK_AXES, route)  13.4 us
    ppermute x4, starting transfers between devices, body(): other = lax.ppermute(held, BLK_AXES, route)  12.8 us
    unnamed x22, local copies, waits for them, and re-layouts  10.3 us
    all_gather x1, blocking collectives, body(): panel_rows = lax.all_gather(panel_rows, 'x_lo', axis=0, tiled=True)  6.08 us
    pallas_call x1, Pallas kernels, seed_rows(): pl.pallas_call(seed_kernel, in_specs=[vmem, vmem, vmem], out_specs=[vmem,...  5.91 us
  transfers between devices with their start and end apart: 4, of which 2 were waited for; matrix products, arithmetic and copies ran while one was open for 6% of the time, Pallas kernels for 20%

profile of v6, /device:TPU:24, one launch (start us, length us, event | category | flops | bytes accessed | tf_op | source)
XLA Modules:
  0.0 146.2 jit_solution(4915353190037568546)
XLA Ops:
  0.6 4.9 %collective-permute-start = (bf16[1,176,640]{2,1,0:T(8,128)(2,1)}, bf16[1,176,640]{2,1,0:T(8,128)(2,1)S(1)}, u32[]{:S(2)}, u32[]{:S(2)}) collective-permute-start(bf16[1,176,640]{2,1,0:T(8,128)(2,1)} %bitcast.67), channel_id=1, source_target_pairs={{0,256},{32,288},{64,320},{96,352},{128,384},{160,416},{192,448},{... | collective-permute-start | bytes 675848 | tf_op jit(solution)/shard_map/ppermute | solution.py:244
  6.9 1.5 %gather_fusion = bf16[8,640]{1,0:T(8,128)(2,1)S(1)} fusion(bf16[176,640]{1,0:T(8,128)(2,1)} %x_ref.1, s32[1024]{0:T(1024)S(1)} %pad_clamp_fusion), kind=kCustom, calls=%fused_computation | custom fusion | bytes 20512 | tf_op jit(solution)/shard_map/jit(_take)/gather | solution.py:216
  11.5 1.8 %stack.212.mw_ref = f32[20,256]{1,0:T(8,128)} concatenate(f32[1,256]{1,0:T(1,128)S(1)} %bitcast.102, f32[1,256]{1,0:T(1,128)S(1)} %bitcast.93, f32[1,256]{1,0:T(1,128)S(1)} %bitcast.94, f32[1,256]{1,0:T(1,128)S(1)} %bitcast.95, f32[1,256]{1,0:T(1,128)S(1)} %bitcast.96, f32[1,256]{1,0:T(1,128)S(1)} %bitcast.101, f32[1,256]{1,0:T(1,128)S(1)} %bitcast.84, f32[1,256]{1,0:T(1,128)S(1)} %bitcast.85, ...), dimensions={0} | concatenate | bytes 40960 | tf_op jit(solution)/shard_map/stack | solution.py:75
  13.3 36.3 %all_gather.6 = bf16[128,640]{1,0:T(8,128)(2,1)S(1)} all-gather(bf16[8,640]{1,0:T(8,128)(2,1)S(1)} %broadcast_select_fusion), channel_id=1, replica_groups=mesh['x_hi'=2,'y'=4,'core'=2,'x_lo'=2,'z'=16] {'z'}, dimensions={0}, use_global_device_ids=true | all-gather | bytes 174080 | tf_op jit(solution)/shard_map/all_gather | solution.py:218
  49.6 6.1 %all_gather.7.x_ref = bf16[256,640]{1,0:T(8,128)(2,1)} all-gather(bf16[128,640]{1,0:T(8,128)(2,1)S(1)} %all_gather.6), channel_id=1, replica_groups=mesh['x_hi'=2,'y'=4,'core'=2,'x_lo'=2,'z'=16] {'x_lo'}, dimensions={0}, use_global_device_ids=true | all-gather | bytes 491520 | tf_op jit(solution)/shard_map/all_gather | solution.py:219
  55.7 5.9 %shard_map.230 = (bf16[20,256,256]{2,1,0:T(8,128)(2,1)}, bf16[256,640]{1,0:T(8,128)(2,1)}) custom-call(bf16[256,640]{1,0:T(8,128)(2,1)} %all_gather.7.x_ref, f32[1,640]{1,0:T(1,128)} %broadcast_in_dim.16.m_ref, f32[20,256]{1,0:T(8,128)} %stack.212.mw_ref), custom_call_target="tpu_custom_call" | custom-call | tf_op jit(solution)/shard_map/pallas_call | solution.py:139
  63.9 1.7 %copy-done.5 = bf16[20,256,256]{2,1,0:T(8,128)(2,1)S(1)} copy-done((bf16[20,256,256]{2,1,0:T(8,128)(2,1)S(1)}, bf16[20,256,256]{2,1,0:T(8,128)(2,1)}, u32[]{:S(2)}) %copy-start.5) | copy-done | bytes 2621464
  65.6 1.0 copy-done.9
  66.6 2.9 %shard_map.231 = (bf16[176,256]{1,0:T(8,128)(2,1)S(1)}, bf16[176,256]{1,0:T(8,128)(2,1)S(1)}) custom-call(bf16[176,640]{1,0:T(8,128)(2,1)S(1)} %copy-done, f32[1,640]{1,0:T(1,128)S(1)} %copy-done.3, f32[20,256]{1,0:T(8,128)S(1)} %copy-done.1, bf16[20,256,256]{2,1,0:T(8,128)(2,1)S(1)} %copy-done.5, bf16[256,640]{1,0:T(8,128)(2,1)S(1)} %copy-done.9), custom_call_target="tpu_custom_call" | custom-call | flops 519045120 | bytes 3026944 | tf_op jit(solution)/shard_map/pallas_call | solution.py:160
  69.7 3.1 %collective-permute-start.1 = (bf16[2,176,640]{2,1,0:T(8,128)(2,1)S(1)}, bf16[2,176,640]{2,1,0:T(8,128)(2,1)S(1)}, u32[]{:S(2)}, u32[]{:S(2)}) collective-permute-start(bf16[2,176,640]{2,1,0:T(8,128)(2,1)S(1)} %maximum_select_fusion.6), channel_id=1, source_target_pairs={{0,128},{32,160},{64,192},{96,224},{128,0},{160,32},{192,64},{224,... | collective-permute-start | bytes 1351688 | tf_op jit(solution)/shard_map/ppermute | solution.py:244
  72.9 1.7 %copy-done.6 = bf16[20,256,256]{2,1,0:T(8,128)(2,1)S(1)} copy-done((bf16[20,256,256]{2,1,0:T(8,128)(2,1)S(1)}, bf16[20,256,256]{2,1,0:T(8,128)(2,1)}, u32[]{:S(2)}) %copy-start.6) | copy-done | bytes 2621464
  74.6 2.9 %shard_map.232 = (bf16[176,256]{1,0:T(8,128)(2,1)S(1)}, bf16[176,256]{1,0:T(8,128)(2,1)S(1)}) custom-call(bf16[176,640]{1,0:T(8,128)(2,1)S(1)} %bitcast.71, f32[1,640]{1,0:T(1,128)S(1)} %copy-done.4, f32[20,256]{1,0:T(8,128)S(1)} %copy-done.2, bf16[20,256,256]{2,1,0:T(8,128)(2,1)S(1)} %copy-done.6, bf16[256,640]{1,0:T(8,128)(2,1)S(1)} %copy-done.10), custom_call_target="tpu_custom_call" | custom-call | flops 519045120 | bytes 3026944 | tf_op jit(solution)/shard_map/pallas_call | solution.py:160
  77.5 8.8 %collective-permute-done.1 = bf16[2,176,640]{2,1,0:T(8,128)(2,1)S(1)} collective-permute-done((bf16[2,176,640]{2,1,0:T(8,128)(2,1)S(1)}, bf16[2,176,640]{2,1,0:T(8,128)(2,1)S(1)}, u32[]{:S(2)}, u32[]{:S(2)}) %collective-permute-start.1) | collective-permute-done | bytes 450592 | tf_op jit(solution)/shard_map/ppermute | solution.py:244
  86.5 2.8 %collective-permute-start.2 = (bf16[4,176,640]{2,1,0:T(8,128)(2,1)S(1)}, bf16[4,176,640]{2,1,0:T(8,128)(2,1)S(1)}, u32[]{:S(2)}, u32[]{:S(2)}) collective-permute-start(bf16[4,176,640]{2,1,0:T(8,128)(2,1)S(1)} %bitcast.78), channel_id=1, source_target_pairs={{0,64},{32,96},{64,0},{96,32},{128,192},{160,224},{192,128},{224,1... | collective-permute-start | bytes 2703368 | tf_op jit(solution)/shard_map/ppermute | solution.py:244
  89.3 1.7 %copy-done.7 = bf16[20,256,256]{2,1,0:T(8,128)(2,1)S(1)} copy-done((bf16[20,256,256]{2,1,0:T(8,128)(2,1)S(1)}, bf16[20,256,256]{2,1,0:T(8,128)(2,1)}, u32[]{:S(2)}) %copy-start.7) | copy-done | bytes 2621464
  91.1 5.9 %shard_map.233 = (bf16[352,256]{1,0:T(8,128)(2,1)S(1)}, bf16[352,256]{1,0:T(8,128)(2,1)S(1)}) custom-call(bf16[352,640]{1,0:T(8,128)(2,1)S(1)} %bitcast.66, f32[1,640]{1,0:T(1,128)S(1)} %copy-done.4, f32[20,256]{1,0:T(8,128)S(1)} %copy-done.2, bf16[20,256,256]{2,1,0:T(8,128)(2,1)S(1)} %copy-done.7, bf16[256,640]{1,0:T(8,128)(2,1)S(1)} %copy-done.10), custom_call_target="tpu_custom_call" | custom-call | flops 1038090240 | bytes 3432448 | tf_op jit(solution)/shard_map/pallas_call | solution.py:160
  96.9 4.7 %collective-permute-done.2 = bf16[4,176,640]{2,1,0:T(8,128)(2,1)S(1)} collective-permute-done((bf16[4,176,640]{2,1,0:T(8,128)(2,1)S(1)}, bf16[4,176,640]{2,1,0:T(8,128)(2,1)S(1)}, u32[]{:S(2)}, u32[]{:S(2)}) %collective-permute-start.2) | collective-permute-done | bytes 901152 | tf_op jit(solution)/shard_map/ppermute | solution.py:244
  101.6 1.6 %maximum_select_fusion = bf16[2,4,176,640]{3,2,1,0:T(8,128)(2,1)} fusion(bf16[1,4,176,640]{3,2,1,0:T(8,128)(2,1)S(1)} %bitcast.61, bf16[1,4,176,640]{3,2,1,0:T(8,128)(2,1)S(1)} %bitcast.79, pred[]{:T(512)S(6)} %eq.11), kind=kLoop, calls=%fused_computation.1 | loop fusion | flops 2703360 | bytes 3604481 | tf_op jit(solution)/shard_map/jit(_where)/select_n | solution.py:197
  103.2 1.9 %collective-permute-start.3 = (bf16[8,176,640]{2,1,0:T(8,128)(2,1)}, bf16[8,176,640]{2,1,0:T(8,128)(2,1)}, u32[]{:S(2)}, u32[]{:S(2)}) collective-permute-start(bf16[8,176,640]{2,1,0:T(8,128)(2,1)} %bitcast.34), channel_id=1, source_target_pairs={{0,32},{32,0},{64,96},{96,64},{128,160},{160,128},{192,224},{224,1... | collective-permute-start | bytes 5406728 | tf_op jit(solution)/shard_map/ppermute | solution.py:244
  105.3 1.7 %copy-done.8 = bf16[20,256,256]{2,1,0:T(8,128)(2,1)S(1)} copy-done((bf16[20,256,256]{2,1,0:T(8,128)(2,1)S(1)}, bf16[20,256,256]{2,1,0:T(8,128)(2,1)}, u32[]{:S(2)}) %copy-start.8) | copy-done | bytes 2621464
  107.0 11.7 %shard_map.234 = (bf16[704,256]{1,0:T(8,128)(2,1)S(1)}, bf16[704,256]{1,0:T(8,128)(2,1)S(1)}) custom-call(bf16[704,640]{1,0:T(8,128)(2,1)S(1)} %bitcast.62, f32[1,640]{1,0:T(1,128)S(1)} %copy-done.4, f32[20,256]{1,0:T(8,128)S(1)} %copy-done.2, bf16[20,256,256]{2,1,0:T(8,128)(2,1)S(1)} %copy-done.8, bf16[256,640]{1,0:T(8,128)(2,1)S(1)} %copy-done.10), custom_call_target="tpu_custom_call" | custom-call | flops 2076180480 | bytes 4243456 | tf_op jit(solution)/shard_map/pallas_call | solution.py:160
  119.0 24.3 %shard_map.235 = (bf16[1408,256]{1,0:T(8,128)(2,1)S(1)}, bf16[1408,256]{1,0:T(8,128)(2,1)S(1)}) custom-call(bf16[1408,640]{1,0:T(8,128)(2,1)} %bitcast.42.x_ref, f32[1,640]{1,0:T(1,128)S(1)} %copy-done.4, f32[20,256]{1,0:T(8,128)S(1)} %copy-done.2, bf16[20,256,256]{2,1,0:T(8,128)(2,1)S(1)} %copy-done.8, bf16[256,640]{1,0:T(8,128)(2,1)S(1)} %copy-done.10), custom_call_target="tpu_custom_call" | custom-call | flops 4152360960 | bytes 5865472 | tf_op jit(solution)/shard_map/pallas_call | solution.py:160
  143.6 1.2 copy.25
  145.0 1.2 copy.26
  (36 shorter events, 7.8 us)
Async XLA Ops:
  0.6 68.9 %collective-permute-start = (bf16[1,176,640]{2,1,0:T(8,128)(2,1)}, bf16[1,176,640]{2,1,0:T(8,128)(2,1)S(1)}, u32[]{:S(2)}, u32[]{:S(2)}) collective-permute-start(bf16[1,176,640]{2,1,0:T(8,128)(2,1)} %bitcast.67), channel_id=1, source_target_pairs={{0,256},{32,288},{64,320},{96,352},{128,384},{160,416},{192,448},{... | collective-permute-start | bytes 675848 | tf_op jit(solution)/shard_map/ppermute | solution.py:244
  61.6 0.9 copy-start
  62.5 0.7 copy-start.1
  63.2 0.7 copy-start.3
  63.9 1.7 %copy-start.5 = (bf16[20,256,256]{2,1,0:T(8,128)(2,1)S(1)}, bf16[20,256,256]{2,1,0:T(8,128)(2,1)}, u32[]{:S(2)}) copy-start(bf16[20,256,256]{2,1,0:T(8,128)(2,1)} %get-tuple-element.23.sw_ref) | copy-start | bytes 7864324
  65.6 1.0 copy-start.9
  66.6 6.2 %copy-start.2 = (f32[20,256]{1,0:T(8,128)S(1)}, f32[20,256]{1,0:T(8,128)}, u32[]{:S(2)}) copy-start(f32[20,256]{1,0:T(8,128)} %stack.212.mw_ref) | copy-start | bytes 61444
  66.6 6.2 %copy-start.4 = (f32[1,640]{1,0:T(1,128)S(1)}, f32[1,640]{1,0:T(1,128)}, u32[]{:S(2)}) copy-start(f32[1,640]{1,0:T(1,128)} %broadcast_in_dim.16.m_ref) | copy-start | bytes 7684
  66.6 6.2 %copy-start.10 = (bf16[256,640]{1,0:T(8,128)(2,1)S(1)}, bf16[256,640]{1,0:T(8,128)(2,1)}, u32[]{:S(2)}) copy-start(bf16[256,640]{1,0:T(8,128)(2,1)} %get-tuple-element.24.sh_ref) | copy-start | bytes 983044
  69.7 16.6 %collective-permute-start.1 = (bf16[2,176,640]{2,1,0:T(8,128)(2,1)S(1)}, bf16[2,176,640]{2,1,0:T(8,128)(2,1)S(1)}, u32[]{:S(2)}, u32[]{:S(2)}) collective-permute-start(bf16[2,176,640]{2,1,0:T(8,128)(2,1)S(1)} %maximum_select_fusion.6), channel_id=1, source_target_pairs={{0,128},{32,160},{64,192},{96,224},{128,0},{160,32},{192,64},{224,... | collective-permute-start | bytes 1351688 | tf_op jit(solution)/shard_map/ppermute | solution.py:244
  72.9 1.7 %copy-start.6 = (bf16[20,256,256]{2,1,0:T(8,128)(2,1)S(1)}, bf16[20,256,256]{2,1,0:T(8,128)(2,1)}, u32[]{:S(2)}) copy-start(bf16[20,256,256]{2,1,0:T(8,128)(2,1)} %get-tuple-element.23.sw_ref) | copy-start | bytes 7864324
  86.5 15.1 %collective-permute-start.2 = (bf16[4,176,640]{2,1,0:T(8,128)(2,1)S(1)}, bf16[4,176,640]{2,1,0:T(8,128)(2,1)S(1)}, u32[]{:S(2)}, u32[]{:S(2)}) collective-permute-start(bf16[4,176,640]{2,1,0:T(8,128)(2,1)S(1)} %bitcast.78), channel_id=1, source_target_pairs={{0,64},{32,96},{64,0},{96,32},{128,192},{160,224},{192,128},{224,1... | collective-permute-start | bytes 2703368 | tf_op jit(solution)/shard_map/ppermute | solution.py:244
  89.3 1.7 %copy-start.7 = (bf16[20,256,256]{2,1,0:T(8,128)(2,1)S(1)}, bf16[20,256,256]{2,1,0:T(8,128)(2,1)}, u32[]{:S(2)}) copy-start(bf16[20,256,256]{2,1,0:T(8,128)(2,1)} %get-tuple-element.23.sw_ref) | copy-start | bytes 7864324
  103.2 15.8 %collective-permute-start.3 = (bf16[8,176,640]{2,1,0:T(8,128)(2,1)}, bf16[8,176,640]{2,1,0:T(8,128)(2,1)}, u32[]{:S(2)}, u32[]{:S(2)}) collective-permute-start(bf16[8,176,640]{2,1,0:T(8,128)(2,1)} %bitcast.34), channel_id=1, source_target_pairs={{0,32},{32,0},{64,96},{96,64},{128,160},{160,128},{192,224},{224,1... | collective-permute-start | bytes 5406728 | tf_op jit(solution)/shard_map/ppermute | solution.py:244
  105.3 1.7 %copy-start.8 = (bf16[20,256,256]{2,1,0:T(8,128)(2,1)S(1)}, bf16[20,256,256]{2,1,0:T(8,128)(2,1)}, u32[]{:S(2)}) copy-start(bf16[20,256,256]{2,1,0:T(8,128)(2,1)} %get-tuple-element.23.sw_ref) | copy-start | bytes 7864324

commit v7 on v6

--- a/solution.py
+++ b/solution.py
@@ -13,6 +13,7 @@
 SPAN = 256
 ROW_TILE = 16
 NT = (((1,), (1,)), ((), ()))
+HALF_LN2 = 0.5 * float(np.log(2.0))
 
 
 EPSILON = 1e-05
@@ -75,11 +76,6 @@
     return jnp.stack(rows)
 
 
-def fisher_ratio(values):
-    clipped = jnp.clip(values, -CLIP_LEVEL, CLIP_LEVEL)
-    return 0.5 * jnp.log((1.0 + clipped) / (1.0 - clipped))
-
-
 def compare_kernel(x_ref, m_ref, mw_ref, sw_ref, sh_ref, disp_ref, stat_ref):
     frames = x_ref.shape[1]
     x = x_ref[...].astype(jnp.float32)
@@ -102,13 +98,14 @@
         sp = jnp.sum(cw * cw, axis=1, keepdims=True)
         w = (cw * lax.rsqrt(sp + EPSILON)).astype(jnp.bfloat16)
         r = lax.dot_general(w, sw_ref[n, :, :width], NT, preferred_element_type=jnp.float32)
-        z = fisher_ratio(r)
+        clipped = jnp.clip(r, -CLIP_LEVEL, CLIP_LEVEL)
+        z2 = lax.log2(1.0 + clipped) - lax.log2(1.0 - clipped)
         if first is None:
-            first, second = z, z * z
+            first, second = z2, z2 * z2
         else:
-            first, second = first + z, second + z * z
-    first = first / NWIN
-    second = second / NWIN
+            first, second = first + z2, second + z2 * z2
+    first = first * (HALF_LN2 / NWIN)
+    second = second * (HALF_LN2 * HALF_LN2 / NWIN)
     disp_ref[...] = ((WIN - 3) * (second - first * first)).astype(disp_ref.dtype)
 
 

time: 148 us -> 145 us (0.980)
  Pallas kernels: 53.7 us -> 50.3 us
    pallas_call x5, Pallas kernels: 47.8 us -> 44.4 us  [compare_rows(): pl.pallas_call(compare_kernel, grid=(steps,), in_specs=[pl.BlockSpec((blo...]
  transfers between devices with their start and end apart: 4 -> 4, of which waited for: 2 -> 2; matrix products, arithmetic and copies ran while one was open for 6% -> 6% of each run, Pallas kernels for 20% -> 19%
where the time goes in v7:
time: 145 us; the launch traced here: 144 us
  Pallas kernels  50.3 us (35%)
  blocking collectives  42.3 us (29%)
  local copies, waits for them, and re-layouts  16.6 us (11%)
  waiting for transfers between devices  14.2 us (10%)
  starting transfers between devices  12.8 us (9%)
  other arithmetic  6.5 us (4%)
    pallas_call x5, Pallas kernels, compare_rows(): pl.pallas_call(compare_kernel, grid=(steps,), in_specs=[pl.BlockSpec((blo...  44.4 us
    all_gather x1, blocking collectives, body(): panel_rows = lax.all_gather(own_seeds, 'z', axis=0, tiled=True)  36.3 us
    ppermute x4, waiting for transfers between devices, body(): other = lax.ppermute(held, BLK_AXES, route)  14.2 us
    ppermute x4, starting transfers between devices, body(): other = lax.ppermute(held, BLK_AXES, route)  12.8 us
    unnamed x22, local copies, waits for them, and re-layouts  10.3 us
    all_gather x1, blocking collectives, body(): panel_rows = lax.all_gather(panel_rows, 'x_lo', axis=0, tiled=True)  6.08 us
    pallas_call x1, Pallas kernels, seed_rows(): pl.pallas_call(seed_kernel, in_specs=[vmem, vmem, vmem], out_specs=[vmem,...  5.91 us
  transfers between devices with their start and end apart: 4, of which 2 were waited for; matrix products, arithmetic and copies ran while one was open for 6% of the time, Pallas kernels for 19%

profile of v7, /device:TPU:24, one launch (start us, length us, event | category | flops | bytes accessed | tf_op | source)
XLA Modules:
  0.0 143.7 jit_solution(16851049286354180448)
XLA Ops:
  0.6 4.9 %collective-permute-start = (bf16[1,176,640]{2,1,0:T(8,128)(2,1)}, bf16[1,176,640]{2,1,0:T(8,128)(2,1)S(1)}, u32[]{:S(2)}, u32[]{:S(2)}) collective-permute-start(bf16[1,176,640]{2,1,0:T(8,128)(2,1)} %bitcast.67), channel_id=1, source_target_pairs={{0,256},{32,288},{64,320},{96,352},{128,384},{160,416},{192,448},{... | collective-permute-start | bytes 675848 | tf_op jit(solution)/shard_map/ppermute | solution.py:241
  6.9 1.5 %gather_fusion = bf16[8,640]{1,0:T(8,128)(2,1)S(1)} fusion(bf16[176,640]{1,0:T(8,128)(2,1)} %x_ref.1, s32[1024]{0:T(1024)S(1)} %pad_clamp_fusion), kind=kCustom, calls=%fused_computation | custom fusion | bytes 20512 | tf_op jit(solution)/shard_map/jit(_take)/gather | solution.py:213
  11.5 1.8 %stack.212.mw_ref = f32[20,256]{1,0:T(8,128)} concatenate(f32[1,256]{1,0:T(1,128)S(1)} %bitcast.102, f32[1,256]{1,0:T(1,128)S(1)} %bitcast.93, f32[1,256]{1,0:T(1,128)S(1)} %bitcast.94, f32[1,256]{1,0:T(1,128)S(1)} %bitcast.95, f32[1,256]{1,0:T(1,128)S(1)} %bitcast.96, f32[1,256]{1,0:T(1,128)S(1)} %bitcast.101, f32[1,256]{1,0:T(1,128)S(1)} %bitcast.84, f32[1,256]{1,0:T(1,128)S(1)} %bitcast.85, ...), dimensions={0} | concatenate | bytes 40960 | tf_op jit(solution)/shard_map/stack | solution.py:76
  13.3 36.3 %all_gather.6 = bf16[128,640]{1,0:T(8,128)(2,1)S(1)} all-gather(bf16[8,640]{1,0:T(8,128)(2,1)S(1)} %broadcast_select_fusion), channel_id=1, replica_groups=mesh['x_hi'=2,'y'=4,'core'=2,'x_lo'=2,'z'=16] {'z'}, dimensions={0}, use_global_device_ids=true | all-gather | bytes 174080 | tf_op jit(solution)/shard_map/all_gather | solution.py:215
  49.6 6.1 %all_gather.7.x_ref = bf16[256,640]{1,0:T(8,128)(2,1)} all-gather(bf16[128,640]{1,0:T(8,128)(2,1)S(1)} %all_gather.6), channel_id=1, replica_groups=mesh['x_hi'=2,'y'=4,'core'=2,'x_lo'=2,'z'=16] {'x_lo'}, dimensions={0}, use_global_device_ids=true | all-gather | bytes 491520 | tf_op jit(solution)/shard_map/all_gather | solution.py:216
  55.7 5.9 %shard_map.230 = (bf16[20,256,256]{2,1,0:T(8,128)(2,1)}, bf16[256,640]{1,0:T(8,128)(2,1)}) custom-call(bf16[256,640]{1,0:T(8,128)(2,1)} %all_gather.7.x_ref, f32[1,640]{1,0:T(1,128)} %broadcast_in_dim.16.m_ref, f32[20,256]{1,0:T(8,128)} %stack.212.mw_ref), custom_call_target="tpu_custom_call" | custom-call | tf_op jit(solution)/shard_map/pallas_call | solution.py:136
  63.9 1.7 %copy-done.5 = bf16[20,256,256]{2,1,0:T(8,128)(2,1)S(1)} copy-done((bf16[20,256,256]{2,1,0:T(8,128)(2,1)S(1)}, bf16[20,256,256]{2,1,0:T(8,128)(2,1)}, u32[]{:S(2)}) %copy-start.5) | copy-done | bytes 2621464
  65.6 1.0 copy-done.9
  66.6 2.7 %shard_map.231 = (bf16[176,256]{1,0:T(8,128)(2,1)S(1)}, bf16[176,256]{1,0:T(8,128)(2,1)S(1)}) custom-call(bf16[176,640]{1,0:T(8,128)(2,1)S(1)} %copy-done, f32[1,640]{1,0:T(1,128)S(1)} %copy-done.3, f32[20,256]{1,0:T(8,128)S(1)} %copy-done.1, bf16[20,256,256]{2,1,0:T(8,128)(2,1)S(1)} %copy-done.5, bf16[256,640]{1,0:T(8,128)(2,1)S(1)} %copy-done.9), custom_call_target="tpu_custom_call" | custom-call | flops 519045120 | bytes 3026944 | tf_op jit(solution)/shard_map/pallas_call | solution.py:157
  69.5 3.1 %collective-permute-start.1 = (bf16[2,176,640]{2,1,0:T(8,128)(2,1)S(1)}, bf16[2,176,640]{2,1,0:T(8,128)(2,1)S(1)}, u32[]{:S(2)}, u32[]{:S(2)}) collective-permute-start(bf16[2,176,640]{2,1,0:T(8,128)(2,1)S(1)} %maximum_select_fusion.6), channel_id=1, source_target_pairs={{0,128},{32,160},{64,192},{96,224},{128,0},{160,32},{192,64},{224,... | collective-permute-start | bytes 1351688 | tf_op jit(solution)/shard_map/ppermute | solution.py:241
  72.7 1.7 %copy-done.6 = bf16[20,256,256]{2,1,0:T(8,128)(2,1)S(1)} copy-done((bf16[20,256,256]{2,1,0:T(8,128)(2,1)S(1)}, bf16[20,256,256]{2,1,0:T(8,128)(2,1)}, u32[]{:S(2)}) %copy-start.6) | copy-done | bytes 2621464
  74.4 2.7 %shard_map.232 = (bf16[176,256]{1,0:T(8,128)(2,1)S(1)}, bf16[176,256]{1,0:T(8,128)(2,1)S(1)}) custom-call(bf16[176,640]{1,0:T(8,128)(2,1)S(1)} %bitcast.71, f32[1,640]{1,0:T(1,128)S(1)} %copy-done.4, f32[20,256]{1,0:T(8,128)S(1)} %copy-done.2, bf16[20,256,256]{2,1,0:T(8,128)(2,1)S(1)} %copy-done.6, bf16[256,640]{1,0:T(8,128)(2,1)S(1)} %copy-done.10), custom_call_target="tpu_custom_call" | custom-call | flops 519045120 | bytes 3026944 | tf_op jit(solution)/shard_map/pallas_call | solution.py:157
  77.1 9.0 %collective-permute-done.1 = bf16[2,176,640]{2,1,0:T(8,128)(2,1)S(1)} collective-permute-done((bf16[2,176,640]{2,1,0:T(8,128)(2,1)S(1)}, bf16[2,176,640]{2,1,0:T(8,128)(2,1)S(1)}, u32[]{:S(2)}, u32[]{:S(2)}) %collective-permute-start.1) | collective-permute-done | bytes 450592 | tf_op jit(solution)/shard_map/ppermute | solution.py:241
  86.3 2.7 %collective-permute-start.2 = (bf16[4,176,640]{2,1,0:T(8,128)(2,1)S(1)}, bf16[4,176,640]{2,1,0:T(8,128)(2,1)S(1)}, u32[]{:S(2)}, u32[]{:S(2)}) collective-permute-start(bf16[4,176,640]{2,1,0:T(8,128)(2,1)S(1)} %bitcast.78), channel_id=1, source_target_pairs={{0,64},{32,96},{64,0},{96,32},{128,192},{160,224},{192,128},{224,1... | collective-permute-start | bytes 2703368 | tf_op jit(solution)/shard_map/ppermute | solution.py:241
  88.9 1.7 %copy-done.7 = bf16[20,256,256]{2,1,0:T(8,128)(2,1)S(1)} copy-done((bf16[20,256,256]{2,1,0:T(8,128)(2,1)S(1)}, bf16[20,256,256]{2,1,0:T(8,128)(2,1)}, u32[]{:S(2)}) %copy-start.7) | copy-done | bytes 2621464
  90.7 5.4 %shard_map.233 = (bf16[352,256]{1,0:T(8,128)(2,1)S(1)}, bf16[352,256]{1,0:T(8,128)(2,1)S(1)}) custom-call(bf16[352,640]{1,0:T(8,128)(2,1)S(1)} %bitcast.66, f32[1,640]{1,0:T(1,128)S(1)} %copy-done.4, f32[20,256]{1,0:T(8,128)S(1)} %copy-done.2, bf16[20,256,256]{2,1,0:T(8,128)(2,1)S(1)} %copy-done.7, bf16[256,640]{1,0:T(8,128)(2,1)S(1)} %copy-done.10), custom_call_target="tpu_custom_call" | custom-call | flops 1038090240 | bytes 3432448 | tf_op jit(solution)/shard_map/pallas_call | solution.py:157
  96.1 5.3 %collective-permute-done.2 = bf16[4,176,640]{2,1,0:T(8,128)(2,1)S(1)} collective-permute-done((bf16[4,176,640]{2,1,0:T(8,128)(2,1)S(1)}, bf16[4,176,640]{2,1,0:T(8,128)(2,1)S(1)}, u32[]{:S(2)}, u32[]{:S(2)}) %collective-permute-start.2) | collective-permute-done | bytes 901152 | tf_op jit(solution)/shard_map/ppermute | solution.py:241
  101.4 1.6 %maximum_select_fusion = bf16[2,4,176,640]{3,2,1,0:T(8,128)(2,1)} fusion(bf16[1,4,176,640]{3,2,1,0:T(8,128)(2,1)S(1)} %bitcast.61, bf16[1,4,176,640]{3,2,1,0:T(8,128)(2,1)S(1)} %bitcast.79, pred[]{:T(512)S(6)} %eq.11), kind=kLoop, calls=%fused_computation.1 | loop fusion | flops 2703360 | bytes 3604481 | tf_op jit(solution)/shard_map/jit(_where)/select_n | solution.py:194
  103.0 2.1 %collective-permute-start.3 = (bf16[8,176,640]{2,1,0:T(8,128)(2,1)}, bf16[8,176,640]{2,1,0:T(8,128)(2,1)}, u32[]{:S(2)}, u32[]{:S(2)}) collective-permute-start(bf16[8,176,640]{2,1,0:T(8,128)(2,1)} %bitcast.34), channel_id=1, source_target_pairs={{0,32},{32,0},{64,96},{96,64},{128,160},{160,128},{192,224},{224,1... | collective-permute-start | bytes 5406728 | tf_op jit(solution)/shard_map/ppermute | solution.py:241
  105.2 1.7 %copy-done.8 = bf16[20,256,256]{2,1,0:T(8,128)(2,1)S(1)} copy-done((bf16[20,256,256]{2,1,0:T(8,128)(2,1)S(1)}, bf16[20,256,256]{2,1,0:T(8,128)(2,1)}, u32[]{:S(2)}) %copy-start.8) | copy-done | bytes 2621464
  107.0 10.8 %shard_map.234 = (bf16[704,256]{1,0:T(8,128)(2,1)S(1)}, bf16[704,256]{1,0:T(8,128)(2,1)S(1)}) custom-call(bf16[704,640]{1,0:T(8,128)(2,1)S(1)} %bitcast.62, f32[1,640]{1,0:T(1,128)S(1)} %copy-done.4, f32[20,256]{1,0:T(8,128)S(1)} %copy-done.2, bf16[20,256,256]{2,1,0:T(8,128)(2,1)S(1)} %copy-done.8, bf16[256,640]{1,0:T(8,128)(2,1)S(1)} %copy-done.10), custom_call_target="tpu_custom_call" | custom-call | flops 2076180480 | bytes 4243456 | tf_op jit(solution)/shard_map/pallas_call | solution.py:157
  118.1 22.7 %shard_map.235 = (bf16[1408,256]{1,0:T(8,128)(2,1)S(1)}, bf16[1408,256]{1,0:T(8,128)(2,1)S(1)}) custom-call(bf16[1408,640]{1,0:T(8,128)(2,1)} %bitcast.42.x_ref, f32[1,640]{1,0:T(1,128)S(1)} %copy-done.4, f32[20,256]{1,0:T(8,128)S(1)} %copy-done.2, bf16[20,256,256]{2,1,0:T(8,128)(2,1)S(1)} %copy-done.8, bf16[256,640]{1,0:T(8,128)(2,1)S(1)} %copy-done.10), custom_call_target="tpu_custom_call" | custom-call | flops 4152360960 | bytes 5865472 | tf_op jit(solution)/shard_map/pallas_call | solution.py:157
  141.1 1.2 copy.25
  142.5 1.2 copy.26
  (36 shorter events, 7.8 us)
Async XLA Ops:
  0.6 68.7 %collective-permute-start = (bf16[1,176,640]{2,1,0:T(8,128)(2,1)}, bf16[1,176,640]{2,1,0:T(8,128)(2,1)S(1)}, u32[]{:S(2)}, u32[]{:S(2)}) collective-permute-start(bf16[1,176,640]{2,1,0:T(8,128)(2,1)} %bitcast.67), channel_id=1, source_target_pairs={{0,256},{32,288},{64,320},{96,352},{128,384},{160,416},{192,448},{... | collective-permute-start | bytes 675848 | tf_op jit(solution)/shard_map/ppermute | solution.py:241
  61.6 0.9 copy-start
  62.5 0.7 copy-start.1
  63.2 0.7 copy-start.3
  63.9 1.7 %copy-start.5 = (bf16[20,256,256]{2,1,0:T(8,128)(2,1)S(1)}, bf16[20,256,256]{2,1,0:T(8,128)(2,1)}, u32[]{:S(2)}) copy-start(bf16[20,256,256]{2,1,0:T(8,128)(2,1)} %get-tuple-element.23.sw_ref) | copy-start | bytes 7864324
  65.6 1.0 copy-start.9
  66.6 6.0 %copy-start.2 = (f32[20,256]{1,0:T(8,128)S(1)}, f32[20,256]{1,0:T(8,128)}, u32[]{:S(2)}) copy-start(f32[20,256]{1,0:T(8,128)} %stack.212.mw_ref) | copy-start | bytes 61444
  66.6 6.0 %copy-start.4 = (f32[1,640]{1,0:T(1,128)S(1)}, f32[1,640]{1,0:T(1,128)}, u32[]{:S(2)}) copy-start(f32[1,640]{1,0:T(1,128)} %broadcast_in_dim.16.m_ref) | copy-start | bytes 7684
  66.6 6.0 %copy-start.10 = (bf16[256,640]{1,0:T(8,128)(2,1)S(1)}, bf16[256,640]{1,0:T(8,128)(2,1)}, u32[]{:S(2)}) copy-start(bf16[256,640]{1,0:T(8,128)(2,1)} %get-tuple-element.24.sh_ref) | copy-start | bytes 983044
  69.5 16.6 %collective-permute-start.1 = (bf16[2,176,640]{2,1,0:T(8,128)(2,1)S(1)}, bf16[2,176,640]{2,1,0:T(8,128)(2,1)S(1)}, u32[]{:S(2)}, u32[]{:S(2)}) collective-permute-start(bf16[2,176,640]{2,1,0:T(8,128)(2,1)S(1)} %maximum_select_fusion.6), channel_id=1, source_target_pairs={{0,128},{32,160},{64,192},{96,224},{128,0},{160,32},{192,64},{224,... | collective-permute-start | bytes 1351688 | tf_op jit(solution)/shard_map/ppermute | solution.py:241
  72.6 1.7 %copy-start.6 = (bf16[20,256,256]{2,1,0:T(8,128)(2,1)S(1)}, bf16[20,256,256]{2,1,0:T(8,128)(2,1)}, u32[]{:S(2)}) copy-start(bf16[20,256,256]{2,1,0:T(8,128)(2,1)} %get-tuple-element.23.sw_ref) | copy-start | bytes 7864324
  86.3 15.1 %collective-permute-start.2 = (bf16[4,176,640]{2,1,0:T(8,128)(2,1)S(1)}, bf16[4,176,640]{2,1,0:T(8,128)(2,1)S(1)}, u32[]{:S(2)}, u32[]{:S(2)}) collective-permute-start(bf16[4,176,640]{2,1,0:T(8,128)(2,1)S(1)} %bitcast.78), channel_id=1, source_target_pairs={{0,64},{32,96},{64,0},{96,32},{128,192},{160,224},{192,128},{224,1... | collective-permute-start | bytes 2703368 | tf_op jit(solution)/shard_map/ppermute | solution.py:241
  88.9 1.7 %copy-start.7 = (bf16[20,256,256]{2,1,0:T(8,128)(2,1)S(1)}, bf16[20,256,256]{2,1,0:T(8,128)(2,1)}, u32[]{:S(2)}) copy-start(bf16[20,256,256]{2,1,0:T(8,128)(2,1)} %get-tuple-element.23.sw_ref) | copy-start | bytes 7864324
  103.0 15.1 %collective-permute-start.3 = (bf16[8,176,640]{2,1,0:T(8,128)(2,1)}, bf16[8,176,640]{2,1,0:T(8,128)(2,1)}, u32[]{:S(2)}, u32[]{:S(2)}) collective-permute-start(bf16[8,176,640]{2,1,0:T(8,128)(2,1)} %bitcast.34), channel_id=1, source_target_pairs={{0,32},{32,0},{64,96},{96,64},{128,160},{160,128},{192,224},{224,1... | collective-permute-start | bytes 5406728 | tf_op jit(solution)/shard_map/ppermute | solution.py:241
  105.2 1.7 %copy-start.8 = (bf16[20,256,256]{2,1,0:T(8,128)(2,1)S(1)}, bf16[20,256,256]{2,1,0:T(8,128)(2,1)}, u32[]{:S(2)}) copy-start(bf16[20,256,256]{2,1,0:T(8,128)(2,1)} %get-tuple-element.23.sw_ref) | copy-start | bytes 7864324

commit v8 on v7

--- a/solution.py
+++ b/solution.py
@@ -212,44 +212,19 @@
     local_rows = seed_index % row_count
     own_seeds = jnp.take(series, local_rows, axis=0)
     weight = scrub_mask.astype(jnp.float32)
+    gathered = lax.all_gather(series, BLK_AXES, axis=0, tiled=True)
     panel_rows = lax.all_gather(own_seeds, "z", axis=0, tiled=True)
     panel_rows = lax.all_gather(panel_rows, "x_lo", axis=0, tiled=True)
     mw = window_masks(weight, frames)
     m = weight[None, :]
     sw, sh = seed_rows(panel_rows, m, mw)
     seeds = panel_rows.shape[0]
-    size = 1
+    blocks = 1
     for a in BLK_AXES:
-        size *= lax.axis_size(a)
-    me = lax.axis_index(BLK_AXES)
-    bits = size.bit_length() - 1
-    order = list(range(bits))[::-1]
-
-    def run(rows):
-        count = rows.shape[0] * rows.shape[1]
-        d, s = compare_rows(rows.reshape(count, frames), m, mw, sw, sh, row_count)
-        return d.reshape(rows.shape[0], row_count, seeds), s.reshape(rows.shape[0], row_count, seeds)
-
-    held = series[None]
-    outs = [run(held)]
-    for idx, bit in enumerate(order):
-        stride = 1 << bit
-        route = [(i, i ^ stride) for i in range(size)]
-        if idx > 0:
-            held, prev_d, prev_s = lax.optimization_barrier((held,) + outs[idx - 1])
-            outs[idx - 1] = (prev_d, prev_s)
-        other = lax.ppermute(held, BLK_AXES, route)
-        outs.append(run(other))
-        held = place_pair(held, other, me, bit).reshape((-1,) + series.shape)
-    held_d, held_s = outs[0]
-    for idx, bit in enumerate(order):
-        other_d, other_s = outs[idx + 1]
-        held_d = place_pair(held_d, other_d, me, bit).reshape((-1, row_count, seeds))
-        held_s = place_pair(held_s, other_s, me, bit).reshape((-1, row_count, seeds))
-    out_block = jnp.zeros((row_count, seeds), jnp.bfloat16)
-    dispersion = unpermute(held_d.reshape((2,) * bits + (row_count, seeds)), order, size, out_block)
-    statistic = unpermute(held_s.reshape((2,) * bits + (row_count, seeds)), order, size, out_block)
-    return (dispersion.reshape(size, row_count, seeds), statistic.reshape(size, row_count, seeds))
+        blocks *= lax.axis_size(a)
+    dispersion, statistic = compare_rows(gathered, m, mw, sw, sh, row_count)
+    shape = (blocks, row_count, seeds)
+    return (dispersion.reshape(shape), statistic.reshape(shape))
 
 
 def solution(mesh):

time: 145 us -> 142 us (0.979); the launches traced: 144 us -> 139 us
  between operations: 0.83 us -> 14 us
  starting transfers between devices: 12.8 us -> 0.04 us
  local copies, waits for them, and re-layouts: 16.6 us -> 8.09 us
  waiting for transfers between devices: 14.2 us -> 19.2 us
  other arithmetic: 6.5 us -> 3.77 us
    all_gather x0 -> x1, waiting for transfers between devices: none -> 18.5 us  [body(): gathered = lax.all_gather(series, BLK_AXES, axis=0, tiled=True)]
    ppermute x4 -> x0, waiting for transfers between devices: 14.2 us -> none  [body(): other = lax.ppermute(held, BLK_AXES, route)]
    ppermute x4 -> x0, starting transfers between devices: 12.8 us -> none  [body(): other = lax.ppermute(held, BLK_AXES, route)]
    unnamed x22 -> x8, local copies, waits for them, and re-layouts: 10.3 us -> 4.11 us
    transpose x2 -> x0, local copies, waits for them, and re-layouts: 2.41 us -> none  [unpermute(): held = jnp.transpose(held, perm + [bits + k for k in range(block.ndim)])]
    select_n x5 -> x0, other arithmetic: 2.12 us -> none  [place_pair(): jnp.where(mine_low, jnp.stack([held, other]), jnp.stack([other, held]))]
    pallas_call x5 -> x1, Pallas kernels: 44.4 us -> 45.6 us  [compare_rows(): pl.pallas_call(compare_kernel, grid=(steps,), in_specs=[pl.BlockSpec((blo...]
  transfers between devices with their start and end apart: 4 -> 1, of which waited for: 2 -> 1; matrix products, arithmetic and copies ran while one was open for 6% -> 6% of each run, Pallas kernels for 19% -> 4%
where the time goes in v8:
time: 142 us; the launch traced here: 139 us
  Pallas kernels  51.5 us (36%)
  blocking collectives  42.3 us (30%)
  waiting for transfers between devices  19.2 us (14%)
  between operations  14 us (10%)
  local copies, waits for them, and re-layouts  8.09 us (6%)
  other arithmetic  3.77 us (3%)
    pallas_call x1, Pallas kernels, compare_rows(): pl.pallas_call(compare_kernel, grid=(steps,), in_specs=[pl.BlockSpec((blo...  45.6 us
    all_gather x1, blocking collectives, body(): panel_rows = lax.all_gather(own_seeds, 'z', axis=0, tiled=True)  36.2 us
    all_gather x1, waiting for transfers between devices, body(): gathered = lax.all_gather(series, BLK_AXES, axis=0, tiled=True)  18.5 us
    all_gather x1, blocking collectives, body(): panel_rows = lax.all_gather(panel_rows, 'x_lo', axis=0, tiled=True)  6.08 us
    pallas_call x1, Pallas kernels, seed_rows(): pl.pallas_call(seed_kernel, in_specs=[vmem, vmem, vmem], out_specs=[vmem,...  5.9 us
    unnamed x8, local copies, waits for them, and re-layouts  4.11 us
  transfers between devices with their start and end apart: 1, of which 1 were waited for; matrix products, arithmetic and copies ran while one was open for 6% of the time, Pallas kernels for 4%

profile of v8, /device:TPU:24, one launch (start us, length us, event | category | flops | bytes accessed | tf_op | source)
XLA Modules:
  0.0 139.0 jit_solution(10345475873765515155)
XLA Ops:
  7.2 0.0 all-gather.2.cloned.1.call-start
  7.2 0.7 all-gather.2.cloned.1.call-update
  7.9 0.7 convert_element_type.5
  8.6 0.6 broadcast_in_dim.15.m_ref
  9.2 0.7 compare_and_fusion
  9.8 1.5 %gather_fusion = bf16[8,640]{1,0:T(8,128)(2,1)S(1)} fusion(bf16[176,640]{1,0:T(8,128)(2,1)} %param.23, s32[1024]{0:T(1024)S(1)} %pad_clamp_fusion), kind=kCustom, calls=%fused_computation | custom fusion | bytes 20512 | tf_op jit(solution)/shard_map/jit(_take)/gather | solution.py:213
  11.4 0.7 slice_multiply_fusion.7
  12.1 0.8 fusion.1
  12.9 0.8 fusion
  13.7 1.8 %stack.83.mw_ref = f32[20,256]{1,0:T(8,128)} concatenate(f32[1,256]{1,0:T(1,128)S(1)} %bitcast.41, f32[1,256]{1,0:T(1,128)S(1)} %bitcast.32, f32[1,256]{1,0:T(1,128)S(1)} %bitcast.33, f32[1,256]{1,0:T(1,128)S(1)} %bitcast.34, f32[1,256]{1,0:T(1,128)S(1)} %bitcast.35, f32[1,256]{1,0:T(1,128)S(1)} %bitcast.40, f32[1,256]{1,0:T(1,128)S(1)} %bitcast.23, f32[1,256]{1,0:T(1,128)S(1)} %bitcast.24, ...), dimensions={0} | concatenate | bytes 40960 | tf_op jit(solution)/shard_map/stack | solution.py:76
  15.6 0.1 broadcast_select_fusion
  15.7 36.2 %all_gather.10 = bf16[128,640]{1,0:T(8,128)(2,1)S(1)} all-gather(bf16[8,640]{1,0:T(8,128)(2,1)S(1)} %broadcast_select_fusion), channel_id=1, replica_groups=mesh['x_hi'=2,'y'=4,'core'=2,'x_lo'=2,'z'=16] {'z'}, dimensions={0}, use_global_device_ids=true | all-gather | bytes 174080 | tf_op jit(solution)/shard_map/all_gather | solution.py:216
  51.9 6.1 %all_gather.11.x_ref = bf16[256,640]{1,0:T(8,128)(2,1)} all-gather(bf16[128,640]{1,0:T(8,128)(2,1)S(1)} %all_gather.10), channel_id=1, replica_groups=mesh['x_hi'=2,'y'=4,'core'=2,'x_lo'=2,'z'=16] {'x_lo'}, dimensions={0}, use_global_device_ids=true | all-gather | bytes 491520 | tf_op jit(solution)/shard_map/all_gather | solution.py:217
  58.0 5.9 %shard_map.230 = (bf16[20,256,256]{2,1,0:T(8,128)(2,1)}, bf16[256,640]{1,0:T(8,128)(2,1)}) custom-call(bf16[256,640]{1,0:T(8,128)(2,1)} %all_gather.11.x_ref, f32[1,640]{1,0:T(1,128)} %broadcast_in_dim.15.m_ref, f32[20,256]{1,0:T(8,128)} %stack.83.mw_ref), custom_call_target="tpu_custom_call" | custom-call | tf_op jit(solution)/shard_map/pallas_call | solution.py:136
  63.9 18.5 %all-gather.2.cloned.1.call-done.x_ref = bf16[2816,640]{1,0:T(8,128)(2,1)} async-done(((bf16[176,640]{1,0:T(8,128)(2,1)}), bf16[2816,640]{1,0:T(8,128)(2,1)}) %all-gather.2.cloned.1.call-update) | async-done | bytes 3604496 | tf_op jit(solution)/shard_map/all_gather | solution.py:215
  82.4 0.0 copy-start
  82.4 0.7 copy-done
  83.2 0.0 copy-start.1
  83.2 0.7 copy-done.1
  83.8 0.0 copy-start.2
  83.8 1.7 %copy-done.2 = bf16[20,256,256]{2,1,0:T(8,128)(2,1)S(1)} copy-done((bf16[20,256,256]{2,1,0:T(8,128)(2,1)S(1)}, bf16[20,256,256]{2,1,0:T(8,128)(2,1)}, u32[]{:S(2)}) %copy-start.2) | copy-done | bytes 2621464
  85.6 0.0 copy-start.3
  85.6 1.0 copy-done.3
  86.5 45.6 %shard_map.231 = (bf16[2816,256]{1,0:T(8,128)(2,1)}, bf16[2816,256]{1,0:T(8,128)(2,1)}) custom-call(bf16[2816,640]{1,0:T(8,128)(2,1)} %all-gather.2.cloned.1.call-done.x_ref, f32[1,640]{1,0:T(1,128)S(1)} %copy-done.1, f32[20,256]{1,0:T(8,128)S(1)} %copy-done, bf16[20,256,256]{2,1,0:T(8,128)(2,1)S(1)} %copy-done.2, bf16[256,640]{1,0:T(8,128)(2,1)S(1)} %copy-done.3), custom_call_target="tpu_custom_call" | custom-call | flops 8304721920 | bytes 9109504 | tf_op jit(solution)/shard_map/pallas_call | solution.py:157
  (1 shorter events, 0.0 us)
Async XLA Ops:
  7.2 75.3 %all-gather.2.cloned.1.call-start = ((), (), s32[]{:S(2)}) async-start(), calls=%async_computation | async-start | bytes 3829760 | tf_op jit(solution)/shard_map/all_gather | solution.py:215
  82.4 0.7 copy-start
  83.2 0.7 copy-start.1
  83.8 1.7 %copy-start.2 = (bf16[20,256,256]{2,1,0:T(8,128)(2,1)S(1)}, bf16[20,256,256]{2,1,0:T(8,128)(2,1)}, u32[]{:S(2)}) copy-start(bf16[20,256,256]{2,1,0:T(8,128)(2,1)} %get-tuple-element.6.sw_ref) | copy-start | bytes 7864324
  85.6 1.0 copy-start.3
Sparse Core Ops, SparseCore 0:
  11.2 71.1 all-gather.1

commit v9 on v8

--- a/solution.py
+++ b/solution.py
@@ -174,6 +174,48 @@
     )(rows, m, mw, sw, sh)
 
 
+def rest_kernel(p_ref, x_ref, m_ref, mw_ref, sw_ref, sh_ref, disp_ref, stat_ref):
+    compare_kernel(x_ref, m_ref, mw_ref, sw_ref, sh_ref, disp_ref, stat_ref)
+
+
+def compare_rest(rows, pair, m, mw, sw, sh, block, skip):
+    count, frames = rows.shape
+    seeds = sh.shape[0]
+    steps = count // block - skip
+
+    def pick(i, p):
+        return jnp.where(i >= p[0], i + skip, i)
+
+    cost = pl.CostEstimate(
+        flops=2 * steps * block * seeds * (frames + NWIN * SPAN),
+        transcendentals=2 * steps * block * seeds * (NWIN + 1),
+        bytes_accessed=steps * block * (frames + 2 * seeds) * 2 + sw.size * 2,
+    )
+    out = jax.ShapeDtypeStruct((count, seeds), jnp.bfloat16)
+    grid_spec = pltpu.PrefetchScalarGridSpec(
+        num_scalar_prefetch=1,
+        grid=(steps,),
+        in_specs=[
+            pl.BlockSpec((block, frames), lambda i, p: (pick(i, p), 0)),
+            pl.BlockSpec((1, frames), lambda i, p: (0, 0)),
+            pl.BlockSpec((NWIN, SPAN), lambda i, p: (0, 0)),
+            pl.BlockSpec((NWIN, seeds, SPAN), lambda i, p: (0, 0, 0)),
+            pl.BlockSpec((seeds, frames), lambda i, p: (0, 0)),
+        ],
+        out_specs=[
+            pl.BlockSpec((block, seeds), lambda i, p: (pick(i, p), 0)),
+            pl.BlockSpec((block, seeds), lambda i, p: (pick(i, p), 0)),
+        ],
+    )
+    return pl.pallas_call(
+        rest_kernel,
+        grid_spec=grid_spec,
+        out_shape=[out, out],
+        cost_estimate=cost,
+        compiler_params=pltpu.CompilerParams(vmem_limit_bytes=48 * 1024 * 1024),
+    )(pair, rows, m, mw, sw, sh)
+
+
 def doubling_gather(block, axis):
     size = lax.axis_size(axis)
     me = lax.axis_index(axis)
@@ -222,7 +264,19 @@
     blocks = 1
     for a in BLK_AXES:
         blocks *= lax.axis_size(a)
-    dispersion, statistic = compare_rows(gathered, m, mw, sw, sh, row_count)
+    core = lax.axis_index("core")
+    partner = lax.ppermute(series, "core", [(0, 1), (1, 0)])
+    first = core == 0
+    pair_rows = jnp.concatenate(
+        [jnp.where(first, series, partner), jnp.where(first, partner, series)]
+    )
+    pair_d, pair_s = compare_rows(pair_rows, m, mw, sw, sh, row_count)
+    me = lax.axis_index(BLK_AXES)
+    pair = (me - core).astype(jnp.int32)
+    rest_d, rest_s = compare_rest(gathered, pair[None], m, mw, sw, sh, row_count, 2)
+    start = pair * row_count
+    dispersion = lax.dynamic_update_slice(rest_d, pair_d, (start, 0))
+    statistic = lax.dynamic_update_slice(rest_s, pair_s, (start, 0))
     shape = (blocks, row_count, seeds)
     return (dispersion.reshape(shape), statistic.reshape(shape))
 

time: 142 us -> 133 us (0.937)
  waiting for transfers between devices: 19.2 us -> 8.99 us
  starting transfers between devices: 0.04 us -> 1.96 us
    pallas_call x0 -> x1, Pallas kernels: none -> 40.2 us  [compare_rest(): pl.pallas_call(rest_kernel, grid_spec=grid_spec, out_shape=[out, out], co...]
    pallas_call x1, Pallas kernels: 45.6 us -> 5.41 us  [compare_rows(): pl.pallas_call(compare_kernel, grid=(steps,), in_specs=[pl.BlockSpec((blo...]
    all_gather x1, waiting for transfers between devices: 18.5 us -> 8.31 us  [body(): gathered = lax.all_gather(series, BLK_AXES, axis=0, tiled=True)]
    ppermute x0 -> x1, starting transfers between devices: none -> 1.92 us  [body(): partner = lax.ppermute(series, 'core', [(0, 1), (1, 0)])]
    unnamed x8 -> x12, local copies, waits for them, and re-layouts: 4.11 us -> 2.59 us
  transfers between devices with their start and end apart: 1 -> 2, of which waited for: 1 -> 1; matrix products, arithmetic and copies ran while one was open for 6% -> 6% of each run, Pallas kernels for 4% -> 9%
where the time goes in v9:
time: 133 us; the launch traced here: 130 us
  Pallas kernels  51.5 us (39%)
  blocking collectives  42.5 us (32%)
  between operations  14.1 us (11%)
  waiting for transfers between devices  8.99 us (7%)
  local copies, waits for them, and re-layouts  7.34 us (6%)
  other arithmetic  3.86 us (3%)
  starting transfers between devices  1.96 us (1%)
    pallas_call x1, Pallas kernels, compare_rest(): pl.pallas_call(rest_kernel, grid_spec=grid_spec, out_shape=[out, out], co...  40.2 us
    all_gather x1, blocking collectives, body(): panel_rows = lax.all_gather(own_seeds, 'z', axis=0, tiled=True)  36.4 us
    all_gather x1, waiting for transfers between devices, body(): gathered = lax.all_gather(series, BLK_AXES, axis=0, tiled=True)  8.31 us
    all_gather x1, blocking collectives, body(): panel_rows = lax.all_gather(panel_rows, 'x_lo', axis=0, tiled=True)  6.08 us
    pallas_call x1, Pallas kernels, seed_rows(): pl.pallas_call(seed_kernel, in_specs=[vmem, vmem, vmem], out_specs=[vmem,...  5.9 us
    pallas_call x1, Pallas kernels, compare_rows(): pl.pallas_call(compare_kernel, grid=(steps,), in_specs=[pl.BlockSpec((blo...  5.41 us
  transfers between devices with their start and end apart: 2, of which 1 were waited for; matrix products, arithmetic and copies ran while one was open for 6% of the time, Pallas kernels for 9%

profile of v9, /device:TPU:24, one launch (start us, length us, event | category | flops | bytes accessed | tf_op | source)
XLA Modules:
  0.0 130.2 jit_solution(10911460952377677264)
XLA Ops:
  7.2 0.0 copy-start.5
  7.2 0.0 all-gather.2.cloned.1.call-start
  7.2 0.7 all-gather.2.cloned.1.call-update
  7.9 1.9 %collective-permute-start = (bf16[176,640]{1,0:T(8,128)(2,1)}, bf16[176,640]{1,0:T(8,128)(2,1)S(1)}, u32[]{:S(2)}, u32[]{:S(2)}) collective-permute-start(bf16[176,640]{1,0:T(8,128)(2,1)} %param.23), channel_id=1, source_target_pairs={{0,32},{32,0},{1,33},{33,1},{2,34},{34,2},{3,35},{35,3},{4,36},{36... | collective-permute-start | bytes 675848 | tf_op jit(solution)/shard_map/ppermute | solution.py:268
  9.8 0.7 convert_element_type.5
  10.5 0.7 compare_and_fusion
  11.2 1.5 %gather_fusion = bf16[8,640]{1,0:T(8,128)(2,1)S(1)} fusion(bf16[176,640]{1,0:T(8,128)(2,1)} %param.23, s32[1024]{0:T(1024)S(1)} %pad_clamp_fusion), kind=kCustom, calls=%fused_computation | custom fusion | bytes 20512 | tf_op jit(solution)/shard_map/jit(_take)/gather | solution.py:255
  12.8 0.1 broadcast_select_fusion.2
  12.8 0.8 fusion
  13.7 0.8 fusion.1
  14.5 0.7 slice_multiply_fusion.7
  15.2 0.6 broadcast_in_dim.19.m_ref
  15.8 1.8 %stack.83.mw_ref = f32[20,256]{1,0:T(8,128)} concatenate(f32[1,256]{1,0:T(1,128)S(1)} %bitcast.42, f32[1,256]{1,0:T(1,128)S(1)} %bitcast.24, f32[1,256]{1,0:T(1,128)S(1)} %bitcast.25, f32[1,256]{1,0:T(1,128)S(1)} %bitcast.26, f32[1,256]{1,0:T(1,128)S(1)} %bitcast.27, f32[1,256]{1,0:T(1,128)S(1)} %bitcast.41, f32[1,256]{1,0:T(1,128)S(1)} %bitcast.33, f32[1,256]{1,0:T(1,128)S(1)} %bitcast.34, ...), dimensions={0} | concatenate | bytes 40960 | tf_op jit(solution)/shard_map/stack | solution.py:76
  17.6 36.4 %all_gather.10 = bf16[128,640]{1,0:T(8,128)(2,1)S(1)} all-gather(bf16[8,640]{1,0:T(8,128)(2,1)S(1)} %broadcast_select_fusion.2), channel_id=1, replica_groups=mesh['x_hi'=2,'y'=4,'core'=2,'x_lo'=2,'z'=16] {'z'}, dimensions={0}, use_global_device_ids=true | all-gather | bytes 174080 | tf_op jit(solution)/shard_map/all_gather | solution.py:258
  54.0 6.1 %all_gather.11.x_ref = bf16[256,640]{1,0:T(8,128)(2,1)} all-gather(bf16[128,640]{1,0:T(8,128)(2,1)S(1)} %all_gather.10), channel_id=1, replica_groups=mesh['x_hi'=2,'y'=4,'core'=2,'x_lo'=2,'z'=16] {'x_lo'}, dimensions={0}, use_global_device_ids=true | all-gather | bytes 491520 | tf_op jit(solution)/shard_map/all_gather | solution.py:259
  60.1 5.9 %shard_map.230 = (bf16[20,256,256]{2,1,0:T(8,128)(2,1)}, bf16[256,640]{1,0:T(8,128)(2,1)}) custom-call(bf16[256,640]{1,0:T(8,128)(2,1)} %all_gather.11.x_ref, f32[1,640]{1,0:T(1,128)} %broadcast_in_dim.19.m_ref, f32[20,256]{1,0:T(8,128)} %stack.83.mw_ref), custom_call_target="tpu_custom_call" | custom-call | tf_op jit(solution)/shard_map/pallas_call | solution.py:136
  66.0 0.0 collective-permute-done
  66.0 0.1 broadcast_select_fusion.1
  66.1 0.8 copy-done.4
  67.0 1.7 %copy-done.2 = bf16[20,256,256]{2,1,0:T(8,128)(2,1)S(1)} copy-done((bf16[20,256,256]{2,1,0:T(8,128)(2,1)S(1)}, bf16[20,256,256]{2,1,0:T(8,128)(2,1)}, u32[]{:S(2)}) %copy-start.2) | copy-done | bytes 2621464
  68.7 5.4 %shard_map.232 = (bf16[352,256]{1,0:T(8,128)(2,1)S(1)}, bf16[352,256]{1,0:T(8,128)(2,1)S(1)}) custom-call(bf16[352,640]{1,0:T(8,128)(2,1)S(1)} %pad_maximum_fusion.x_ref, f32[1,640]{1,0:T(1,128)S(1)} %copy-done.1, f32[20,256]{1,0:T(8,128)S(1)} %copy-done, bf16[20,256,256]{2,1,0:T(8,128)(2,1)S(1)} %copy-done.2, bf16[256,640]{1,0:T(8,128)(2,1)S(1)} %copy-done.4), custom_call_target="tpu_custom_call" | custom-call | flops 1038090240 | bytes 3432448 | tf_op jit(solution)/shard_map/pallas_call | solution.py:157
  74.1 8.3 %all-gather.2.cloned.1.call-done.x_ref = bf16[2816,640]{1,0:T(8,128)(2,1)} async-done(((bf16[176,640]{1,0:T(8,128)(2,1)}), bf16[2816,640]{1,0:T(8,128)(2,1)}) %all-gather.2.cloned.1.call-update) | async-done | bytes 3604496 | tf_op jit(solution)/shard_map/all_gather | solution.py:257
  82.4 40.2 %shard_map.231 = (bf16[2816,256]{1,0:T(8,128)(2,1)}, bf16[2816,256]{1,0:T(8,128)(2,1)}) custom-call(s32[1]{0:T(128)} %bitcast.p_ref, bf16[2816,640]{1,0:T(8,128)(2,1)} %all-gather.2.cloned.1.call-done.x_ref, f32[1,640]{1,0:T(1,128)S(1)} %copy-done.1, f32[20,256]{1,0:T(8,128)S(1)} %copy-done, bf16[20,256,256]{2,1,0:T(8,128)(2,1)S(1)} %copy-done.3, ...), custom_call_target="tpu_custom_call" | custom-call | flops 7266631680 | bytes 8298496 | tf_op jit(solution)/shard_map/pallas_call | solution.py:210
  122.6 0.8 constant_dynamic-update-slice_fusion
  (11 shorter events, 0.1 us)
Async XLA Ops:
  7.2 58.8 %copy-start.5 = (bf16[176,640]{1,0:T(8,128)(2,1)S(1)}, bf16[176,640]{1,0:T(8,128)(2,1)}, u32[]{:S(2)}) copy-start(bf16[176,640]{1,0:T(8,128)(2,1)} %param.23) | copy-start | bytes 675844
  7.2 75.3 %all-gather.2.cloned.1.call-start = ((), (), s32[]{:S(2)}) async-start(), calls=%async_computation | async-start | bytes 3829760 | tf_op jit(solution)/shard_map/all_gather | solution.py:257
  7.9 58.1 %collective-permute-start = (bf16[176,640]{1,0:T(8,128)(2,1)}, bf16[176,640]{1,0:T(8,128)(2,1)S(1)}, u32[]{:S(2)}, u32[]{:S(2)}) collective-permute-start(bf16[176,640]{1,0:T(8,128)(2,1)} %param.23), channel_id=1, source_target_pairs={{0,32},{32,0},{1,33},{33,1},{2,34},{34,2},{3,35},{35,3},{4,36},{36... | collective-permute-start | bytes 675848 | tf_op jit(solution)/shard_map/ppermute | solution.py:268
  15.8 50.3 %copy-start.1 = (f32[1,640]{1,0:T(1,128)S(1)}, f32[1,640]{1,0:T(1,128)}, u32[]{:S(2)}) copy-start(f32[1,640]{1,0:T(1,128)} %broadcast_in_dim.19.m_ref) | copy-start | bytes 7684
  17.6 48.5 %copy-start = (f32[20,256]{1,0:T(8,128)S(1)}, f32[20,256]{1,0:T(8,128)}, u32[]{:S(2)}) copy-start(f32[20,256]{1,0:T(8,128)} %stack.83.mw_ref) | copy-start | bytes 61444
  66.0 1.0 copy-start.4
  67.0 1.7 %copy-start.2 = (bf16[20,256,256]{2,1,0:T(8,128)(2,1)S(1)}, bf16[20,256,256]{2,1,0:T(8,128)(2,1)}, u32[]{:S(2)}) copy-start(bf16[20,256,256]{2,1,0:T(8,128)(2,1)} %get-tuple-element.8.sw_ref) | copy-start | bytes 7864324
  68.7 13.7 %copy-start.3 = (bf16[20,256,256]{2,1,0:T(8,128)(2,1)S(1)}, bf16[20,256,256]{2,1,0:T(8,128)(2,1)}, u32[]{:S(2)}) copy-start(bf16[20,256,256]{2,1,0:T(8,128)(2,1)} %get-tuple-element.8.sw_ref) | copy-start | bytes 7864324
Sparse Core Ops, SparseCore 0:
  11.3 71.1 all-gather.1

commit v10 on v9

--- a/solution.py
+++ b/solution.py
@@ -264,16 +264,20 @@
     blocks = 1
     for a in BLK_AXES:
         blocks *= lax.axis_size(a)
-    core = lax.axis_index("core")
-    partner = lax.ppermute(series, "core", [(0, 1), (1, 0)])
-    first = core == 0
-    pair_rows = jnp.concatenate(
-        [jnp.where(first, series, partner), jnp.where(first, partner, series)]
-    )
-    pair_d, pair_s = compare_rows(pair_rows, m, mw, sw, sh, row_count)
+    near = ("y", "core")
+    near_size = lax.axis_size("y") * lax.axis_size("core")
+    mine = lax.axis_index(near)
+    group = min(4, near_size)
+    moved = [series]
+    for flip in range(1, group):
+        route = [(i, i ^ flip) for i in range(near_size)]
+        moved.append(lax.ppermute(series, near, route))
+    local = mine % group
+    near_rows = jnp.take(jnp.stack(moved), jnp.arange(group) ^ local, axis=0)
+    pair_d, pair_s = compare_rows(near_rows.reshape(-1, frames), m, mw, sw, sh, row_count)
     me = lax.axis_index(BLK_AXES)
-    pair = (me - core).astype(jnp.int32)
-    rest_d, rest_s = compare_rest(gathered, pair[None], m, mw, sw, sh, row_count, 2)
+    pair = (me - local).astype(jnp.int32)
+    rest_d, rest_s = compare_rest(gathered, pair[None], m, mw, sw, sh, row_count, group)
     start = pair * row_count
     dispersion = lax.dynamic_update_slice(rest_d, pair_d, (start, 0))
     statistic = lax.dynamic_update_slice(rest_s, pair_s, (start, 0))

time: 133 us -> 132 us (level); the launches traced: 130 us -> 131 us
  waiting for transfers between devices: 8.99 us -> 0.71 us
  starting transfers between devices: 1.96 us -> 7.63 us
  other arithmetic: 3.86 us -> 6.37 us
  local copies, waits for them, and re-layouts: 7.34 us -> 8.91 us
    all_gather x1, waiting for transfers between devices: 8.31 us -> 0.02 us  [body(): gathered = lax.all_gather(series, BLK_AXES, axis=0, tiled=True)]
    pallas_call x1, Pallas kernels: 40.2 us -> 34.2 us  [compare_rest(): pl.pallas_call(rest_kernel, grid_spec=grid_spec, out_shape=[out, out], co...]
    ppermute x1 -> x3, starting transfers between devices: 1.92 us -> 7.59 us  [body(): moved.append(lax.ppermute(series, near, route))]
    pallas_call x1, Pallas kernels: 5.41 us -> 10.8 us  [compare_rows(): pl.pallas_call(compare_kernel, grid=(steps,), in_specs=[pl.BlockSpec((blo...]
    gather x0 -> x1, local copies, waits for them, and re-layouts: none -> 2.9 us  [body(): near_rows = jnp.take(jnp.stack(moved), jnp.arange(group) ^ local, axis=0)]
    unnamed x12, local copies, waits for them, and re-layouts: 2.59 us -> 0.99 us
    select_n x1 -> x2, other arithmetic: 0.05 us -> 1.5 us  [body(): near_rows = jnp.take(jnp.stack(moved), jnp.arange(group) ^ local, axis=0)]
  transfers between devices with their start and end apart: 2 -> 4, of which waited for: 1 -> 0; matrix products, arithmetic and copies ran while one was open for 6% -> 10% of each run, Pallas kernels for 9% -> 13%
where the time goes in v10:
time: 132 us; the launch traced here: 131 us
  Pallas kernels  51 us (39%)
  blocking collectives  42.4 us (32%)
  between operations  14.2 us (11%)
  local copies, waits for them, and re-layouts  8.91 us (7%)
  starting transfers between devices  7.63 us (6%)
  other arithmetic  6.37 us (5%)
    all_gather x1, blocking collectives, body(): panel_rows = lax.all_gather(own_seeds, 'z', axis=0, tiled=True)  36.3 us
    pallas_call x1, Pallas kernels, compare_rest(): pl.pallas_call(rest_kernel, grid_spec=grid_spec, out_shape=[out, out], co...  34.2 us
    pallas_call x1, Pallas kernels, compare_rows(): pl.pallas_call(compare_kernel, grid=(steps,), in_specs=[pl.BlockSpec((blo...  10.8 us
    ppermute x3, starting transfers between devices, body(): moved.append(lax.ppermute(series, near, route))  7.59 us
    all_gather x1, blocking collectives, body(): panel_rows = lax.all_gather(panel_rows, 'x_lo', axis=0, tiled=True)  6.08 us
    pallas_call x1, Pallas kernels, seed_rows(): pl.pallas_call(seed_kernel, in_specs=[vmem, vmem, vmem], out_specs=[vmem,...  5.9 us
    gather x1, local copies, waits for them, and re-layouts, body(): near_rows = jnp.take(jnp.stack(moved), jnp.arange(group) ^ local, axis=0)  2.9 us
  transfers between devices with their start and end apart: 4, of which 0 were waited for; matrix products, arithmetic and copies ran while one was open for 10% of the time, Pallas kernels for 13%

profile of v10, /device:TPU:24, one launch (start us, length us, event | category | flops | bytes accessed | tf_op | source)
XLA Modules:
  0.0 131.2 jit_solution(5312279453805879742)
XLA Ops:
  7.2 0.7 all-gather.2.cloned.1.call-update
  7.9 2.1 %collective-permute-start.2 = (bf16[176,640]{1,0:T(8,128)(2,1)}, bf16[176,640]{1,0:T(8,128)(2,1)S(1)}, u32[]{:S(2)}, u32[]{:S(2)}) collective-permute-start(bf16[176,640]{1,0:T(8,128)(2,1)} %param.23), channel_id=1, source_target_pairs={{0,96},{32,64},{64,32},{96,0},{128,224},{160,192},{192,160},{224,1... | collective-permute-start | bytes 675848 | tf_op jit(solution)/shard_map/ppermute | solution.py:274
  10.0 3.2 %collective-permute-start.1 = (bf16[176,640]{1,0:T(8,128)(2,1)}, bf16[176,640]{1,0:T(8,128)(2,1)S(1)}, u32[]{:S(2)}, u32[]{:S(2)}) collective-permute-start(bf16[176,640]{1,0:T(8,128)(2,1)} %param.23), channel_id=1, source_target_pairs={{0,64},{32,96},{64,0},{96,32},{128,192},{160,224},{192,128},{224,1... | collective-permute-start | bytes 675848 | tf_op jit(solution)/shard_map/ppermute | solution.py:274
  13.2 2.3 %collective-permute-start = (bf16[176,640]{1,0:T(8,128)(2,1)}, bf16[176,640]{1,0:T(8,128)(2,1)S(1)}, u32[]{:S(2)}, u32[]{:S(2)}) collective-permute-start(bf16[176,640]{1,0:T(8,128)(2,1)} %param.23), channel_id=1, source_target_pairs={{0,32},{32,0},{64,96},{96,64},{128,160},{160,128},{192,224},{224,1... | collective-permute-start | bytes 675848 | tf_op jit(solution)/shard_map/ppermute | solution.py:274
  15.5 0.7 convert_element_type.5
  16.2 0.6 broadcast_in_dim.33.m_ref
  16.8 0.7 compare_and_fusion.1
  17.5 1.5 %gather_fusion = bf16[8,640]{1,0:T(8,128)(2,1)S(1)} fusion(bf16[176,640]{1,0:T(8,128)(2,1)} %param.23, s32[1024]{0:T(1024)S(1)} %pad_clamp_fusion.1), kind=kCustom, calls=%fused_computation | custom fusion | bytes 20512 | tf_op jit(solution)/shard_map/jit(_take)/gather | solution.py:255
  19.2 0.1 broadcast_in_dim.38
  19.2 0.1 broadcast_select_fusion
  19.3 36.3 %all_gather.10 = bf16[128,640]{1,0:T(8,128)(2,1)S(1)} all-gather(bf16[8,640]{1,0:T(8,128)(2,1)S(1)} %broadcast_select_fusion), channel_id=1, replica_groups=mesh['x_hi'=2,'y'=4,'core'=2,'x_lo'=2,'z'=16] {'z'}, dimensions={0}, use_global_device_ids=true | all-gather | bytes 174080 | tf_op jit(solution)/shard_map/all_gather | solution.py:258
  55.6 6.1 %all_gather.11.x_ref = bf16[256,640]{1,0:T(8,128)(2,1)} all-gather(bf16[128,640]{1,0:T(8,128)(2,1)S(1)} %all_gather.10), channel_id=1, replica_groups=mesh['x_hi'=2,'y'=4,'core'=2,'x_lo'=2,'z'=16] {'x_lo'}, dimensions={0}, use_global_device_ids=true | all-gather | bytes 491520 | tf_op jit(solution)/shard_map/all_gather | solution.py:259
  61.7 0.7 slice_multiply_fusion.7
  62.4 0.8 fusion
  63.2 0.8 fusion.1
  64.1 1.8 %stack.98.mw_ref = f32[20,256]{1,0:T(8,128)} concatenate(f32[1,256]{1,0:T(1,128)S(1)} %bitcast.54, f32[1,256]{1,0:T(1,128)S(1)} %bitcast.36, f32[1,256]{1,0:T(1,128)S(1)} %bitcast.37, f32[1,256]{1,0:T(1,128)S(1)} %bitcast.38, f32[1,256]{1,0:T(1,128)S(1)} %bitcast.39, f32[1,256]{1,0:T(1,128)S(1)} %bitcast.53, f32[1,256]{1,0:T(1,128)S(1)} %bitcast.45, f32[1,256]{1,0:T(1,128)S(1)} %bitcast.46, ...), dimensions={0} | concatenate | bytes 40960 | tf_op jit(solution)/shard_map/stack | solution.py:76
  65.9 5.9 %shard_map.230 = (bf16[20,256,256]{2,1,0:T(8,128)(2,1)}, bf16[256,640]{1,0:T(8,128)(2,1)}) custom-call(bf16[256,640]{1,0:T(8,128)(2,1)} %all_gather.11.x_ref, f32[1,640]{1,0:T(1,128)} %broadcast_in_dim.33.m_ref, f32[20,256]{1,0:T(8,128)} %stack.98.mw_ref), custom_call_target="tpu_custom_call" | custom-call | tf_op jit(solution)/shard_map/pallas_call | solution.py:136
  71.8 1.1 pad_maximum_fusion
  72.9 2.9 %gather_fusion.1 = bf16[4,176,640]{2,1,0:T(8,128)(2,1)} fusion(bf16[4,176,640]{2,1,0:T(8,128)(2,1)} %pad_maximum_fusion, s32[1024]{0:T(1024)S(1)} %pad_clamp_fusion), kind=kCustom, calls=%fused_computation.1 | custom fusion | bytes 1802256 | tf_op jit(solution)/shard_map/jit(_take)/gather | solution.py:276
  75.8 1.5 %bitcast_select_fusion.x_ref = bf16[704,640]{1,0:T(8,128)(2,1)S(1)} fusion(bf16[4,176,640]{2,1,0:T(8,128)(2,1)} %gather_fusion.1, pred[704]{0:T(1024)(128)(4,1)S(1)} %broadcast_in_dim.38), kind=kLoop, calls=%fused_computation.3 | loop fusion | flops 450560 | bytes 1802944 | tf_op jit(solution)/shard_map/jit(_take)/select_n | solution.py:276
  77.4 10.8 %shard_map.232 = (bf16[704,256]{1,0:T(8,128)(2,1)S(1)}, bf16[704,256]{1,0:T(8,128)(2,1)S(1)}) custom-call(bf16[704,640]{1,0:T(8,128)(2,1)S(1)} %bitcast_select_fusion.x_ref, f32[1,640]{1,0:T(1,128)S(1)} %copy-done.1, f32[20,256]{1,0:T(8,128)S(1)} %copy-done, bf16[20,256,256]{2,1,0:T(8,128)(2,1)S(1)} %copy-done.2, bf16[256,640]{1,0:T(8,128)(2,1)S(1)} %copy-done.3), custom_call_target="tpu_custom_call" | custom-call | flops 2076180480 | bytes 4243456 | tf_op jit(solution)/shard_map/pallas_call | solution.py:157
  88.2 1.0 copy-done.4
  89.2 34.2 %shard_map.231 = (bf16[2816,256]{1,0:T(8,128)(2,1)}, bf16[2816,256]{1,0:T(8,128)(2,1)}) custom-call(s32[1]{0:T(128)} %bitcast.p_ref, bf16[2816,640]{1,0:T(8,128)(2,1)} %all-gather.2.cloned.1.call-done.x_ref, f32[1,640]{1,0:T(1,128)S(1)} %copy-done.1, f32[20,256]{1,0:T(8,128)S(1)} %copy-done, bf16[20,256,256]{2,1,0:T(8,128)(2,1)S(1)} %copy-done.2, ...), custom_call_target="tpu_custom_call" | custom-call | flops 6228541440 | bytes 7487488 | tf_op jit(solution)/shard_map/pallas_call | solution.py:210
  123.4 0.9 constant_dynamic-update-slice_fusion
  (21 shorter events, 0.2 us)
Async XLA Ops:
  7.2 64.7 %copy-start.5 = (bf16[176,640]{1,0:T(8,128)(2,1)S(1)}, bf16[176,640]{1,0:T(8,128)(2,1)}, u32[]{:S(2)}) copy-start(bf16[176,640]{1,0:T(8,128)(2,1)} %param.23) | copy-start | bytes 675844
  7.2 81.0 %all-gather.2.cloned.1.call-start = ((), (), s32[]{:S(2)}) async-start(), calls=%async_computation | async-start | bytes 3829760 | tf_op jit(solution)/shard_map/all_gather | solution.py:257
  7.9 63.9 %collective-permute-start.2 = (bf16[176,640]{1,0:T(8,128)(2,1)}, bf16[176,640]{1,0:T(8,128)(2,1)S(1)}, u32[]{:S(2)}, u32[]{:S(2)}) collective-permute-start(bf16[176,640]{1,0:T(8,128)(2,1)} %param.23), channel_id=1, source_target_pairs={{0,96},{32,64},{64,32},{96,0},{128,224},{160,192},{192,160},{224,1... | collective-permute-start | bytes 675848 | tf_op jit(solution)/shard_map/ppermute | solution.py:274
  10.0 61.8 %collective-permute-start.1 = (bf16[176,640]{1,0:T(8,128)(2,1)}, bf16[176,640]{1,0:T(8,128)(2,1)S(1)}, u32[]{:S(2)}, u32[]{:S(2)}) collective-permute-start(bf16[176,640]{1,0:T(8,128)(2,1)} %param.23), channel_id=1, source_target_pairs={{0,64},{32,96},{64,0},{96,32},{128,192},{160,224},{192,128},{224,1... | collective-permute-start | bytes 675848 | tf_op jit(solution)/shard_map/ppermute | solution.py:274
  13.2 58.6 %collective-permute-start = (bf16[176,640]{1,0:T(8,128)(2,1)}, bf16[176,640]{1,0:T(8,128)(2,1)S(1)}, u32[]{:S(2)}, u32[]{:S(2)}) collective-permute-start(bf16[176,640]{1,0:T(8,128)(2,1)} %param.23), channel_id=1, source_target_pairs={{0,32},{32,0},{64,96},{96,64},{128,160},{160,128},{192,224},{224,1... | collective-permute-start | bytes 675848 | tf_op jit(solution)/shard_map/ppermute | solution.py:274
  72.9 4.4 %copy-start = (f32[20,256]{1,0:T(8,128)S(1)}, f32[20,256]{1,0:T(8,128)}, u32[]{:S(2)}) copy-start(f32[20,256]{1,0:T(8,128)} %stack.98.mw_ref) | copy-start | bytes 61444
  72.9 4.4 %copy-start.1 = (f32[1,640]{1,0:T(1,128)S(1)}, f32[1,640]{1,0:T(1,128)}, u32[]{:S(2)}) copy-start(f32[1,640]{1,0:T(1,128)} %broadcast_in_dim.33.m_ref) | copy-start | bytes 7684
  72.9 4.4 %copy-start.2 = (bf16[20,256,256]{2,1,0:T(8,128)(2,1)S(1)}, bf16[20,256,256]{2,1,0:T(8,128)(2,1)}, u32[]{:S(2)}) copy-start(bf16[20,256,256]{2,1,0:T(8,128)(2,1)} %get-tuple-element.8.sw_ref) | copy-start | bytes 7864324
  75.8 1.5 %copy-start.3 = (bf16[256,640]{1,0:T(8,128)(2,1)S(1)}, bf16[256,640]{1,0:T(8,128)(2,1)}, u32[]{:S(2)}) copy-start(bf16[256,640]{1,0:T(8,128)(2,1)} %get-tuple-element.9.sh_ref) | copy-start | bytes 983044
  88.2 1.0 copy-start.4
Sparse Core Ops, SparseCore 0:
  11.3 71.1 all-gather.1

commit v11 on v10

--- a/solution.py
+++ b/solution.py
@@ -268,10 +268,11 @@
     near_size = lax.axis_size("y") * lax.axis_size("core")
     mine = lax.axis_index(near)
     group = min(4, near_size)
+    late, panel_rows = lax.optimization_barrier((series, panel_rows))
     moved = [series]
     for flip in range(1, group):
         route = [(i, i ^ flip) for i in range(near_size)]
-        moved.append(lax.ppermute(series, near, route))
+        moved.append(lax.ppermute(late, near, route))
     local = mine % group
     near_rows = jnp.take(jnp.stack(moved), jnp.arange(group) ^ local, axis=0)
     pair_d, pair_s = compare_rows(near_rows.reshape(-1, frames), m, mw, sw, sh, row_count)

time: 132 us -> 133 us (level)
  no operation moved by 1% of the time
where the time goes in v11:
time: 133 us; the launch traced here: 131 us
  Pallas kernels  51 us (38%)
  blocking collectives  42.3 us (32%)
  between operations  14.2 us (11%)
  local copies, waits for them, and re-layouts  8.92 us (7%)
  starting transfers between devices  7.62 us (6%)
  other arithmetic  6.3 us (5%)
    all_gather x1, blocking collectives, body(): panel_rows = lax.all_gather(own_seeds, 'z', axis=0, tiled=True)  36.3 us
    pallas_call x1, Pallas kernels, compare_rest(): pl.pallas_call(rest_kernel, grid_spec=grid_spec, out_shape=[out, out], co...  34.2 us
    pallas_call x1, Pallas kernels, compare_rows(): pl.pallas_call(compare_kernel, grid=(steps,), in_specs=[pl.BlockSpec((blo...  10.8 us
    ppermute x3, starting transfers between devices, body(): moved.append(lax.ppermute(late, near, route))  7.58 us
    all_gather x1, blocking collectives, body(): panel_rows = lax.all_gather(panel_rows, 'x_lo', axis=0, tiled=True)  6.08 us
    pallas_call x1, Pallas kernels, seed_rows(): pl.pallas_call(seed_kernel, in_specs=[vmem, vmem, vmem], out_specs=[vmem,...  5.9 us
    gather x1, local copies, waits for them, and re-layouts, body(): near_rows = jnp.take(jnp.stack(moved), jnp.arange(group) ^ local, axis=0)  2.9 us
  transfers between devices with their start and end apart: 4, of which 0 were waited for; matrix products, arithmetic and copies ran while one was open for 10% of the time, Pallas kernels for 13%

profile of v11, /device:TPU:24, one launch (start us, length us, event | category | flops | bytes accessed | tf_op | source)
XLA Modules:
  0.0 131.0 jit_solution(15941081274823594632)
XLA Ops:
  7.2 0.7 all-gather.2.cloned.1.call-update
  7.9 0.7 compare_and_fusion.1
  8.6 1.5 %gather_fusion = bf16[8,640]{1,0:T(8,128)(2,1)S(1)} fusion(bf16[176,640]{1,0:T(8,128)(2,1)} %param.23, s32[1024]{0:T(1024)S(1)} %pad_clamp_fusion.1), kind=kCustom, calls=%fused_computation | custom fusion | bytes 20512 | tf_op jit(solution)/shard_map/jit(_take)/gather | solution.py:255
  10.1 0.1 broadcast_select_fusion
  10.2 36.3 %all_gather.10 = bf16[128,640]{1,0:T(8,128)(2,1)S(1)} all-gather(bf16[8,640]{1,0:T(8,128)(2,1)S(1)} %broadcast_select_fusion), channel_id=1, replica_groups=mesh['x_hi'=2,'y'=4,'core'=2,'x_lo'=2,'z'=16] {'z'}, dimensions={0}, use_global_device_ids=true | all-gather | bytes 174080 | tf_op jit(solution)/shard_map/all_gather | solution.py:258
  46.5 6.1 %all_gather.11.x_ref = bf16[256,640]{1,0:T(8,128)(2,1)} all-gather(bf16[128,640]{1,0:T(8,128)(2,1)S(1)} %all_gather.10), channel_id=1, replica_groups=mesh['x_hi'=2,'y'=4,'core'=2,'x_lo'=2,'z'=16] {'x_lo'}, dimensions={0}, use_global_device_ids=true | all-gather | bytes 491520 | tf_op jit(solution)/shard_map/all_gather | solution.py:259
  52.6 1.9 %collective-permute-start.2 = (bf16[176,640]{1,0:T(8,128)(2,1)}, bf16[176,640]{1,0:T(8,128)(2,1)S(1)}, u32[]{:S(2)}, u32[]{:S(2)}) collective-permute-start(bf16[176,640]{1,0:T(8,128)(2,1)} %param.23), channel_id=1, source_target_pairs={{0,96},{32,64},{64,32},{96,0},{128,224},{160,192},{192,160},{224,1... | collective-permute-start | bytes 675848 | tf_op jit(solution)/shard_map/ppermute | solution.py:275
  54.5 2.7 %collective-permute-start.1 = (bf16[176,640]{1,0:T(8,128)(2,1)}, bf16[176,640]{1,0:T(8,128)(2,1)S(1)}, u32[]{:S(2)}, u32[]{:S(2)}) collective-permute-start(bf16[176,640]{1,0:T(8,128)(2,1)} %param.23), channel_id=1, source_target_pairs={{0,64},{32,96},{64,0},{96,32},{128,192},{160,224},{192,128},{224,1... | collective-permute-start | bytes 675848 | tf_op jit(solution)/shard_map/ppermute | solution.py:275
  57.1 3.0 %collective-permute-start = (bf16[176,640]{1,0:T(8,128)(2,1)}, bf16[176,640]{1,0:T(8,128)(2,1)S(1)}, u32[]{:S(2)}, u32[]{:S(2)}) collective-permute-start(bf16[176,640]{1,0:T(8,128)(2,1)} %param.23), channel_id=1, source_target_pairs={{0,32},{32,0},{64,96},{96,64},{128,160},{160,128},{192,224},{224,1... | collective-permute-start | bytes 675848 | tf_op jit(solution)/shard_map/ppermute | solution.py:275
  60.2 0.7 convert_element_type.5
  60.9 0.6 broadcast_in_dim.33.m_ref
  61.5 0.1 broadcast_in_dim.38
  61.6 0.7 slice_multiply_fusion.7
  62.3 0.8 fusion
  63.1 0.8 fusion.1
  64.0 1.8 %stack.98.mw_ref = f32[20,256]{1,0:T(8,128)} concatenate(f32[1,256]{1,0:T(1,128)S(1)} %bitcast.54, f32[1,256]{1,0:T(1,128)S(1)} %bitcast.36, f32[1,256]{1,0:T(1,128)S(1)} %bitcast.37, f32[1,256]{1,0:T(1,128)S(1)} %bitcast.38, f32[1,256]{1,0:T(1,128)S(1)} %bitcast.39, f32[1,256]{1,0:T(1,128)S(1)} %bitcast.53, f32[1,256]{1,0:T(1,128)S(1)} %bitcast.45, f32[1,256]{1,0:T(1,128)S(1)} %bitcast.46, ...), dimensions={0} | concatenate | bytes 40960 | tf_op jit(solution)/shard_map/stack | solution.py:76
  65.8 5.9 %shard_map.230 = (bf16[20,256,256]{2,1,0:T(8,128)(2,1)}, bf16[256,640]{1,0:T(8,128)(2,1)}) custom-call(bf16[256,640]{1,0:T(8,128)(2,1)} %all_gather.11.x_ref, f32[1,640]{1,0:T(1,128)} %broadcast_in_dim.33.m_ref, f32[20,256]{1,0:T(8,128)} %stack.98.mw_ref), custom_call_target="tpu_custom_call" | custom-call | tf_op jit(solution)/shard_map/pallas_call | solution.py:136
  71.8 1.1 pad_maximum_fusion
  72.8 2.9 %gather_fusion.1 = bf16[4,176,640]{2,1,0:T(8,128)(2,1)} fusion(bf16[4,176,640]{2,1,0:T(8,128)(2,1)} %pad_maximum_fusion, s32[1024]{0:T(1024)S(1)} %pad_clamp_fusion), kind=kCustom, calls=%fused_computation.1 | custom fusion | bytes 1802256 | tf_op jit(solution)/shard_map/jit(_take)/gather | solution.py:277
  75.7 1.4 %bitcast_select_fusion.x_ref = bf16[704,640]{1,0:T(8,128)(2,1)S(1)} fusion(bf16[4,176,640]{2,1,0:T(8,128)(2,1)} %gather_fusion.1, pred[704]{0:T(1024)(128)(4,1)S(1)} %broadcast_in_dim.38), kind=kLoop, calls=%fused_computation.3 | loop fusion | flops 450560 | bytes 1802944 | tf_op jit(solution)/shard_map/jit(_take)/select_n | solution.py:277
  77.2 10.8 %shard_map.232 = (bf16[704,256]{1,0:T(8,128)(2,1)S(1)}, bf16[704,256]{1,0:T(8,128)(2,1)S(1)}) custom-call(bf16[704,640]{1,0:T(8,128)(2,1)S(1)} %bitcast_select_fusion.x_ref, f32[1,640]{1,0:T(1,128)S(1)} %copy-done.1, f32[20,256]{1,0:T(8,128)S(1)} %copy-done, bf16[20,256,256]{2,1,0:T(8,128)(2,1)S(1)} %copy-done.2, bf16[256,640]{1,0:T(8,128)(2,1)S(1)} %copy-done.3), custom_call_target="tpu_custom_call" | custom-call | flops 2076180480 | bytes 4243456 | tf_op jit(solution)/shard_map/pallas_call | solution.py:157
  88.1 1.0 copy-done.4
  89.0 34.2 %shard_map.231 = (bf16[2816,256]{1,0:T(8,128)(2,1)}, bf16[2816,256]{1,0:T(8,128)(2,1)}) custom-call(s32[1]{0:T(128)} %bitcast.p_ref, bf16[2816,640]{1,0:T(8,128)(2,1)} %all-gather.2.cloned.1.call-done.x_ref, f32[1,640]{1,0:T(1,128)S(1)} %copy-done.1, f32[20,256]{1,0:T(8,128)S(1)} %copy-done, bf16[20,256,256]{2,1,0:T(8,128)(2,1)S(1)} %copy-done.2, ...), custom_call_target="tpu_custom_call" | custom-call | flops 6228541440 | bytes 7487488 | tf_op jit(solution)/shard_map/pallas_call | solution.py:210
  123.3 0.9 constant_dynamic-update-slice_fusion
  (21 shorter events, 0.2 us)
Async XLA Ops:
  7.2 64.6 %copy-start.5 = (bf16[176,640]{1,0:T(8,128)(2,1)S(1)}, bf16[176,640]{1,0:T(8,128)(2,1)}, u32[]{:S(2)}) copy-start(bf16[176,640]{1,0:T(8,128)(2,1)} %param.23) | copy-start | bytes 675844
  7.2 80.9 %all-gather.2.cloned.1.call-start = ((), (), s32[]{:S(2)}) async-start(), calls=%async_computation | async-start | bytes 3829760 | tf_op jit(solution)/shard_map/all_gather | solution.py:257
  52.6 19.2 %collective-permute-start.2 = (bf16[176,640]{1,0:T(8,128)(2,1)}, bf16[176,640]{1,0:T(8,128)(2,1)S(1)}, u32[]{:S(2)}, u32[]{:S(2)}) collective-permute-start(bf16[176,640]{1,0:T(8,128)(2,1)} %param.23), channel_id=1, source_target_pairs={{0,96},{32,64},{64,32},{96,0},{128,224},{160,192},{192,160},{224,1... | collective-permute-start | bytes 675848 | tf_op jit(solution)/shard_map/ppermute | solution.py:275
  54.5 17.3 %collective-permute-start.1 = (bf16[176,640]{1,0:T(8,128)(2,1)}, bf16[176,640]{1,0:T(8,128)(2,1)S(1)}, u32[]{:S(2)}, u32[]{:S(2)}) collective-permute-start(bf16[176,640]{1,0:T(8,128)(2,1)} %param.23), channel_id=1, source_target_pairs={{0,64},{32,96},{64,0},{96,32},{128,192},{160,224},{192,128},{224,1... | collective-permute-start | bytes 675848 | tf_op jit(solution)/shard_map/ppermute | solution.py:275
  57.1 14.6 %collective-permute-start = (bf16[176,640]{1,0:T(8,128)(2,1)}, bf16[176,640]{1,0:T(8,128)(2,1)S(1)}, u32[]{:S(2)}, u32[]{:S(2)}) collective-permute-start(bf16[176,640]{1,0:T(8,128)(2,1)} %param.23), channel_id=1, source_target_pairs={{0,32},{32,0},{64,96},{96,64},{128,160},{160,128},{192,224},{224,1... | collective-permute-start | bytes 675848 | tf_op jit(solution)/shard_map/ppermute | solution.py:275
  72.8 4.3 %copy-start = (f32[20,256]{1,0:T(8,128)S(1)}, f32[20,256]{1,0:T(8,128)}, u32[]{:S(2)}) copy-start(f32[20,256]{1,0:T(8,128)} %stack.98.mw_ref) | copy-start | bytes 61444
  72.8 4.3 %copy-start.1 = (f32[1,640]{1,0:T(1,128)S(1)}, f32[1,640]{1,0:T(1,128)}, u32[]{:S(2)}) copy-start(f32[1,640]{1,0:T(1,128)} %broadcast_in_dim.33.m_ref) | copy-start | bytes 7684
  72.8 4.3 %copy-start.2 = (bf16[20,256,256]{2,1,0:T(8,128)(2,1)S(1)}, bf16[20,256,256]{2,1,0:T(8,128)(2,1)}, u32[]{:S(2)}) copy-start(bf16[20,256,256]{2,1,0:T(8,128)(2,1)} %get-tuple-element.9.sw_ref) | copy-start | bytes 7864324
  75.7 1.5 %copy-start.3 = (bf16[256,640]{1,0:T(8,128)(2,1)S(1)}, bf16[256,640]{1,0:T(8,128)(2,1)}, u32[]{:S(2)}) copy-start(bf16[256,640]{1,0:T(8,128)(2,1)} %get-tuple-element.10.sh_ref) | copy-start | bytes 983044
  88.0 1.0 copy-start.4
Sparse Core Ops, SparseCore 0:
  11.3 72.1 all-gather.1

commit v12 on v10

--- a/solution.py
+++ b/solution.py
@@ -216,6 +216,34 @@
     )(pair, rows, m, mw, sw, sh)
 
 
+def compare_near(rows, local, m, mw, sw, sh, block):
+    count, frames = rows.shape
+    seeds = sh.shape[0]
+    steps = count // block
+    out = jax.ShapeDtypeStruct((count, seeds), jnp.bfloat16)
+    grid_spec = pltpu.PrefetchScalarGridSpec(
+        num_scalar_prefetch=1,
+        grid=(steps,),
+        in_specs=[
+            pl.BlockSpec((block, frames), lambda i, p: (jnp.bitwise_xor(i, p[0]), 0)),
+            pl.BlockSpec((1, frames), lambda i, p: (0, 0)),
+            pl.BlockSpec((NWIN, SPAN), lambda i, p: (0, 0)),
+            pl.BlockSpec((NWIN, seeds, SPAN), lambda i, p: (0, 0, 0)),
+            pl.BlockSpec((seeds, frames), lambda i, p: (0, 0)),
+        ],
+        out_specs=[
+            pl.BlockSpec((block, seeds), lambda i, p: (i, 0)),
+            pl.BlockSpec((block, seeds), lambda i, p: (i, 0)),
+        ],
+    )
+    return pl.pallas_call(
+        rest_kernel,
+        grid_spec=grid_spec,
+        out_shape=[out, out],
+        compiler_params=pltpu.CompilerParams(vmem_limit_bytes=48 * 1024 * 1024),
+    )(local, rows, m, mw, sw, sh)
+
+
 def doubling_gather(block, axis):
     size = lax.axis_size(axis)
     me = lax.axis_index(axis)
@@ -273,8 +301,8 @@
         route = [(i, i ^ flip) for i in range(near_size)]
         moved.append(lax.ppermute(series, near, route))
     local = mine % group
-    near_rows = jnp.take(jnp.stack(moved), jnp.arange(group) ^ local, axis=0)
-    pair_d, pair_s = compare_rows(near_rows.reshape(-1, frames), m, mw, sw, sh, row_count)
+    near_rows = jnp.stack(moved).reshape(-1, frames)
+    pair_d, pair_s = compare_near(near_rows, local.astype(jnp.int32)[None], m, mw, sw, sh, row_count)
     me = lax.axis_index(BLK_AXES)
     pair = (me - local).astype(jnp.int32)
     rest_d, rest_s = compare_rest(gathered, pair[None], m, mw, sw, sh, row_count, group)

time: 132 us -> 132 us (level)
  blocking collectives: 42.4 us -> 45.6 us
  other arithmetic: 6.37 us -> 3.91 us
    all_gather x1, blocking collectives: 6.08 us -> 9.13 us  [body(): panel_rows = lax.all_gather(panel_rows, 'x_lo', axis=0, tiled=True)]
    gather x1 -> x0, local copies, waits for them, and re-layouts: 2.9 us -> none  [body(): near_rows = jnp.take(jnp.stack(moved), jnp.arange(group) ^ local, axis=0)]
    unnamed x12 -> x14, local copies, waits for them, and re-layouts: 0.99 us -> 3.5 us
    select_n x2 -> x0, other arithmetic: 1.5 us -> none  [body(): near_rows = jnp.take(jnp.stack(moved), jnp.arange(group) ^ local, axis=0)]
  transfers between devices with their start and end apart: 4 -> 4, of which waited for: 0 -> 0; matrix products, arithmetic and copies ran while one was open for 10% -> 6% of each run, Pallas kernels for 13% -> 13%
where the time goes in v12:
time: 132 us
  Pallas kernels  51.2 us (39%)
  blocking collectives  45.6 us (35%)
  between operations  14.1 us (11%)
  local copies, waits for them, and re-layouts  8.37 us (6%)
  starting transfers between devices  7.63 us (6%)
  other arithmetic  3.91 us (3%)
    all_gather x1, blocking collectives, body(): panel_rows = lax.all_gather(own_seeds, 'z', axis=0, tiled=True)  36.4 us
    pallas_call x1, Pallas kernels, compare_rest(): pl.pallas_call(rest_kernel, grid_spec=grid_spec, out_shape=[out, out], co...  34.4 us
    pallas_call x1, Pallas kernels, compare_near(): pl.pallas_call(rest_kernel, grid_spec=grid_spec, out_shape=[out, out], co...  10.9 us
    all_gather x1, blocking collectives, body(): panel_rows = lax.all_gather(panel_rows, 'x_lo', axis=0, tiled=True)  9.13 us
    ppermute x3, starting transfers between devices, body(): moved.append(lax.ppermute(series, near, route))  7.59 us
    pallas_call x1, Pallas kernels, seed_rows(): pl.pallas_call(seed_kernel, in_specs=[vmem, vmem, vmem], out_specs=[vmem,...  5.91 us
    unnamed x14, local copies, waits for them, and re-layouts  3.5 us
  transfers between devices with their start and end apart: 4, of which 0 were waited for; matrix products, arithmetic and copies ran while one was open for 6% of the time, Pallas kernels for 13%

profile of v12, /device:TPU:24, one launch (start us, length us, event | category | flops | bytes accessed | tf_op | source)
XLA Modules:
  0.0 131.5 jit_solution(7326502933992228024)
XLA Ops:
  7.2 0.0 all-gather.2.cloned.1.call-start
  7.2 0.7 all-gather.2.cloned.1.call-update
  7.9 2.1 %collective-permute-start.2 = (bf16[176,640]{1,0:T(8,128)(2,1)}, bf16[176,640]{1,0:T(8,128)(2,1)S(1)}, u32[]{:S(2)}, u32[]{:S(2)}) collective-permute-start(bf16[176,640]{1,0:T(8,128)(2,1)} %param.23), channel_id=1, source_target_pairs={{0,96},{32,64},{64,32},{96,0},{128,224},{160,192},{192,160},{224,1... | collective-permute-start | bytes 675848 | tf_op jit(solution)/shard_map/ppermute | solution.py:302
  10.0 3.2 %collective-permute-start.1 = (bf16[176,640]{1,0:T(8,128)(2,1)}, bf16[176,640]{1,0:T(8,128)(2,1)S(1)}, u32[]{:S(2)}, u32[]{:S(2)}) collective-permute-start(bf16[176,640]{1,0:T(8,128)(2,1)} %param.23), channel_id=1, source_target_pairs={{0,64},{32,96},{64,0},{96,32},{128,192},{160,224},{192,128},{224,1... | collective-permute-start | bytes 675848 | tf_op jit(solution)/shard_map/ppermute | solution.py:302
  13.2 2.3 %collective-permute-start = (bf16[176,640]{1,0:T(8,128)(2,1)}, bf16[176,640]{1,0:T(8,128)(2,1)S(1)}, u32[]{:S(2)}, u32[]{:S(2)}) collective-permute-start(bf16[176,640]{1,0:T(8,128)(2,1)} %param.23), channel_id=1, source_target_pairs={{0,32},{32,0},{64,96},{96,64},{128,160},{160,128},{192,224},{224,1... | collective-permute-start | bytes 675848 | tf_op jit(solution)/shard_map/ppermute | solution.py:302
  15.5 0.7 convert_element_type.5
  16.2 0.7 compare_and_fusion
  16.9 1.5 %gather_fusion = bf16[8,640]{1,0:T(8,128)(2,1)S(1)} fusion(bf16[176,640]{1,0:T(8,128)(2,1)} %param.23, s32[1024]{0:T(1024)S(1)} %pad_clamp_fusion), kind=kCustom, calls=%fused_computation | custom fusion | bytes 20512 | tf_op jit(solution)/shard_map/jit(_take)/gather | solution.py:283
  18.4 0.1 broadcast_select_fusion
  18.5 0.8 fusion
  19.3 0.8 fusion.1
  20.2 0.7 slice_multiply_fusion.7
  20.9 0.6 broadcast_in_dim.22.m_ref
  21.4 1.8 %stack.98.mw_ref = f32[20,256]{1,0:T(8,128)} concatenate(f32[1,256]{1,0:T(1,128)S(1)} %bitcast.53, f32[1,256]{1,0:T(1,128)S(1)} %bitcast.35, f32[1,256]{1,0:T(1,128)S(1)} %bitcast.36, f32[1,256]{1,0:T(1,128)S(1)} %bitcast.37, f32[1,256]{1,0:T(1,128)S(1)} %bitcast.38, f32[1,256]{1,0:T(1,128)S(1)} %bitcast.52, f32[1,256]{1,0:T(1,128)S(1)} %bitcast.44, f32[1,256]{1,0:T(1,128)S(1)} %bitcast.45, ...), dimensions={0} | concatenate | bytes 40960 | tf_op jit(solution)/shard_map/stack | solution.py:76
  23.3 36.4 %all_gather.10 = bf16[128,640]{1,0:T(8,128)(2,1)S(1)} all-gather(bf16[8,640]{1,0:T(8,128)(2,1)S(1)} %broadcast_select_fusion), channel_id=1, replica_groups=mesh['x_hi'=2,'y'=4,'core'=2,'x_lo'=2,'z'=16] {'z'}, dimensions={0}, use_global_device_ids=true | all-gather | bytes 174080 | tf_op jit(solution)/shard_map/all_gather | solution.py:286
  59.7 9.1 %all_gather.11.x_ref = bf16[256,640]{1,0:T(8,128)(2,1)} all-gather(bf16[128,640]{1,0:T(8,128)(2,1)S(1)} %all_gather.10), channel_id=1, replica_groups=mesh['x_hi'=2,'y'=4,'core'=2,'x_lo'=2,'z'=16] {'x_lo'}, dimensions={0}, use_global_device_ids=true | all-gather | bytes 491520 | tf_op jit(solution)/shard_map/all_gather | solution.py:287
  68.8 5.9 %shard_map.230 = (bf16[20,256,256]{2,1,0:T(8,128)(2,1)}, bf16[256,640]{1,0:T(8,128)(2,1)}) custom-call(bf16[256,640]{1,0:T(8,128)(2,1)} %all_gather.11.x_ref, f32[1,640]{1,0:T(1,128)} %broadcast_in_dim.22.m_ref, f32[20,256]{1,0:T(8,128)} %stack.98.mw_ref), custom_call_target="tpu_custom_call" | custom-call | tf_op jit(solution)/shard_map/pallas_call | solution.py:136
  74.8 0.1 pad_maximum_fusion
  74.9 0.8 copy-done.2
  75.7 1.7 %copy-done = bf16[20,256,256]{2,1,0:T(8,128)(2,1)S(1)} copy-done((bf16[20,256,256]{2,1,0:T(8,128)(2,1)S(1)}, bf16[20,256,256]{2,1,0:T(8,128)(2,1)}, u32[]{:S(2)}) %copy-start) | copy-done | bytes 2621464
  77.5 10.9 %shard_map.232 = (bf16[704,256]{1,0:T(8,128)(2,1)S(1)}, bf16[704,256]{1,0:T(8,128)(2,1)S(1)}) custom-call(s32[1]{0:T(128)} %bitcast.21.p_ref, bf16[704,640]{1,0:T(8,128)(2,1)S(1)} %bitcast.29, f32[1,640]{1,0:T(1,128)S(1)} %copy-done.5, f32[20,256]{1,0:T(8,128)S(1)} %copy-done.4, bf16[20,256,256]{2,1,0:T(8,128)(2,1)S(1)} %copy-done, ...), custom_call_target="tpu_custom_call" | custom-call | tf_op jit(solution)/shard_map/pallas_call | solution.py:239
  88.4 1.0 copy-done.3
  89.4 34.4 %shard_map.231 = (bf16[2816,256]{1,0:T(8,128)(2,1)}, bf16[2816,256]{1,0:T(8,128)(2,1)}) custom-call(s32[1]{0:T(128)} %bitcast.p_ref, bf16[2816,640]{1,0:T(8,128)(2,1)} %all-gather.2.cloned.1.call-done.x_ref, f32[1,640]{1,0:T(1,128)S(1)} %copy-done.5, f32[20,256]{1,0:T(8,128)S(1)} %copy-done.4, bf16[20,256,256]{2,1,0:T(8,128)(2,1)S(1)} %copy-done.1, ...), custom_call_target="tpu_custom_call" | custom-call | flops 6228541440 | bytes 7487488 | tf_op jit(solution)/shard_map/pallas_call | solution.py:210
  123.8 0.9 constant_dynamic-update-slice_fusion
  (16 shorter events, 0.1 us)
Async XLA Ops:
  7.2 67.6 %copy-start.6 = (bf16[176,640]{1,0:T(8,128)(2,1)S(1)}, bf16[176,640]{1,0:T(8,128)(2,1)}, u32[]{:S(2)}) copy-start(bf16[176,640]{1,0:T(8,128)(2,1)} %param.23) | copy-start | bytes 675844
  7.2 81.2 %all-gather.2.cloned.1.call-start = ((), (), s32[]{:S(2)}) async-start(), calls=%async_computation | async-start | bytes 3829760 | tf_op jit(solution)/shard_map/all_gather | solution.py:285
  7.9 66.8 %collective-permute-start.2 = (bf16[176,640]{1,0:T(8,128)(2,1)}, bf16[176,640]{1,0:T(8,128)(2,1)S(1)}, u32[]{:S(2)}, u32[]{:S(2)}) collective-permute-start(bf16[176,640]{1,0:T(8,128)(2,1)} %param.23), channel_id=1, source_target_pairs={{0,96},{32,64},{64,32},{96,0},{128,224},{160,192},{192,160},{224,1... | collective-permute-start | bytes 675848 | tf_op jit(solution)/shard_map/ppermute | solution.py:302
  10.0 64.7 %collective-permute-start.1 = (bf16[176,640]{1,0:T(8,128)(2,1)}, bf16[176,640]{1,0:T(8,128)(2,1)S(1)}, u32[]{:S(2)}, u32[]{:S(2)}) collective-permute-start(bf16[176,640]{1,0:T(8,128)(2,1)} %param.23), channel_id=1, source_target_pairs={{0,64},{32,96},{64,0},{96,32},{128,192},{160,224},{192,128},{224,1... | collective-permute-start | bytes 675848 | tf_op jit(solution)/shard_map/ppermute | solution.py:302
  13.2 61.5 %collective-permute-start = (bf16[176,640]{1,0:T(8,128)(2,1)}, bf16[176,640]{1,0:T(8,128)(2,1)S(1)}, u32[]{:S(2)}, u32[]{:S(2)}) collective-permute-start(bf16[176,640]{1,0:T(8,128)(2,1)} %param.23), channel_id=1, source_target_pairs={{0,32},{32,0},{64,96},{96,64},{128,160},{160,128},{192,224},{224,1... | collective-permute-start | bytes 675848 | tf_op jit(solution)/shard_map/ppermute | solution.py:302
  21.4 53.5 %copy-start.5 = (f32[1,640]{1,0:T(1,128)S(1)}, f32[1,640]{1,0:T(1,128)}, u32[]{:S(2)}) copy-start(f32[1,640]{1,0:T(1,128)} %broadcast_in_dim.22.m_ref) | copy-start | bytes 7684
  23.3 51.7 %copy-start.4 = (f32[20,256]{1,0:T(8,128)S(1)}, f32[20,256]{1,0:T(8,128)}, u32[]{:S(2)}) copy-start(f32[20,256]{1,0:T(8,128)} %stack.98.mw_ref) | copy-start | bytes 61444
  74.7 1.0 copy-start.2
  75.7 1.7 %copy-start = (bf16[20,256,256]{2,1,0:T(8,128)(2,1)S(1)}, bf16[20,256,256]{2,1,0:T(8,128)(2,1)}, u32[]{:S(2)}) copy-start(bf16[20,256,256]{2,1,0:T(8,128)(2,1)} %get-tuple-element.8.sw_ref) | copy-start | bytes 7864324
  77.5 10.9 %copy-start.1 = (bf16[20,256,256]{2,1,0:T(8,128)(2,1)S(1)}, bf16[20,256,256]{2,1,0:T(8,128)(2,1)}, u32[]{:S(2)}) copy-start(bf16[20,256,256]{2,1,0:T(8,128)(2,1)} %get-tuple-element.8.sw_ref) | copy-start | bytes 7864324
  88.4 1.0 copy-start.3
Sparse Core Ops, SparseCore 0:
  11.3 72.8 all-gather.1
